TPU v7x, 32 devices: a whole 2x2x4 slice. The times are simulated.
32 devices in a mesh: tm: 2 (over x), state: 16 (over z, y, core).
Axes of the slice: x: 2, y: 2, z: 4, core: 2. Of those that a mesh axis runs over, the one named last changes fastest.
Arguments:
- anomalies: bfloat16 [4, 24576, 256], P('tm', 'state'), may hold values from -23 to 23, as said below
- obs_weight: float32 [4, 24576], P('tm', 'state'), may hold values from 0.05 to 6, as said below
Outputs:
- smoothed: bfloat16 [4, 24576, 256], P('tm', 'state')
- suffix: float32 [4, 256, 256], P('tm')
Inputs may be any that keep to these rules, and one draw needn't show every extreme that they name: Member anomalies of order one, with member columns correlated. `obs_weight`: positive weights.
All inputs are finite; a program needn't handle non-finite values. Where the computation divides by a largest or mean magnitude, that divisor is 1e-20 or more.
Results may differ from a plain program's by a relative error of at most 0.001.
The roundings to bfloat16 on the way count: a program that leaves them out, or rounds other values in their place, can miss the bound.
Values sent between devices are 32-bit elements; how exact they have to be, the bound alone decides.
No kernel may reach another device: no remote copies, remote signals or barrier semaphores. Data moves between devices by JAX's collectives and lax.ppermute only.
A program may use at most 64 MiB of HBM per device.

v0:
```python
import jax
import jax.numpy as jnp
from jax import lax
from jax.sharding import PartitionSpec as P

NS_STEPS = 4


def carried_in(value, axis, join, neutral):
    count, mine = (lax.axis_size(axis), lax.axis_index(axis))
    pieces = lax.all_gather(value, axis)
    pieces = pieces[::-1]
    mine = count - 1 - mine
    so_far = jnp.full_like(value, 0) + jnp.asarray(neutral, value.dtype)

    def hop(position, so_far):
        longer = join(so_far, pieces[position])
        return jnp.where(position < mine, longer, so_far)

    return lax.fori_loop(0, count - 1, hop, so_far)


def newton_root(covariance):
    identity = jnp.eye(covariance.shape[-1], dtype=jnp.float32)
    row_bound = jnp.max(jnp.sum(jnp.abs(covariance), axis=-1), axis=-1)
    iterate = covariance / row_bound[:, None, None]
    inverse_root = jnp.broadcast_to(identity, covariance.shape)
    for sweep_index in range(NS_STEPS):
        factor = 1.5 * identity - 0.5 * jnp.matmul(
            inverse_root, iterate, precision=lax.Precision.HIGHEST
        )
        iterate = jnp.matmul(iterate, factor, precision=lax.Precision.HIGHEST)
        inverse_root = jnp.matmul(factor, inverse_root, precision=lax.Precision.HIGHEST)
    return inverse_root / jnp.sqrt(row_bound)[:, None, None]


def combine(earlier, later):
    return jnp.matmul(later, earlier, precision=lax.Precision.HIGHEST)


def on_device(anomalies, obs_weight):
    times_dev, rows_dev, members = anomalies.shape
    total_rows = rows_dev * lax.axis_size("state")
    weighted = (anomalies * obs_weight[:, :, None]).astype(jnp.bfloat16)
    partial_gram = jnp.einsum(
        "trm,trn->tmn", weighted, weighted, preferred_element_type=jnp.float32
    )
    gram_sum = lax.psum(partial_gram, "state")
    covariance = gram_sum / total_rows + jnp.eye(members, dtype=jnp.float32)
    transform = newton_root(covariance)
    local_product = transform[times_dev - 1]
    time_index = 0
    local_product = jnp.matmul(
        transform[time_index], local_product, precision=lax.Precision.HIGHEST
    )
    identity = jnp.eye(members, dtype=jnp.float32)
    remote = carried_in(local_product, "tm", combine, identity)
    product = remote
    suffixes = []
    for time_index in range(times_dev - 1, -1, -1):
        product = jnp.matmul(transform[time_index], product, precision=lax.Precision.HIGHEST)
        suffixes.append(product)
    suffix = jnp.stack(suffixes[::-1])
    smoothed = jnp.einsum(
        "trm,tmn->trn", anomalies, suffix.astype(jnp.bfloat16), preferred_element_type=jnp.float32
    ).astype(jnp.bfloat16)
    return (smoothed, suffix)


def solution(mesh):
    placed = (P("tm", "state", None), P("tm", "state"))
    return jax.shard_map(
        on_device,
        mesh=mesh,
        in_specs=placed,
        out_specs=(P("tm", "state", None), P("tm", None, None)),
        check_vma=False,
    )
```

profile of v0, /device:TPU:0, one launch (start us, length us, event | category | flops | bytes accessed | tf_op | source)
XLA Modules:
  0.0 135.0 jit_solution(14095974973290434030)
XLA Ops:
  7.2 0.0 all-reduce.2.cloned.1.call-start
  7.2 4.3 %fusion.1 = f32[2,256,256]{2,1,0:T(8,128)} fusion(bf16[2,1536,256]{2,1,0:T(8,128)(2,1)} %param.2, f32[2,1536]{1,0:T(2,128)} %param.3), kind=kOutput, calls=%fused_computation.3 | convolution fusion | flops 405012480 | bytes 2109440 | tf_op jit(solution)/shard_map/trm,trn->tmn/dot_general | solution.py:45
  11.5 0.0 all-reduce.2.cloned.1.call-update
  11.6 93.2 %all-reduce.2.cloned.1.call-done = f32[2,256,256]{2,1,0:T(8,128)} async-done(((f32[2,256,256]{2,1,0:T(8,128)}), f32[2,256,256]{2,1,0:T(8,128)}) %all-reduce.2.cloned.1.call-update) | async-done | bytes 524304 | tf_op jit(solution)/shard_map/psum | solution.py:48
  104.9 1.2 abs_reduce_fusion
  106.1 0.1 reduce_max.9
  106.2 0.0 copy-start.2
  106.2 1.8 %fusion.6 = f32[2,256,256]{2,1,0:T(8,128)S(1)} fusion(f32[256,256]{1,0:T(8,128)S(1)} %fusion.13, f32[256,256]{1,0:T(8,128)S(1)} %fusion.14, f32[2,256,256]{2,1,0:T(8,128)} %all-reduce.2.cloned.1.call-done, f32[2]{0:T(128)S(1)} %reduce_max.9), kind=kOutput, calls=%fused_computation.13 | convolution fusion | flops 403308544 | bytes 1572872 | tf_op jit(solution)/shard_map/dot_general | solution.py:29
  108.0 0.6 fusion.10
  108.7 0.0 copy-done.2
  108.7 0.7 fusion.17
  109.4 0.7 fusion.5
  110.1 0.7 fusion.23
  110.7 0.7 fusion.22
  111.4 0.7 fusion.4
  112.1 0.7 fusion.24
  112.7 0.7 fusion.25
  113.4 0.7 fusion.3
  114.0 0.7 convolution_divide_fusion
  114.7 0.4 fusion.15
  115.1 9.4 %all-gather = f32[512,256]{1,0:T(8,128)S(1)} all-gather(f32[256,256]{1,0:T(8,128)S(1)} %fusion.15), channel_id=2, replica_groups=mesh['tm'=2,'state'=16] {'tm'}, dimensions={0}, use_global_device_ids=true | all-gather | bytes 786432 | tf_op jit(solution)/shard_map/all_gather | solution.py:11
  124.4 0.0 copy-start.1
  124.4 0.3 convolution_select_fusion
  124.7 0.4 fusion.16
  125.1 0.4 convolution_bitcast_fusion
  125.6 0.3 copy-done.1
  125.9 0.0 copy-start
  125.9 0.7 fusion
  126.5 0.1 copy-done
  126.6 1.6 %copy.9 = bf16[2,1536,256]{2,1,0:T(8,128)(2,1)} copy(bf16[2,1536,256]{1,2,0:T(8,128)(2,1)S(1)} %fusion) | data formatting | bytes 3145728
  (4 shorter events, 0.1 us)
Async XLA Ops:
  7.2 97.7 %all-reduce.2.cloned.1.call-start = ((), (), s32[]{:S(2)}) async-start(), calls=%async_computation | async-start | bytes 1048576 | tf_op jit(solution)/shard_map/psum | solution.py:48
  106.2 2.5 %copy-start.2 = (f32[2,256,256]{2,1,0:T(8,128)S(1)}, f32[2,256,256]{2,1,0:T(8,128)}, u32[]{:S(2)}) copy-start(f32[2,256,256]{2,1,0:T(8,128)} %all-reduce.2.cloned.1.call-done) | copy-start | bytes 1572868
  124.4 1.4 %copy-start.1 = (bf16[2,1536,256]{2,1,0:T(8,128)(2,1)S(1)}, bf16[2,1536,256]{2,1,0:T(8,128)(2,1)}, u32[]{:S(2)}) copy-start(bf16[2,1536,256]{2,1,0:T(8,128)(2,1)} %param.2) | copy-start | bytes 4718596
  125.9 0.8 copy-start
Sparse Core Ops, SparseCore 0:
  12.0 92.8 all-reduce.1
where the time goes:
time: 135 us
  waiting for transfers between devices  93.3 us (69%)
  matrix products  14.8 us (11%)
  between operations  14.2 us (11%)
  blocking collectives  9.35 us (7%)
  local copies, waits for them, and re-layouts  1.98 us (1%)
  other arithmetic  1.4 us (1%)
    psum x1, waiting for transfers between devices, on_device(): gram_sum = lax.psum(partial_gram, 'state')  93.2 us
    all_gather x1, blocking collectives, carried_in(): pieces = lax.all_gather(value, axis)  9.35 us
    dot_general x1, matrix products, on_device(): jnp.einsum('trm,trn->tmn', weighted, weighted, preferred_element_type=jnp...  4.31 us
    dot_general x4, matrix products, newton_root(): jnp.matmul(inverse_root, iterate, precision=lax.Precision.HIGHEST)  3.79 us
  transfers between devices with their start and end apart: 1, of which 1 were waited for; matrix products, arithmetic and copies ran while one was open for 0% of the time, Pallas kernels for 0%

commit v1 on v0

v1 whole, which is shorter than its diff:
```python
import jax
import jax.numpy as jnp
from jax import lax
from jax.sharding import PartitionSpec as P

NS_STEPS = 4
HI = lax.Precision.HIGHEST


def xor_pairs(count, stride):
    return [(source, source ^ stride) for source in range(count)]


def strides_of(count):
    out, stride = [], 1
    while stride < count:
        out.append(stride)
        stride *= 2
    return out


def halving_sum(value, axis):
    count, me = lax.axis_size(axis), lax.axis_index(axis)
    strides = strides_of(count)
    rows = value.shape[0]
    padded = -(-rows // count) * count
    if padded != rows:
        value = jnp.concatenate([value, jnp.zeros((padded - rows,) + value.shape[1:], value.dtype)])
    for stride in strides:
        upper = (me // stride) % 2 == 1
        half = value.shape[0] // 2
        low, high = value[:half], value[half:]
        send = jnp.where(upper, low, high)
        keep = jnp.where(upper, high, low)
        value = keep + lax.ppermute(send, axis, xor_pairs(count, stride))
    for stride in strides[::-1]:
        upper = (me // stride) % 2 == 1
        other = lax.ppermute(value, axis, xor_pairs(count, stride))
        value = jnp.where(upper, jnp.concatenate([other, value]), jnp.concatenate([value, other]))
    return value[:rows]


def state_sum(partial_gram, axis):
    times, n, _ = partial_gram.shape
    return halving_sum(partial_gram.reshape(times * n, n), axis).reshape(times, n, n)


def newton_root(covariance):
    identity = jnp.eye(covariance.shape[-1], dtype=jnp.float32)
    row_bound = jnp.max(jnp.sum(jnp.abs(covariance), axis=-1), axis=-1)
    iterate = covariance / row_bound[:, None, None]
    inverse_root = jnp.broadcast_to(identity, covariance.shape)
    for sweep_index in range(NS_STEPS):
        factor = 1.5 * identity - 0.5 * jnp.matmul(inverse_root, iterate, precision=HI)
        iterate = jnp.matmul(iterate, factor, precision=HI)
        inverse_root = jnp.matmul(factor, inverse_root, precision=HI)
    return inverse_root / jnp.sqrt(row_bound)[:, None, None]


def later_product(local, axis):
    count, me = lax.axis_size(axis), lax.axis_index(axis)
    identity = jnp.eye(local.shape[-1], dtype=local.dtype)
    if count == 1:
        return identity
    shifted = lax.ppermute(local, axis, [(j, j - 1) for j in range(1, count)])
    carried = jnp.where(me + 1 < count, shifted, identity)
    reach = 1
    while reach < count - 1:
        further = lax.ppermute(carried, axis, [(j, j - reach) for j in range(reach, count)])
        further = jnp.where(me + reach < count, further, identity)
        carried = jnp.matmul(carried, further, precision=HI)
        reach *= 2
    return carried


def on_device(anomalies, obs_weight):
    times_dev, rows_dev, members = anomalies.shape
    total_rows = rows_dev * lax.axis_size("state")
    weighted = (anomalies * obs_weight[:, :, None]).astype(jnp.bfloat16)
    partial_gram = jnp.einsum("trm,trn->tmn", weighted, weighted, preferred_element_type=jnp.float32)
    gram_sum = state_sum(partial_gram, "state")
    covariance = gram_sum / total_rows + jnp.eye(members, dtype=jnp.float32)
    transform = newton_root(covariance)
    local_product = transform[times_dev - 1]
    for time_index in range(times_dev - 2, -1, -1):
        local_product = jnp.matmul(transform[time_index], local_product, precision=HI)
    product = later_product(local_product, "tm")
    suffixes = []
    for time_index in range(times_dev - 1, -1, -1):
        product = jnp.matmul(transform[time_index], product, precision=HI)
        suffixes.append(product)
    suffix = jnp.stack(suffixes[::-1])
    smoothed = jnp.einsum("trm,tmn->trn", anomalies, suffix.astype(jnp.bfloat16), preferred_element_type=jnp.float32).astype(jnp.bfloat16)
    return (smoothed, suffix)


def solution(mesh):
    placed = (P("tm", "state", None), P("tm", "state"))
    return jax.shard_map(on_device, mesh=mesh, in_specs=placed, out_specs=(P("tm", "state", None), P("tm", None, None)), check_vma=False)
```

time: 135 us -> 61.3 us (0.45)
  waiting for transfers between devices: 93.3 us -> 27.6 us
  starting transfers between devices: 0.04 us -> 16.2 us
  between operations: 14.2 us -> 0.9 us
  blocking collectives: 9.35 us -> 0 us
    psum x1 -> x0, waiting for transfers between devices: 93.2 us -> none  [on_device(): gram_sum = lax.psum(partial_gram, 'state')]
    ppermute x0 -> x9, waiting for transfers between devices: none -> 27.6 us  [the longest x4 9.43 us: halving_sum(): value = keep + lax.ppermute(send, axis, xor_pairs(count, stride))]
    ppermute x0 -> x9, starting transfers between devices: none -> 16.2 us  [the longest x4 8.21 us: halving_sum(): value = keep + lax.ppermute(send, axis, xor_pairs(count, stride))]
    all_gather x1 -> x0, blocking collectives: 9.35 us -> none  [carried_in(): pieces = lax.all_gather(value, axis)]
    dot_general x1, matrix products: 0.67 us -> 2.23 us  [on_device(): jnp.einsum('trm,tmn->trn', anomalies, suffix.astype(jnp.bfloat16), prefer...]
    dot_general x15 -> x14, matrix products: 9.82 us -> 8.44 us  [the longest x4 2.69 us: newton_root(): jnp.matmul(inverse_root, iterate, precision=HI)]
  transfers between devices with their start and end apart: 1 -> 9, of which waited for: 1 -> 9; matrix products, arithmetic and copies ran while one was open for 0% -> 0% of each run, Pallas kernels for 0% -> 0%
where the time goes in v1:
time: 61.3 us; the launch traced here: 61.1 us
  waiting for transfers between devices  27.6 us (45%)
  starting transfers between devices  16.2 us (26%)
  matrix products  14.2 us (23%)
  local copies, waits for them, and re-layouts  1.58 us (3%)
  between operations  0.9 us (1%)
    ppermute x4, waiting for transfers between devices, halving_sum(): value = keep + lax.ppermute(send, axis, xor_pairs(count, stride))  9.43 us
    ppermute x4, waiting for transfers between devices, halving_sum(): other = lax.ppermute(value, axis, xor_pairs(count, stride))  9.25 us
    ppermute x1, waiting for transfers between devices, later_product(): shifted = lax.ppermute(local, axis, [(j, j - 1) for j in range(1, count)])  8.93 us
    ppermute x4, starting transfers between devices, halving_sum(): value = keep + lax.ppermute(send, axis, xor_pairs(count, stride))  8.21 us
    ppermute x4, starting transfers between devices, halving_sum(): other = lax.ppermute(value, axis, xor_pairs(count, stride))  6.69 us
    dot_general x1, matrix products, on_device(): jnp.einsum('trm,trn->tmn', weighted, weighted, preferred_element_type=jnp...  3.57 us
    dot_general x4, matrix products, newton_root(): jnp.matmul(inverse_root, iterate, precision=HI)  2.69 us
    dot_general x4, matrix products, newton_root(): inverse_root = jnp.matmul(factor, inverse_root, precision=HI)  2.59 us
  transfers between devices with their start and end apart: 9, of which 9 were waited for; matrix products, arithmetic and copies ran while one was open for 0% of the time, Pallas kernels for 0%

profile of v1, /device:TPU:0, one launch (start us, length us, event | category | flops | bytes accessed | tf_op | source)
XLA Modules:
  0.0 61.1 jit_solution(17459537501268701989)
XLA Ops:
  0.6 3.6 %fusion.1 = f32[2,256,256]{2,1,0:T(8,128)S(1)} fusion(bf16[2,1536,256]{2,1,0:T(8,128)(2,1)} %param.2, f32[2,1536]{1,0:T(2,128)} %param.3), kind=kOutput, calls=%fused_computation.3 | convolution fusion | flops 405012480 | bytes 2109440 | tf_op jit(solution)/shard_map/trm,trn->tmn/dot_general | solution.py:80
  4.3 0.5 collective-permute-start
  4.8 1.2 %collective-permute-done = f32[256,256]{1,0:T(8,128)S(1)} collective-permute-done((f32[256,256]{1,0:T(8,128)S(1)}, f32[256,256]{1,0:T(8,128)S(1)}, u32[]{:S(2)}, u32[]{:S(2)}) %collective-permute-start) | collective-permute-done | bytes 262176 | tf_op jit(solution)/shard_map/ppermute | solution.py:35
  6.0 3.0 %collective-permute-start.1 = (f32[128,256]{1,0:T(8,128)S(1)}, f32[128,256]{1,0:T(8,128)S(1)}, u32[]{:S(2)}, u32[]{:S(2)}) collective-permute-start(f32[128,256]{1,0:T(8,128)S(1)} %slice_select_fusion), channel_id=1, source_target_pairs={{0,2},{1,3},{2,0},{3,1},{4,6},{5,7},{6,4},{7,5},{8,10},{9,11},{10,... | collective-permute-start | bytes 393224 | tf_op jit(solution)/shard_map/ppermute | solution.py:35
  9.0 3.8 %collective-permute-done.1 = f32[128,256]{1,0:T(8,128)S(1)} collective-permute-done((f32[128,256]{1,0:T(8,128)S(1)}, f32[128,256]{1,0:T(8,128)S(1)}, u32[]{:S(2)}, u32[]{:S(2)}) %collective-permute-start.1) | collective-permute-done | bytes 131104 | tf_op jit(solution)/shard_map/ppermute | solution.py:35
  12.8 1.9 %collective-permute-start.2 = (f32[64,256]{1,0:T(8,128)S(1)}, f32[64,256]{1,0:T(8,128)S(1)}, u32[]{:S(2)}, u32[]{:S(2)}) collective-permute-start(f32[64,256]{1,0:T(8,128)S(1)} %slice_select_fusion.1), channel_id=1, source_target_pairs={{0,4},{1,5},{2,6},{3,7},{4,0},{5,1},{6,2},{7,3},{8,12},{9,13},{10,... | collective-permute-start | bytes 196616 | tf_op jit(solution)/shard_map/ppermute | solution.py:35
  14.7 2.5 %collective-permute-done.2 = f32[64,256]{1,0:T(8,128)S(1)} collective-permute-done((f32[64,256]{1,0:T(8,128)S(1)}, f32[64,256]{1,0:T(8,128)S(1)}, u32[]{:S(2)}, u32[]{:S(2)}) %collective-permute-start.2) | collective-permute-done | bytes 65568 | tf_op jit(solution)/shard_map/ppermute | solution.py:35
  17.2 2.9 %collective-permute-start.3 = (f32[32,256]{1,0:T(8,128)S(1)}, f32[32,256]{1,0:T(8,128)S(1)}, u32[]{:S(2)}, u32[]{:S(2)}) collective-permute-start(f32[32,256]{1,0:T(8,128)S(1)} %slice_select_fusion.2), channel_id=1, source_target_pairs={{0,8},{1,9},{2,10},{3,11},{4,12},{5,13},{6,14},{7,15},{8,0},{9,1},... | collective-permute-start | bytes 98312 | tf_op jit(solution)/shard_map/ppermute | solution.py:35
  20.1 2.0 %collective-permute-done.3 = f32[32,256]{1,0:T(8,128)S(1)} collective-permute-done((f32[32,256]{1,0:T(8,128)S(1)}, f32[32,256]{1,0:T(8,128)S(1)}, u32[]{:S(2)}, u32[]{:S(2)}) %collective-permute-start.3) | collective-permute-done | bytes 32800 | tf_op jit(solution)/shard_map/ppermute | solution.py:35
  22.1 2.8 %collective-permute-start.4 = (f32[32,256]{1,0:T(8,128)S(1)}, f32[32,256]{1,0:T(8,128)S(1)}, u32[]{:S(2)}, u32[]{:S(2)}) collective-permute-start(f32[32,256]{1,0:T(8,128)S(1)} %select_add_fusion.2), channel_id=1, source_target_pairs={{0,8},{1,9},{2,10},{3,11},{4,12},{5,13},{6,14},{7,15},{8,0},{9,1},... | collective-permute-start | bytes 98312 | tf_op jit(solution)/shard_map/ppermute | solution.py:38
  24.9 2.1 %collective-permute-done.4 = f32[32,256]{1,0:T(8,128)S(1)} collective-permute-done((f32[32,256]{1,0:T(8,128)S(1)}, f32[32,256]{1,0:T(8,128)S(1)}, u32[]{:S(2)}, u32[]{:S(2)}) %collective-permute-start.4) | collective-permute-done | bytes 32800 | tf_op jit(solution)/shard_map/ppermute | solution.py:38
  27.0 2.2 %collective-permute-start.5 = (f32[64,256]{1,0:T(8,128)S(1)}, f32[64,256]{1,0:T(8,128)S(1)}, u32[]{:S(2)}, u32[]{:S(2)}) collective-permute-start(f32[64,256]{1,0:T(8,128)S(1)} %maximum_select_fusion.3), channel_id=1, source_target_pairs={{0,4},{1,5},{2,6},{3,7},{4,0},{5,1},{6,2},{7,3},{8,12},{9,13},{10,... | collective-permute-start | bytes 196616 | tf_op jit(solution)/shard_map/ppermute | solution.py:38
  29.2 2.2 %collective-permute-done.5 = f32[64,256]{1,0:T(8,128)S(1)} collective-permute-done((f32[64,256]{1,0:T(8,128)S(1)}, f32[64,256]{1,0:T(8,128)S(1)}, u32[]{:S(2)}, u32[]{:S(2)}) %collective-permute-start.5) | collective-permute-done | bytes 65568 | tf_op jit(solution)/shard_map/ppermute | solution.py:38
  31.5 1.6 %collective-permute-start.6 = (f32[128,256]{1,0:T(8,128)S(1)}, f32[128,256]{1,0:T(8,128)S(1)}, u32[]{:S(2)}, u32[]{:S(2)}) collective-permute-start(f32[128,256]{1,0:T(8,128)S(1)} %maximum_select_fusion.2), channel_id=1, source_target_pairs={{0,2},{1,3},{2,0},{3,1},{4,6},{5,7},{6,4},{7,5},{8,10},{9,11},{10,... | collective-permute-start | bytes 393224 | tf_op jit(solution)/shard_map/ppermute | solution.py:38
  33.1 3.4 %collective-permute-done.6 = f32[128,256]{1,0:T(8,128)S(1)} collective-permute-done((f32[128,256]{1,0:T(8,128)S(1)}, f32[128,256]{1,0:T(8,128)S(1)}, u32[]{:S(2)}, u32[]{:S(2)}) %collective-permute-start.6) | collective-permute-done | bytes 131104 | tf_op jit(solution)/shard_map/ppermute | solution.py:38
  36.5 0.1 collective-permute-start.7
  36.7 1.5 %collective-permute-done.7 = f32[256,256]{1,0:T(8,128)S(1)} collective-permute-done((f32[256,256]{1,0:T(8,128)S(1)}, f32[256,256]{1,0:T(8,128)S(1)}, u32[]{:S(2)}, u32[]{:S(2)}) %collective-permute-start.7) | collective-permute-done | bytes 262176 | tf_op jit(solution)/shard_map/ppermute | solution.py:38
  38.1 0.1 fusion.7
  38.2 0.2 abs_reduce_fusion
  38.3 0.1 reduce_max.9
  38.5 0.7 %fusion.6 = f32[2,256,256]{2,1,0:T(8,128)S(1)} fusion(f32[256,256]{1,0:T(8,128)S(1)} %fusion.14, f32[256,256]{1,0:T(8,128)S(1)} %fusion.15, f32[2,256,256]{2,1,0:T(8,128)S(1)} %bitcast.40, f32[2]{0:T(128)S(1)} %reduce_max.9), kind=kOutput, calls=%fused_computation.13 | convolution fusion | flops 403177472 | bytes 1572872 | tf_op jit(solution)/shard_map/dot_general | solution.py:54
  39.2 0.7 %fusion.19 = f32[2,256,256]{2,1,0:T(8,128)S(1)} fusion(f32[2,256,256]{2,1,0:T(8,128)S(1)} %fusion.6, f32[2,256,256]{2,1,0:T(8,128)S(1)} %bitcast.41, f32[2]{0:T(128)S(1)} %reduce_max.9, f32[256,256]{1,0:T(8,128)S(1)} %fusion.14), kind=kOutput, calls=%fused_computation.42 | convolution fusion | flops 402915328 | bytes 1835016 | tf_op jit(solution)/shard_map/dot_general | solution.py:55
  39.9 0.6 %fusion.11 = f32[2,256,256]{2,1,0:T(8,128)S(1)} fusion(f32[2,256,256]{2,1,0:T(8,128)S(1)} %fusion.6, f32[256,256]{1,0:T(8,128)S(1)} %fusion.14), kind=kOutput, calls=%fused_computation.28 | convolution fusion | flops 402653184 | bytes 1310720 | tf_op jit(solution)/shard_map/dot_general | solution.py:56
  40.6 0.7 %fusion.5 = f32[2,256,256]{2,1,0:T(8,128)S(1)} fusion(f32[2,256,256]{2,1,0:T(8,128)S(1)} %fusion.11, f32[2,256,256]{2,1,0:T(8,128)S(1)} %fusion.19, f32[256,256]{1,0:T(8,128)S(1)} %fusion.15), kind=kOutput, calls=%fused_computation.11 | convolution fusion | flops 402915328 | bytes 1835008 | tf_op jit(solution)/shard_map/dot_general | solution.py:54
  41.2 0.7 %fusion.21 = f32[2,256,256]{2,1,0:T(8,128)S(1)} fusion(f32[2,256,256]{2,1,0:T(8,128)S(1)} %fusion.19, f32[2,256,256]{2,1,0:T(8,128)S(1)} %fusion.5), kind=kOutput, calls=%fused_computation.46 | convolution fusion | flops 402653184 | bytes 1572864 | tf_op jit(solution)/shard_map/dot_general | solution.py:55
  41.9 0.7 %fusion.20 = f32[2,256,256]{2,1,0:T(8,128)S(1)} fusion(f32[2,256,256]{2,1,0:T(8,128)S(1)} %fusion.5, f32[2,256,256]{2,1,0:T(8,128)S(1)} %fusion.11), kind=kOutput, calls=%fused_computation.45 | convolution fusion | flops 402653184 | bytes 1572864 | tf_op jit(solution)/shard_map/dot_general | solution.py:56
  42.5 0.7 %fusion.4 = f32[2,256,256]{2,1,0:T(8,128)S(1)} fusion(f32[2,256,256]{2,1,0:T(8,128)S(1)} %fusion.20, f32[2,256,256]{2,1,0:T(8,128)S(1)} %fusion.21, f32[256,256]{1,0:T(8,128)S(1)} %fusion.15), kind=kOutput, calls=%fused_computation.9 | convolution fusion | flops 402915328 | bytes 1835008 | tf_op jit(solution)/shard_map/dot_general | solution.py:54
  43.2 0.7 %fusion.22 = f32[2,256,256]{2,1,0:T(8,128)S(1)} fusion(f32[2,256,256]{2,1,0:T(8,128)S(1)} %fusion.4, f32[2,256,256]{2,1,0:T(8,128)S(1)} %fusion.20), kind=kOutput, calls=%fused_computation.47 | convolution fusion | flops 402653184 | bytes 1572864 | tf_op jit(solution)/shard_map/dot_general | solution.py:56
  43.9 0.7 %fusion.23 = f32[2,256,256]{2,1,0:T(8,128)S(1)} fusion(f32[2,256,256]{2,1,0:T(8,128)S(1)} %fusion.21, f32[2,256,256]{2,1,0:T(8,128)S(1)} %fusion.4), kind=kOutput, calls=%fused_computation.48 | convolution fusion | flops 402653184 | bytes 1572864 | tf_op jit(solution)/shard_map/dot_general | solution.py:55
  44.5 0.7 %fusion.3 = f32[2,256,256]{2,1,0:T(8,128)S(1)} fusion(f32[2,256,256]{2,1,0:T(8,128)S(1)} %fusion.22, f32[2,256,256]{2,1,0:T(8,128)S(1)} %fusion.23, f32[256,256]{1,0:T(8,128)S(1)} %fusion.15), kind=kOutput, calls=%fused_computation.7 | convolution fusion | flops 402915328 | bytes 1835008 | tf_op jit(solution)/shard_map/dot_general | solution.py:54
  45.2 0.7 %convolution_divide_fusion = f32[2,256,256]{2,1,0:T(8,128)S(1)} fusion(f32[2,256,256]{2,1,0:T(8,128)S(1)} %fusion.3, f32[2,256,256]{2,1,0:T(8,128)S(1)} %fusion.22, f32[2]{0:T(128)S(1)} %sqrt.7), kind=kOutput, calls=%fused_computation.5 | convolution fusion | flops 402784256 | bytes 1572872 | tf_op jit(solution)/shard_map/dot_general | solution.py:56
  45.8 0.4 fusion.16
  46.2 1.3 %collective-permute-start.8 = (f32[256,256]{1,0:T(8,128)S(1)}, f32[256,256]{1,0:T(8,128)S(1)}, u32[]{:S(2)}, u32[]{:S(2)}) collective-permute-start(f32[256,256]{1,0:T(8,128)S(1)} %fusion.16), channel_id=1, source_target_pairs={{16,0},{17,1},{18,2},{19,3},{20,4},{21,5},{22,6},{23,7},{24,8},{25... | collective-permute-start | bytes 786440 | tf_op jit(solution)/shard_map/ppermute | solution.py:65
  47.5 8.9 %collective-permute-done.8 = f32[256,256]{1,0:T(8,128)S(1)} collective-permute-done((f32[256,256]{1,0:T(8,128)S(1)}, f32[256,256]{1,0:T(8,128)S(1)}, u32[]{:S(2)}, u32[]{:S(2)}) %collective-permute-start.8) | collective-permute-done | bytes 262176 | tf_op jit(solution)/shard_map/ppermute | solution.py:65
  56.5 0.4 fusion.9
  56.9 0.4 convolution_bitcast_fusion
  57.3 0.0 copy-start
  57.3 2.2 %fusion = bf16[2,1536,256]{1,2,0:T(8,128)(2,1)S(1)} fusion(bf16[2,1536,256]{2,1,0:T(8,128)(2,1)} %param.2, f32[2,256,256]{2,1,0:T(8,128)S(1)} %pad_maximum_fusion), kind=kOutput, calls=%fused_computation.2 | convolution fusion | flops 403570688 | bytes 3670016 | tf_op jit(solution)/shard_map/trm,tmn->trn/dot_general | solution.py:93
  59.6 0.0 copy-done
  59.6 1.6 %copy.9 = bf16[2,1536,256]{2,1,0:T(8,128)(2,1)} copy(bf16[2,1536,256]{1,2,0:T(8,128)(2,1)S(1)} %fusion) | data formatting | bytes 3145728
  (15 shorter events, 0.3 us)
Async XLA Ops:
  4.3 1.7 %collective-permute-start = (f32[256,256]{1,0:T(8,128)S(1)}, f32[256,256]{1,0:T(8,128)S(1)}, u32[]{:S(2)}, u32[]{:S(2)}) collective-permute-start(f32[256,256]{1,0:T(8,128)S(1)} %select_bitcast_fusion), channel_id=1, source_target_pairs={{0,1},{1,0},{2,3},{3,2},{4,5},{5,4},{6,7},{7,6},{8,9},{9,8},{10,11... | collective-permute-start | bytes 786440 | tf_op jit(solution)/shard_map/ppermute | solution.py:35
  6.0 6.8 %collective-permute-start.1 = (f32[128,256]{1,0:T(8,128)S(1)}, f32[128,256]{1,0:T(8,128)S(1)}, u32[]{:S(2)}, u32[]{:S(2)}) collective-permute-start(f32[128,256]{1,0:T(8,128)S(1)} %slice_select_fusion), channel_id=1, source_target_pairs={{0,2},{1,3},{2,0},{3,1},{4,6},{5,7},{6,4},{7,5},{8,10},{9,11},{10,... | collective-permute-start | bytes 393224 | tf_op jit(solution)/shard_map/ppermute | solution.py:35
  12.8 4.3 %collective-permute-start.2 = (f32[64,256]{1,0:T(8,128)S(1)}, f32[64,256]{1,0:T(8,128)S(1)}, u32[]{:S(2)}, u32[]{:S(2)}) collective-permute-start(f32[64,256]{1,0:T(8,128)S(1)} %slice_select_fusion.1), channel_id=1, source_target_pairs={{0,4},{1,5},{2,6},{3,7},{4,0},{5,1},{6,2},{7,3},{8,12},{9,13},{10,... | collective-permute-start | bytes 196616 | tf_op jit(solution)/shard_map/ppermute | solution.py:35
  17.2 4.9 %collective-permute-start.3 = (f32[32,256]{1,0:T(8,128)S(1)}, f32[32,256]{1,0:T(8,128)S(1)}, u32[]{:S(2)}, u32[]{:S(2)}) collective-permute-start(f32[32,256]{1,0:T(8,128)S(1)} %slice_select_fusion.2), channel_id=1, source_target_pairs={{0,8},{1,9},{2,10},{3,11},{4,12},{5,13},{6,14},{7,15},{8,0},{9,1},... | collective-permute-start | bytes 98312 | tf_op jit(solution)/shard_map/ppermute | solution.py:35
  22.1 4.9 %collective-permute-start.4 = (f32[32,256]{1,0:T(8,128)S(1)}, f32[32,256]{1,0:T(8,128)S(1)}, u32[]{:S(2)}, u32[]{:S(2)}) collective-permute-start(f32[32,256]{1,0:T(8,128)S(1)} %select_add_fusion.2), channel_id=1, source_target_pairs={{0,8},{1,9},{2,10},{3,11},{4,12},{5,13},{6,14},{7,15},{8,0},{9,1},... | collective-permute-start | bytes 98312 | tf_op jit(solution)/shard_map/ppermute | solution.py:38
  27.0 4.5 %collective-permute-start.5 = (f32[64,256]{1,0:T(8,128)S(1)}, f32[64,256]{1,0:T(8,128)S(1)}, u32[]{:S(2)}, u32[]{:S(2)}) collective-permute-start(f32[64,256]{1,0:T(8,128)S(1)} %maximum_select_fusion.3), channel_id=1, source_target_pairs={{0,4},{1,5},{2,6},{3,7},{4,0},{5,1},{6,2},{7,3},{8,12},{9,13},{10,... | collective-permute-start | bytes 196616 | tf_op jit(solution)/shard_map/ppermute | solution.py:38
  31.5 5.0 %collective-permute-start.6 = (f32[128,256]{1,0:T(8,128)S(1)}, f32[128,256]{1,0:T(8,128)S(1)}, u32[]{:S(2)}, u32[]{:S(2)}) collective-permute-start(f32[128,256]{1,0:T(8,128)S(1)} %maximum_select_fusion.2), channel_id=1, source_target_pairs={{0,2},{1,3},{2,0},{3,1},{4,6},{5,7},{6,4},{7,5},{8,10},{9,11},{10,... | collective-permute-start | bytes 393224 | tf_op jit(solution)/shard_map/ppermute | solution.py:38
  36.5 1.6 %collective-permute-start.7 = (f32[256,256]{1,0:T(8,128)S(1)}, f32[256,256]{1,0:T(8,128)S(1)}, u32[]{:S(2)}, u32[]{:S(2)}) collective-permute-start(f32[256,256]{1,0:T(8,128)S(1)} %maximum_select_fusion.1), channel_id=1, source_target_pairs={{0,1},{1,0},{2,3},{3,2},{4,5},{5,4},{6,7},{7,6},{8,9},{9,8},{10,11... | collective-permute-start | bytes 786440 | tf_op jit(solution)/shard_map/ppermute | solution.py:38
  46.2 10.2 %collective-permute-start.8 = (f32[256,256]{1,0:T(8,128)S(1)}, f32[256,256]{1,0:T(8,128)S(1)}, u32[]{:S(2)}, u32[]{:S(2)}) collective-permute-start(f32[256,256]{1,0:T(8,128)S(1)} %fusion.16), channel_id=1, source_target_pairs={{16,0},{17,1},{18,2},{19,3},{20,4},{21,5},{22,6},{23,7},{24,8},{25... | collective-permute-start | bytes 786440 | tf_op jit(solution)/shard_map/ppermute | solution.py:65
  57.3 2.2 %copy-start = (f32[2,256,256]{2,1,0:T(8,128)}, f32[2,256,256]{2,1,0:T(8,128)S(1)}, u32[]{:S(2)}) copy-start(f32[2,256,256]{2,1,0:T(8,128)S(1)} %pad_maximum_fusion) | copy-start | bytes 1572868

commit v2 on v1

--- a/solution.py
+++ b/solution.py
@@ -4,45 +4,66 @@
 from jax.sharding import PartitionSpec as P
 
 NS_STEPS = 4
-HI = lax.Precision.HIGHEST
+HI = lax.Precision.HIGH
+CHIP_RADIX = 4
 
 
-def xor_pairs(count, stride):
-    return [(source, source ^ stride) for source in range(count)]
+def radix_plan(count):
+    plan, place = [], 1
+    if count % 2 == 0 and count > 1:
+        plan.append((2, 1))
+        place = 2
+    while place < count:
+        radix = min(CHIP_RADIX, count // place)
+        plan.append((radix, place))
+        place *= radix
+    return plan
 
 
-def strides_of(count):
-    out, stride = [], 1
-    while stride < count:
-        out.append(stride)
-        stride *= 2
-    return out
+def digit_pairs(count, radix, place, offset):
+    pairs = []
+    for source in range(count):
+        digit = (source // place) % radix
+        pairs.append((source, source + (((digit + offset) % radix) - digit) * place))
+    return pairs
 
 
-def halving_sum(value, axis):
+def grouped_sum(value, axis):
     count, me = lax.axis_size(axis), lax.axis_index(axis)
-    strides = strides_of(count)
+    plan = radix_plan(count)
     rows = value.shape[0]
-    padded = -(-rows // count) * count
-    if padded != rows:
-        value = jnp.concatenate([value, jnp.zeros((padded - rows,) + value.shape[1:], value.dtype)])
-    for stride in strides:
-        upper = (me // stride) % 2 == 1
-        half = value.shape[0] // 2
-        low, high = value[:half], value[half:]
-        send = jnp.where(upper, low, high)
-        keep = jnp.where(upper, high, low)
-        value = keep + lax.ppermute(send, axis, xor_pairs(count, stride))
-    for stride in strides[::-1]:
-        upper = (me // stride) % 2 == 1
-        other = lax.ppermute(value, axis, xor_pairs(count, stride))
-        value = jnp.where(upper, jnp.concatenate([other, value]), jnp.concatenate([value, other]))
-    return value[:rows]
+    for radix, place in plan:
+        digit = (me // place) % radix
+        if radix == 2:
+            upper = digit == 1
+            half = value.shape[0] // 2
+            low, high = value[:half], value[half:]
+            send, keep = jnp.where(upper, low, high), jnp.where(upper, high, low)
+            value = keep + lax.ppermute(send, axis, digit_pairs(count, radix, place, 1))
+            continue
+        chunk = value.shape[0] // radix
+        pieces = value.reshape((radix, chunk) + value.shape[1:])
+        total = lax.dynamic_index_in_dim(pieces, digit, 0, keepdims=False)
+        for offset in range(1, radix):
+            send = lax.dynamic_index_in_dim(pieces, (digit + offset) % radix, 0, keepdims=False)
+            total = total + lax.ppermute(send, axis, digit_pairs(count, radix, place, offset))
+        value = total
+    for radix, place in plan[::-1]:
+        digit = (me // place) % radix
+        if radix == 2:
+            other = lax.ppermute(value, axis, digit_pairs(count, radix, place, 1))
+            value = jnp.where(digit == 1, jnp.concatenate([other, value]), jnp.concatenate([value, other]))
+            continue
+        got = [value] + [lax.ppermute(value, axis, digit_pairs(count, radix, place, offset)) for offset in range(1, radix)]
+        stacked = jnp.stack(got)
+        order = (digit - jnp.arange(radix)) % radix
+        value = jnp.take(stacked, order, axis=0).reshape((radix * value.shape[0],) + value.shape[1:])
+    return value
 
 
 def state_sum(partial_gram, axis):
     times, n, _ = partial_gram.shape
-    return halving_sum(partial_gram.reshape(times * n, n), axis).reshape(times, n, n)
+    return grouped_sum(partial_gram.reshape(times * n, n), axis).reshape(times, n, n)
 
 
 def newton_root(covariance):

time: 61.3 us -> 54.6 us (0.89)
  waiting for transfers between devices: 27.6 us -> 23.5 us
  matrix products: 14.2 us -> 11 us
  local copies, waits for them, and re-layouts: 1.58 us -> 2.33 us
    ppermute x8 -> x10, waiting for transfers between devices: 18.7 us -> 14.6 us  [the longest x3 4.34 us: grouped_sum(): lax.ppermute(value, axis, digit_pairs(count, radix, place, offset))]
    dot_general x4, matrix products: 2.59 us -> 1.54 us  [newton_root(): inverse_root = jnp.matmul(factor, inverse_root, precision=HI)]
    dot_general x4, matrix products: 2.69 us -> 1.64 us  [newton_root(): jnp.matmul(inverse_root, iterate, precision=HI)]
    dot_general x3, matrix products: 2.01 us -> 1.19 us  [newton_root(): iterate = jnp.matmul(iterate, factor, precision=HI)]
    ppermute x8 -> x10, starting transfers between devices: 14.9 us -> 14.8 us  [the longest x3 5.92 us: grouped_sum(): lax.ppermute(send, axis, digit_pairs(count, radix, place, offset))]
  transfers between devices with their start and end apart: 9 -> 11, of which waited for: 9 -> 11; matrix products, arithmetic and copies ran while one was open for 0% -> 0% of each run, Pallas kernels for 0% -> 0%
where the time goes in v2:
time: 54.6 us; the launch traced here: 54.4 us
  waiting for transfers between devices  23.5 us (43%)
  starting transfers between devices  16.1 us (29%)
  matrix products  11 us (20%)
  local copies, waits for them, and re-layouts  2.33 us (4%)
  between operations  0.91 us (2%)
  other arithmetic  0.69 us (1%)
    ppermute x1, waiting for transfers between devices, later_product(): shifted = lax.ppermute(local, axis, [(j, j - 1) for j in range(1, count)])  8.93 us
    ppermute x3, starting transfers between devices, grouped_sum(): lax.ppermute(send, axis, digit_pairs(count, radix, place, offset))  5.92 us
    ppermute x3, waiting for transfers between devices, grouped_sum(): lax.ppermute(value, axis, digit_pairs(count, radix, place, offset))  4.34 us
    ppermute x2, waiting for transfers between devices, grouped_sum(): other = lax.ppermute(value, axis, digit_pairs(count, radix, place, 1))  3.62 us
    dot_general x1, matrix products, on_device(): jnp.einsum('trm,trn->tmn', weighted, weighted, preferred_element_type=jnp...  3.57 us
    ppermute x2, waiting for transfers between devices, grouped_sum(): value = keep + lax.ppermute(send, axis, digit_pairs(count, radix, place, 1))  3.38 us
    ppermute x3, waiting for transfers between devices, grouped_sum(): lax.ppermute(send, axis, digit_pairs(count, radix, place, offset))  3.22 us
    ppermute x2, starting transfers between devices, grouped_sum(): value = keep + lax.ppermute(send, axis, digit_pairs(count, radix, place, 1))  3.17 us
  transfers between devices with their start and end apart: 11, of which 11 were waited for; matrix products, arithmetic and copies ran while one was open for 0% of the time, Pallas kernels for 0%

profile of v2, /device:TPU:0, one launch (start us, length us, event | category | flops | bytes accessed | tf_op | source)
XLA Modules:
  0.0 54.4 jit_solution(8047033599002769099)
XLA Ops:
  0.6 3.6 %fusion.1 = f32[2,256,256]{2,1,0:T(8,128)S(1)} fusion(bf16[2,1536,256]{2,1,0:T(8,128)(2,1)} %param.2, f32[2,1536]{1,0:T(2,128)} %param.3), kind=kOutput, calls=%fused_computation.4 | convolution fusion | flops 405012480 | bytes 2109440 | tf_op jit(solution)/shard_map/trm,trn->tmn/dot_general | solution.py:101
  4.3 0.5 collective-permute-start
  4.8 1.2 %collective-permute-done = f32[256,256]{1,0:T(8,128)S(1)} collective-permute-done((f32[256,256]{1,0:T(8,128)S(1)}, f32[256,256]{1,0:T(8,128)S(1)}, u32[]{:S(2)}, u32[]{:S(2)}) %collective-permute-start) | collective-permute-done | bytes 262176 | tf_op jit(solution)/shard_map/ppermute | solution.py:42
  6.0 2.9 %collective-permute-start.1 = (f32[64,256]{1,0:T(8,128)S(1)}, f32[64,256]{1,0:T(8,128)S(1)}, u32[]{:S(2)}, u32[]{:S(2)}) collective-permute-start(f32[64,256]{1,0:T(8,128)S(1)} %get-tuple-element.6), channel_id=1, source_target_pairs={{0,2},{1,3},{2,4},{3,5},{4,6},{5,7},{6,0},{7,1},{8,10},{9,11},{10,... | collective-permute-start | bytes 196616 | tf_op jit(solution)/shard_map/ppermute | solution.py:49
  9.0 1.1 %collective-permute-start.3 = (f32[64,256]{1,0:T(8,128)S(1)}, f32[64,256]{1,0:T(8,128)S(1)}, u32[]{:S(2)}, u32[]{:S(2)}) collective-permute-start(f32[64,256]{1,0:T(8,128)S(1)} %get-tuple-element.7), channel_id=1, source_target_pairs={{0,6},{1,7},{2,0},{3,1},{4,2},{5,3},{6,4},{7,5},{8,14},{9,15},{10,... | collective-permute-start | bytes 196616 | tf_op jit(solution)/shard_map/ppermute | solution.py:49
  10.0 1.9 %collective-permute-start.2 = (f32[64,256]{1,0:T(8,128)S(1)}, f32[64,256]{1,0:T(8,128)S(1)}, u32[]{:S(2)}, u32[]{:S(2)}) collective-permute-start(f32[64,256]{1,0:T(8,128)S(1)} %get-tuple-element.8), channel_id=1, source_target_pairs={{0,4},{1,5},{2,6},{3,7},{4,0},{5,1},{6,2},{7,3},{8,12},{9,13},{10,... | collective-permute-start | bytes 196616 | tf_op jit(solution)/shard_map/ppermute | solution.py:49
  12.0 0.5 collective-permute-done.1
  12.5 1.3 %collective-permute-done.3 = f32[64,256]{1,0:T(8,128)S(1)} collective-permute-done((f32[64,256]{1,0:T(8,128)S(1)}, f32[64,256]{1,0:T(8,128)S(1)}, u32[]{:S(2)}, u32[]{:S(2)}) %collective-permute-start.3) | collective-permute-done | bytes 65568 | tf_op jit(solution)/shard_map/ppermute | solution.py:49
  13.8 1.4 %collective-permute-done.2 = f32[64,256]{1,0:T(8,128)S(1)} collective-permute-done((f32[64,256]{1,0:T(8,128)S(1)}, f32[64,256]{1,0:T(8,128)S(1)}, u32[]{:S(2)}, u32[]{:S(2)}) %collective-permute-start.2) | collective-permute-done | bytes 65568 | tf_op jit(solution)/shard_map/ppermute | solution.py:49
  15.2 2.7 %collective-permute-start.4 = (f32[32,256]{1,0:T(8,128)S(1)}, f32[32,256]{1,0:T(8,128)S(1)}, u32[]{:S(2)}, u32[]{:S(2)}) collective-permute-start(f32[32,256]{1,0:T(8,128)S(1)} %slice_select_fusion), channel_id=1, source_target_pairs={{0,8},{1,9},{2,10},{3,11},{4,12},{5,13},{6,14},{7,15},{8,0},{9,1},... | collective-permute-start | bytes 98312 | tf_op jit(solution)/shard_map/ppermute | solution.py:42
  17.9 2.2 %collective-permute-done.4 = f32[32,256]{1,0:T(8,128)S(1)} collective-permute-done((f32[32,256]{1,0:T(8,128)S(1)}, f32[32,256]{1,0:T(8,128)S(1)}, u32[]{:S(2)}, u32[]{:S(2)}) %collective-permute-start.4) | collective-permute-done | bytes 32800 | tf_op jit(solution)/shard_map/ppermute | solution.py:42
  20.1 2.6 %collective-permute-start.5 = (f32[32,256]{1,0:T(8,128)S(1)}, f32[32,256]{1,0:T(8,128)S(1)}, u32[]{:S(2)}, u32[]{:S(2)}) collective-permute-start(f32[32,256]{1,0:T(8,128)S(1)} %select_add_fusion), channel_id=1, source_target_pairs={{0,8},{1,9},{2,10},{3,11},{4,12},{5,13},{6,14},{7,15},{8,0},{9,1},... | collective-permute-start | bytes 98312 | tf_op jit(solution)/shard_map/ppermute | solution.py:54
  22.7 0.1 broadcast_in_dim.30
  22.8 0.1 broadcast_in_dim.31
  22.9 2.1 %collective-permute-done.5 = f32[32,256]{1,0:T(8,128)S(1)} collective-permute-done((f32[32,256]{1,0:T(8,128)S(1)}, f32[32,256]{1,0:T(8,128)S(1)}, u32[]{:S(2)}, u32[]{:S(2)}) %collective-permute-start.5) | collective-permute-done | bytes 32800 | tf_op jit(solution)/shard_map/ppermute | solution.py:54
  25.0 1.1 %collective-permute-start.8 = (f32[64,256]{1,0:T(8,128)S(1)}, f32[64,256]{1,0:T(8,128)S(1)}, u32[]{:S(2)}, u32[]{:S(2)}) collective-permute-start(f32[64,256]{1,0:T(8,128)S(1)} %maximum_select_fusion.2), channel_id=1, source_target_pairs={{0,6},{1,7},{2,0},{3,1},{4,2},{5,3},{6,4},{7,5},{8,14},{9,15},{10,... | collective-permute-start | bytes 196616 | tf_op jit(solution)/shard_map/ppermute | solution.py:57
  26.1 1.1 %collective-permute-start.7 = (f32[64,256]{1,0:T(8,128)S(1)}, f32[64,256]{1,0:T(8,128)S(1)}, u32[]{:S(2)}, u32[]{:S(2)}) collective-permute-start(f32[64,256]{1,0:T(8,128)S(1)} %maximum_select_fusion.2), channel_id=1, source_target_pairs={{0,4},{1,5},{2,6},{3,7},{4,0},{5,1},{6,2},{7,3},{8,12},{9,13},{10,... | collective-permute-start | bytes 196616 | tf_op jit(solution)/shard_map/ppermute | solution.py:57
  27.2 0.8 %collective-permute-start.6 = (f32[64,256]{1,0:T(8,128)S(1)}, f32[64,256]{1,0:T(8,128)S(1)}, u32[]{:S(2)}, u32[]{:S(2)}) collective-permute-start(f32[64,256]{1,0:T(8,128)S(1)} %maximum_select_fusion.2), channel_id=1, source_target_pairs={{0,2},{1,3},{2,4},{3,5},{4,6},{5,7},{6,0},{7,1},{8,10},{9,11},{10,... | collective-permute-start | bytes 196616 | tf_op jit(solution)/shard_map/ppermute | solution.py:57
  28.1 1.3 %collective-permute-done.8 = f32[64,256]{1,0:T(8,128)S(1)} collective-permute-done((f32[64,256]{1,0:T(8,128)S(1)}, f32[64,256]{1,0:T(8,128)S(1)}, u32[]{:S(2)}, u32[]{:S(2)}) %collective-permute-start.8) | collective-permute-done | bytes 65568 | tf_op jit(solution)/shard_map/ppermute | solution.py:57
  29.3 1.0 %collective-permute-done.7 = f32[64,256]{1,0:T(8,128)S(1)} collective-permute-done((f32[64,256]{1,0:T(8,128)S(1)}, f32[64,256]{1,0:T(8,128)S(1)}, u32[]{:S(2)}, u32[]{:S(2)}) %collective-permute-start.7) | collective-permute-done | bytes 65568 | tf_op jit(solution)/shard_map/ppermute | solution.py:57
  30.4 2.0 %collective-permute-done.6 = f32[64,256]{1,0:T(8,128)S(1)} collective-permute-done((f32[64,256]{1,0:T(8,128)S(1)}, f32[64,256]{1,0:T(8,128)S(1)}, u32[]{:S(2)}, u32[]{:S(2)}) %collective-permute-start.6) | collective-permute-done | bytes 65568 | tf_op jit(solution)/shard_map/ppermute | solution.py:57
  32.4 0.6 %gather_fusion = f32[4,64,256]{2,1,0:T(8,128)S(1)} fusion(f32[4,64,256]{2,1,0:T(8,128)S(1)} %pad_maximum_fusion.1, s32[1024]{0:T(1024)S(1)} %pad_clamp_fusion), kind=kCustom, calls=%fused_computation | custom fusion | bytes 524304 | tf_op jit(solution)/shard_map/jit(_take)/gather | solution.py:60
  33.0 0.1 bitcast_select_fusion
  33.1 0.1 collective-permute-start.9
  33.2 1.5 %collective-permute-done.9 = f32[256,256]{1,0:T(8,128)S(1)} collective-permute-done((f32[256,256]{1,0:T(8,128)S(1)}, f32[256,256]{1,0:T(8,128)S(1)}, u32[]{:S(2)}, u32[]{:S(2)}) %collective-permute-start.9) | collective-permute-done | bytes 262176 | tf_op jit(solution)/shard_map/ppermute | solution.py:54
  34.7 0.1 fusion.7
  34.8 0.2 abs_reduce_fusion
  34.9 0.1 reduce_max.9
  35.1 0.5 fusion.6
  35.5 0.4 fusion.21
  36.0 0.4 fusion.11
  36.3 0.4 fusion.5
  36.7 0.4 fusion.26
  37.1 0.4 fusion.25
  37.5 0.4 fusion.4
  37.9 0.4 fusion.27
  38.3 0.4 fusion.28
  38.7 0.4 fusion.3
  39.1 0.4 convolution_divide_fusion
  39.5 0.3 fusion.16
  39.8 1.3 %collective-permute-start.10 = (f32[256,256]{1,0:T(8,128)S(1)}, f32[256,256]{1,0:T(8,128)S(1)}, u32[]{:S(2)}, u32[]{:S(2)}) collective-permute-start(f32[256,256]{1,0:T(8,128)S(1)} %fusion.16), channel_id=1, source_target_pairs={{16,0},{17,1},{18,2},{19,3},{20,4},{21,5},{22,6},{23,7},{24,8},{25... | collective-permute-start | bytes 786440 | tf_op jit(solution)/shard_map/ppermute | solution.py:86
  41.1 8.9 %collective-permute-done.10 = f32[256,256]{1,0:T(8,128)S(1)} collective-permute-done((f32[256,256]{1,0:T(8,128)S(1)}, f32[256,256]{1,0:T(8,128)S(1)}, u32[]{:S(2)}, u32[]{:S(2)}) %collective-permute-start.10) | collective-permute-done | bytes 262176 | tf_op jit(solution)/shard_map/ppermute | solution.py:86
  50.0 0.3 fusion.9
  50.3 0.3 convolution_bitcast_fusion
  50.6 0.0 copy-start
  50.6 2.2 %fusion = bf16[2,1536,256]{1,2,0:T(8,128)(2,1)S(1)} fusion(bf16[2,1536,256]{2,1,0:T(8,128)(2,1)} %param.2, f32[2,256,256]{2,1,0:T(8,128)S(1)} %pad_maximum_fusion), kind=kOutput, calls=%fused_computation.3 | convolution fusion | flops 403570688 | bytes 3670016 | tf_op jit(solution)/shard_map/trm,tmn->trn/dot_general | solution.py:114
  52.9 0.0 copy-done
  52.9 1.6 %copy.9 = bf16[2,1536,256]{2,1,0:T(8,128)(2,1)} copy(bf16[2,1536,256]{1,2,0:T(8,128)(2,1)S(1)} %fusion) | data formatting | bytes 3145728
  (16 shorter events, 0.3 us)
Async XLA Ops:
  4.3 1.7 %collective-permute-start = (f32[256,256]{1,0:T(8,128)S(1)}, f32[256,256]{1,0:T(8,128)S(1)}, u32[]{:S(2)}, u32[]{:S(2)}) collective-permute-start(f32[256,256]{1,0:T(8,128)S(1)} %select_bitcast_fusion), channel_id=1, source_target_pairs={{0,1},{1,0},{2,3},{3,2},{4,5},{5,4},{6,7},{7,6},{8,9},{9,8},{10,11... | collective-permute-start | bytes 786440 | tf_op jit(solution)/shard_map/ppermute | solution.py:42
  6.0 6.5 %collective-permute-start.1 = (f32[64,256]{1,0:T(8,128)S(1)}, f32[64,256]{1,0:T(8,128)S(1)}, u32[]{:S(2)}, u32[]{:S(2)}) collective-permute-start(f32[64,256]{1,0:T(8,128)S(1)} %get-tuple-element.6), channel_id=1, source_target_pairs={{0,2},{1,3},{2,4},{3,5},{4,6},{5,7},{6,0},{7,1},{8,10},{9,11},{10,... | collective-permute-start | bytes 196616 | tf_op jit(solution)/shard_map/ppermute | solution.py:49
  9.0 4.8 %collective-permute-start.3 = (f32[64,256]{1,0:T(8,128)S(1)}, f32[64,256]{1,0:T(8,128)S(1)}, u32[]{:S(2)}, u32[]{:S(2)}) collective-permute-start(f32[64,256]{1,0:T(8,128)S(1)} %get-tuple-element.7), channel_id=1, source_target_pairs={{0,6},{1,7},{2,0},{3,1},{4,2},{5,3},{6,4},{7,5},{8,14},{9,15},{10,... | collective-permute-start | bytes 196616 | tf_op jit(solution)/shard_map/ppermute | solution.py:49
  10.0 5.1 %collective-permute-start.2 = (f32[64,256]{1,0:T(8,128)S(1)}, f32[64,256]{1,0:T(8,128)S(1)}, u32[]{:S(2)}, u32[]{:S(2)}) collective-permute-start(f32[64,256]{1,0:T(8,128)S(1)} %get-tuple-element.8), channel_id=1, source_target_pairs={{0,4},{1,5},{2,6},{3,7},{4,0},{5,1},{6,2},{7,3},{8,12},{9,13},{10,... | collective-permute-start | bytes 196616 | tf_op jit(solution)/shard_map/ppermute | solution.py:49
  15.2 4.9 %collective-permute-start.4 = (f32[32,256]{1,0:T(8,128)S(1)}, f32[32,256]{1,0:T(8,128)S(1)}, u32[]{:S(2)}, u32[]{:S(2)}) collective-permute-start(f32[32,256]{1,0:T(8,128)S(1)} %slice_select_fusion), channel_id=1, source_target_pairs={{0,8},{1,9},{2,10},{3,11},{4,12},{5,13},{6,14},{7,15},{8,0},{9,1},... | collective-permute-start | bytes 98312 | tf_op jit(solution)/shard_map/ppermute | solution.py:42
  20.1 4.9 %collective-permute-start.5 = (f32[32,256]{1,0:T(8,128)S(1)}, f32[32,256]{1,0:T(8,128)S(1)}, u32[]{:S(2)}, u32[]{:S(2)}) collective-permute-start(f32[32,256]{1,0:T(8,128)S(1)} %select_add_fusion), channel_id=1, source_target_pairs={{0,8},{1,9},{2,10},{3,11},{4,12},{5,13},{6,14},{7,15},{8,0},{9,1},... | collective-permute-start | bytes 98312 | tf_op jit(solution)/shard_map/ppermute | solution.py:54
  25.0 4.3 %collective-permute-start.8 = (f32[64,256]{1,0:T(8,128)S(1)}, f32[64,256]{1,0:T(8,128)S(1)}, u32[]{:S(2)}, u32[]{:S(2)}) collective-permute-start(f32[64,256]{1,0:T(8,128)S(1)} %maximum_select_fusion.2), channel_id=1, source_target_pairs={{0,6},{1,7},{2,0},{3,1},{4,2},{5,3},{6,4},{7,5},{8,14},{9,15},{10,... | collective-permute-start | bytes 196616 | tf_op jit(solution)/shard_map/ppermute | solution.py:57
  26.1 4.3 %collective-permute-start.7 = (f32[64,256]{1,0:T(8,128)S(1)}, f32[64,256]{1,0:T(8,128)S(1)}, u32[]{:S(2)}, u32[]{:S(2)}) collective-permute-start(f32[64,256]{1,0:T(8,128)S(1)} %maximum_select_fusion.2), channel_id=1, source_target_pairs={{0,4},{1,5},{2,6},{3,7},{4,0},{5,1},{6,2},{7,3},{8,12},{9,13},{10,... | collective-permute-start | bytes 196616 | tf_op jit(solution)/shard_map/ppermute | solution.py:57
  27.2 5.2 %collective-permute-start.6 = (f32[64,256]{1,0:T(8,128)S(1)}, f32[64,256]{1,0:T(8,128)S(1)}, u32[]{:S(2)}, u32[]{:S(2)}) collective-permute-start(f32[64,256]{1,0:T(8,128)S(1)} %maximum_select_fusion.2), channel_id=1, source_target_pairs={{0,2},{1,3},{2,4},{3,5},{4,6},{5,7},{6,0},{7,1},{8,10},{9,11},{10,... | collective-permute-start | bytes 196616 | tf_op jit(solution)/shard_map/ppermute | solution.py:57
  33.1 1.6 %collective-permute-start.9 = (f32[256,256]{1,0:T(8,128)S(1)}, f32[256,256]{1,0:T(8,128)S(1)}, u32[]{:S(2)}, u32[]{:S(2)}) collective-permute-start(f32[256,256]{1,0:T(8,128)S(1)} %bitcast_select_fusion), channel_id=1, source_target_pairs={{0,1},{1,0},{2,3},{3,2},{4,5},{5,4},{6,7},{7,6},{8,9},{9,8},{10,11... | collective-permute-start | bytes 786440 | tf_op jit(solution)/shard_map/ppermute | solution.py:54
  39.8 10.2 %collective-permute-start.10 = (f32[256,256]{1,0:T(8,128)S(1)}, f32[256,256]{1,0:T(8,128)S(1)}, u32[]{:S(2)}, u32[]{:S(2)}) collective-permute-start(f32[256,256]{1,0:T(8,128)S(1)} %fusion.16), channel_id=1, source_target_pairs={{16,0},{17,1},{18,2},{19,3},{20,4},{21,5},{22,6},{23,7},{24,8},{25... | collective-permute-start | bytes 786440 | tf_op jit(solution)/shard_map/ppermute | solution.py:86
  50.6 2.2 %copy-start = (f32[2,256,256]{2,1,0:T(8,128)}, f32[2,256,256]{2,1,0:T(8,128)S(1)}, u32[]{:S(2)}) copy-start(f32[2,256,256]{2,1,0:T(8,128)S(1)} %pad_maximum_fusion) | copy-start | bytes 1572868

commit v3 on v2

--- a/solution.py
+++ b/solution.py
@@ -2,10 +2,14 @@
 import jax.numpy as jnp
 from jax import lax
 from jax.sharding import PartitionSpec as P
+from jax.experimental import pallas as pl
+from jax.experimental.pallas import tpu as pltpu
 
 NS_STEPS = 4
 HI = lax.Precision.HIGH
 CHIP_RADIX = 4
+SPLIT = True
+PALLAS_SMOOTH = True
 
 
 def radix_plan(count):
@@ -78,20 +82,48 @@
     return inverse_root / jnp.sqrt(row_bound)[:, None, None]
 
 
+def split_shift(value, axis, pairs):
+    count = lax.axis_size("state")
+    if not SPLIT or count % 2:
+        return lax.ppermute(value, axis, pairs)
+    upper = lax.axis_index("state") % 2 == 1
+    half = value.shape[0] // 2
+    part = jnp.where(upper, value[half:], value[:half])
+    got = lax.ppermute(part, axis, pairs)
+    other = lax.ppermute(got, "state", digit_pairs(count, 2, 1, 1))
+    return jnp.where(upper, jnp.concatenate([other, got]), jnp.concatenate([got, other]))
+
+
 def later_product(local, axis):
     count, me = lax.axis_size(axis), lax.axis_index(axis)
     identity = jnp.eye(local.shape[-1], dtype=local.dtype)
     if count == 1:
         return identity
-    shifted = lax.ppermute(local, axis, [(j, j - 1) for j in range(1, count)])
+    shifted = split_shift(local, axis, [(j, j - 1) for j in range(1, count)])
     carried = jnp.where(me + 1 < count, shifted, identity)
     reach = 1
     while reach < count - 1:
-        further = lax.ppermute(carried, axis, [(j, j - reach) for j in range(reach, count)])
+        further = split_shift(carried, axis, [(j, j - reach) for j in range(reach, count)])
         further = jnp.where(me + reach < count, further, identity)
         carried = jnp.matmul(carried, further, precision=HI)
         reach *= 2
     return carried
+
+
+def smooth_kernel(anomaly_ref, suffix_ref, out_ref):
+    out_ref[0] = jnp.dot(anomaly_ref[0], suffix_ref[0].astype(jnp.bfloat16), preferred_element_type=jnp.float32).astype(out_ref.dtype)
+
+
+def smooth(anomalies, suffix):
+    times, rows, members = anomalies.shape
+    return pl.pallas_call(
+        smooth_kernel,
+        out_shape=jax.ShapeDtypeStruct(anomalies.shape, anomalies.dtype),
+        grid=(times,),
+        in_specs=[pl.BlockSpec((1, rows, members), lambda t: (t, 0, 0)), pl.BlockSpec((1, members, members), lambda t: (t, 0, 0))],
+        out_specs=pl.BlockSpec((1, rows, members), lambda t: (t, 0, 0)),
+        cost_estimate=pl.CostEstimate(flops=2 * times * rows * members * members, transcendentals=0, bytes_accessed=2 * anomalies.size * 2 + suffix.size * 4),
+    )(anomalies, suffix)
 
 
 def on_device(anomalies, obs_weight):
@@ -111,7 +143,10 @@
         product = jnp.matmul(transform[time_index], product, precision=HI)
         suffixes.append(product)
     suffix = jnp.stack(suffixes[::-1])
-    smoothed = jnp.einsum("trm,tmn->trn", anomalies, suffix.astype(jnp.bfloat16), preferred_element_type=jnp.float32).astype(jnp.bfloat16)
+    if PALLAS_SMOOTH:
+        smoothed = smooth(anomalies, suffix)
+    else:
+        smoothed = jnp.einsum("trm,tmn->trn", anomalies, suffix.astype(jnp.bfloat16), preferred_element_type=jnp.float32).astype(jnp.bfloat16)
     return (smoothed, suffix)
 
 

time: 54.6 us -> 53 us (0.971)
  Pallas kernels: 0 us -> 2.83 us
  matrix products: 11 us -> 8.76 us
  local copies, waits for them, and re-layouts: 2.33 us -> 0.76 us
  waiting for transfers between devices: 23.5 us -> 22 us
  other arithmetic: 0.69 us -> 1.5 us
    pallas_call x0 -> x1, Pallas kernels: none -> 2.83 us  [smooth(): pl.pallas_call(smooth_kernel, out_shape=jax.ShapeDtypeStruct(anomalies.sh...]
    dot_general x1 -> x0, matrix products: 2.22 us -> none  [on_device(): jnp.einsum('trm,tmn->trn', anomalies, suffix.astype(jnp.bfloat16), prefer...]
    unnamed x3 -> x0, local copies, waits for them, and re-layouts: 1.57 us -> none
    ppermute x1 -> x2, waiting for transfers between devices: 8.93 us -> 7.47 us  [the longest x1 6.13 us: split_shift(): got = lax.ppermute(part, axis, pairs)]
    another operation x1, other arithmetic: 0.04 us -> 0.83 us  [on_device(): suffix = jnp.stack(suffixes[::-1])]
    ppermute x1 -> x2, starting transfers between devices: 1.29 us -> 1.29 us  [the longest x1 1.29 us: split_shift(): got = lax.ppermute(part, axis, pairs)]
  transfers between devices with their start and end apart: 11 -> 12, of which waited for: 11 -> 12; matrix products, arithmetic and copies ran while one was open for 0% -> 0% of each run, Pallas kernels for 0% -> 0%
where the time goes in v3:
time: 53 us; the launch traced here: 52.8 us
  waiting for transfers between devices  22 us (42%)
  starting transfers between devices  16.1 us (30%)
  matrix products  8.76 us (17%)
  Pallas kernels  2.83 us (5%)
  other arithmetic  1.5 us (3%)
  between operations  0.88 us (2%)
  local copies, waits for them, and re-layouts  0.76 us (1%)
    ppermute x1, waiting for transfers between devices, split_shift(): got = lax.ppermute(part, axis, pairs)  6.13 us
    ppermute x3, starting transfers between devices, grouped_sum(): lax.ppermute(send, axis, digit_pairs(count, radix, place, offset))  5.92 us
    ppermute x3, waiting for transfers between devices, grouped_sum(): lax.ppermute(value, axis, digit_pairs(count, radix, place, offset))  4.34 us
    ppermute x2, waiting for transfers between devices, grouped_sum(): other = lax.ppermute(value, axis, digit_pairs(count, radix, place, 1))  3.62 us
    dot_general x1, matrix products, on_device(): jnp.einsum('trm,trn->tmn', weighted, weighted, preferred_element_type=jnp...  3.57 us
    ppermute x2, waiting for transfers between devices, grouped_sum(): value = keep + lax.ppermute(send, axis, digit_pairs(count, radix, place, 1))  3.38 us
    ppermute x3, waiting for transfers between devices, grouped_sum(): lax.ppermute(send, axis, digit_pairs(count, radix, place, offset))  3.22 us
    ppermute x2, starting transfers between devices, grouped_sum(): value = keep + lax.ppermute(send, axis, digit_pairs(count, radix, place, 1))  3.17 us
  transfers between devices with their start and end apart: 12, of which 12 were waited for; matrix products, arithmetic and copies ran while one was open for 0% of the time, Pallas kernels for 0%

profile of v3, /device:TPU:0, one launch (start us, length us, event | category | flops | bytes accessed | tf_op | source)
XLA Modules:
  0.0 52.8 jit_solution(12471756990428838079)
XLA Ops:
  0.6 3.6 %fusion = f32[2,256,256]{2,1,0:T(8,128)S(1)} fusion(bf16[2,1536,256]{2,1,0:T(8,128)(2,1)} %anomaly_ref.1, f32[2,1536]{1,0:T(2,128)} %param.3), kind=kOutput, calls=%fused_computation.2 | convolution fusion | flops 405012480 | bytes 2109440 | tf_op jit(solution)/shard_map/trm,trn->tmn/dot_general | solution.py:133
  4.3 0.5 collective-permute-start
  4.8 1.2 %collective-permute-done = f32[256,256]{1,0:T(8,128)S(1)} collective-permute-done((f32[256,256]{1,0:T(8,128)S(1)}, f32[256,256]{1,0:T(8,128)S(1)}, u32[]{:S(2)}, u32[]{:S(2)}) %collective-permute-start) | collective-permute-done | bytes 262176 | tf_op jit(solution)/shard_map/ppermute | solution.py:46
  6.0 2.9 %collective-permute-start.1 = (f32[64,256]{1,0:T(8,128)S(1)}, f32[64,256]{1,0:T(8,128)S(1)}, u32[]{:S(2)}, u32[]{:S(2)}) collective-permute-start(f32[64,256]{1,0:T(8,128)S(1)} %get-tuple-element.2), channel_id=1, source_target_pairs={{0,2},{1,3},{2,4},{3,5},{4,6},{5,7},{6,0},{7,1},{8,10},{9,11},{10,... | collective-permute-start | bytes 196616 | tf_op jit(solution)/shard_map/ppermute | solution.py:53
  9.0 1.1 %collective-permute-start.3 = (f32[64,256]{1,0:T(8,128)S(1)}, f32[64,256]{1,0:T(8,128)S(1)}, u32[]{:S(2)}, u32[]{:S(2)}) collective-permute-start(f32[64,256]{1,0:T(8,128)S(1)} %get-tuple-element.3), channel_id=1, source_target_pairs={{0,6},{1,7},{2,0},{3,1},{4,2},{5,3},{6,4},{7,5},{8,14},{9,15},{10,... | collective-permute-start | bytes 196616 | tf_op jit(solution)/shard_map/ppermute | solution.py:53
  10.0 1.9 %collective-permute-start.2 = (f32[64,256]{1,0:T(8,128)S(1)}, f32[64,256]{1,0:T(8,128)S(1)}, u32[]{:S(2)}, u32[]{:S(2)}) collective-permute-start(f32[64,256]{1,0:T(8,128)S(1)} %get-tuple-element.4), channel_id=1, source_target_pairs={{0,4},{1,5},{2,6},{3,7},{4,0},{5,1},{6,2},{7,3},{8,12},{9,13},{10,... | collective-permute-start | bytes 196616 | tf_op jit(solution)/shard_map/ppermute | solution.py:53
  12.0 0.5 collective-permute-done.1
  12.5 1.3 %collective-permute-done.3 = f32[64,256]{1,0:T(8,128)S(1)} collective-permute-done((f32[64,256]{1,0:T(8,128)S(1)}, f32[64,256]{1,0:T(8,128)S(1)}, u32[]{:S(2)}, u32[]{:S(2)}) %collective-permute-start.3) | collective-permute-done | bytes 65568 | tf_op jit(solution)/shard_map/ppermute | solution.py:53
  13.8 1.4 %collective-permute-done.2 = f32[64,256]{1,0:T(8,128)S(1)} collective-permute-done((f32[64,256]{1,0:T(8,128)S(1)}, f32[64,256]{1,0:T(8,128)S(1)}, u32[]{:S(2)}, u32[]{:S(2)}) %collective-permute-start.2) | collective-permute-done | bytes 65568 | tf_op jit(solution)/shard_map/ppermute | solution.py:53
  15.2 2.7 %collective-permute-start.4 = (f32[32,256]{1,0:T(8,128)S(1)}, f32[32,256]{1,0:T(8,128)S(1)}, u32[]{:S(2)}, u32[]{:S(2)}) collective-permute-start(f32[32,256]{1,0:T(8,128)S(1)} %slice_select_fusion.1), channel_id=1, source_target_pairs={{0,8},{1,9},{2,10},{3,11},{4,12},{5,13},{6,14},{7,15},{8,0},{9,1},... | collective-permute-start | bytes 98312 | tf_op jit(solution)/shard_map/ppermute | solution.py:46
  17.9 2.2 %collective-permute-done.4 = f32[32,256]{1,0:T(8,128)S(1)} collective-permute-done((f32[32,256]{1,0:T(8,128)S(1)}, f32[32,256]{1,0:T(8,128)S(1)}, u32[]{:S(2)}, u32[]{:S(2)}) %collective-permute-start.4) | collective-permute-done | bytes 32800 | tf_op jit(solution)/shard_map/ppermute | solution.py:46
  20.1 2.6 %collective-permute-start.5 = (f32[32,256]{1,0:T(8,128)S(1)}, f32[32,256]{1,0:T(8,128)S(1)}, u32[]{:S(2)}, u32[]{:S(2)}) collective-permute-start(f32[32,256]{1,0:T(8,128)S(1)} %select_add_fusion), channel_id=1, source_target_pairs={{0,8},{1,9},{2,10},{3,11},{4,12},{5,13},{6,14},{7,15},{8,0},{9,1},... | collective-permute-start | bytes 98312 | tf_op jit(solution)/shard_map/ppermute | solution.py:58
  22.7 0.1 broadcast_in_dim.30
  22.8 0.1 broadcast_in_dim.31
  22.9 2.1 %collective-permute-done.5 = f32[32,256]{1,0:T(8,128)S(1)} collective-permute-done((f32[32,256]{1,0:T(8,128)S(1)}, f32[32,256]{1,0:T(8,128)S(1)}, u32[]{:S(2)}, u32[]{:S(2)}) %collective-permute-start.5) | collective-permute-done | bytes 32800 | tf_op jit(solution)/shard_map/ppermute | solution.py:58
  25.0 1.1 %collective-permute-start.8 = (f32[64,256]{1,0:T(8,128)S(1)}, f32[64,256]{1,0:T(8,128)S(1)}, u32[]{:S(2)}, u32[]{:S(2)}) collective-permute-start(f32[64,256]{1,0:T(8,128)S(1)} %maximum_select_fusion.3), channel_id=1, source_target_pairs={{0,6},{1,7},{2,0},{3,1},{4,2},{5,3},{6,4},{7,5},{8,14},{9,15},{10,... | collective-permute-start | bytes 196616 | tf_op jit(solution)/shard_map/ppermute | solution.py:61
  26.1 1.1 %collective-permute-start.7 = (f32[64,256]{1,0:T(8,128)S(1)}, f32[64,256]{1,0:T(8,128)S(1)}, u32[]{:S(2)}, u32[]{:S(2)}) collective-permute-start(f32[64,256]{1,0:T(8,128)S(1)} %maximum_select_fusion.3), channel_id=1, source_target_pairs={{0,4},{1,5},{2,6},{3,7},{4,0},{5,1},{6,2},{7,3},{8,12},{9,13},{10,... | collective-permute-start | bytes 196616 | tf_op jit(solution)/shard_map/ppermute | solution.py:61
  27.2 0.8 %collective-permute-start.6 = (f32[64,256]{1,0:T(8,128)S(1)}, f32[64,256]{1,0:T(8,128)S(1)}, u32[]{:S(2)}, u32[]{:S(2)}) collective-permute-start(f32[64,256]{1,0:T(8,128)S(1)} %maximum_select_fusion.3), channel_id=1, source_target_pairs={{0,2},{1,3},{2,4},{3,5},{4,6},{5,7},{6,0},{7,1},{8,10},{9,11},{10,... | collective-permute-start | bytes 196616 | tf_op jit(solution)/shard_map/ppermute | solution.py:61
  28.1 1.3 %collective-permute-done.8 = f32[64,256]{1,0:T(8,128)S(1)} collective-permute-done((f32[64,256]{1,0:T(8,128)S(1)}, f32[64,256]{1,0:T(8,128)S(1)}, u32[]{:S(2)}, u32[]{:S(2)}) %collective-permute-start.8) | collective-permute-done | bytes 65568 | tf_op jit(solution)/shard_map/ppermute | solution.py:61
  29.3 1.0 %collective-permute-done.7 = f32[64,256]{1,0:T(8,128)S(1)} collective-permute-done((f32[64,256]{1,0:T(8,128)S(1)}, f32[64,256]{1,0:T(8,128)S(1)}, u32[]{:S(2)}, u32[]{:S(2)}) %collective-permute-start.7) | collective-permute-done | bytes 65568 | tf_op jit(solution)/shard_map/ppermute | solution.py:61
  30.4 2.0 %collective-permute-done.6 = f32[64,256]{1,0:T(8,128)S(1)} collective-permute-done((f32[64,256]{1,0:T(8,128)S(1)}, f32[64,256]{1,0:T(8,128)S(1)}, u32[]{:S(2)}, u32[]{:S(2)}) %collective-permute-start.6) | collective-permute-done | bytes 65568 | tf_op jit(solution)/shard_map/ppermute | solution.py:61
  32.4 0.6 %gather_fusion = f32[4,64,256]{2,1,0:T(8,128)S(1)} fusion(f32[4,64,256]{2,1,0:T(8,128)S(1)} %pad_maximum_fusion.1, s32[1024]{0:T(1024)S(1)} %pad_clamp_fusion), kind=kCustom, calls=%fused_computation | custom fusion | bytes 524304 | tf_op jit(solution)/shard_map/jit(_take)/gather | solution.py:64
  33.0 0.1 bitcast_select_fusion
  33.1 0.1 collective-permute-start.9
  33.2 1.5 %collective-permute-done.9 = f32[256,256]{1,0:T(8,128)S(1)} collective-permute-done((f32[256,256]{1,0:T(8,128)S(1)}, f32[256,256]{1,0:T(8,128)S(1)}, u32[]{:S(2)}, u32[]{:S(2)}) %collective-permute-start.9) | collective-permute-done | bytes 262176 | tf_op jit(solution)/shard_map/ppermute | solution.py:58
  34.7 0.1 fusion.6
  34.8 0.2 abs_reduce_fusion
  34.9 0.1 reduce_max.9
  35.1 0.5 fusion.5
  35.5 0.4 fusion.26
  36.0 0.4 fusion.15
  36.3 0.4 fusion.4
  36.7 0.4 fusion.32
  37.1 0.4 fusion.31
  37.5 0.4 fusion.3
  37.9 0.4 fusion.33
  38.3 0.4 fusion.34
  38.7 0.4 fusion.2
  39.1 0.4 convolution_divide_fusion
  39.5 0.3 fusion.20
  39.8 1.3 %collective-permute-start.10 = (f32[128,256]{1,0:T(8,128)S(1)}, f32[128,256]{1,0:T(8,128)S(1)}, u32[]{:S(2)}, u32[]{:S(2)}) collective-permute-start(f32[128,256]{1,0:T(8,128)S(1)} %slice_select_fusion), channel_id=1, source_target_pairs={{16,0},{17,1},{18,2},{19,3},{20,4},{21,5},{22,6},{23,7},{24,8},{25... | collective-permute-start | bytes 393224 | tf_op jit(solution)/shard_map/ppermute | solution.py:92
  41.1 6.1 %collective-permute-done.10 = f32[128,256]{1,0:T(8,128)S(1)} collective-permute-done((f32[128,256]{1,0:T(8,128)S(1)}, f32[128,256]{1,0:T(8,128)S(1)}, u32[]{:S(2)}, u32[]{:S(2)}) %collective-permute-start.10) | collective-permute-done | bytes 131104 | tf_op jit(solution)/shard_map/ppermute | solution.py:92
  47.2 0.0 collective-permute-start.11
  47.2 1.3 %collective-permute-done.11 = f32[128,256]{1,0:T(8,128)S(1)} collective-permute-done((f32[128,256]{1,0:T(8,128)S(1)}, f32[128,256]{1,0:T(8,128)S(1)}, u32[]{:S(2)}, u32[]{:S(2)}) %collective-permute-start.11) | collective-permute-done | bytes 131104 | tf_op jit(solution)/shard_map/ppermute | solution.py:93
  48.6 0.3 fusion.8
  48.9 0.3 convolution_bitcast_fusion
  49.2 0.8 %pad_maximum_fusion.suffix_ref = f32[2,256,256]{2,1,0:T(8,128)} fusion(f32[1,256,256]{2,1,0:T(8,128)S(1)} %bitcast.60, f32[1,256,256]{2,1,0:T(8,128)S(1)} %convolution_bitcast_fusion), kind=kLoop, calls=%fused_computation.16 | loop fusion | flops 131072 | bytes 1048576 | tf_op jit(solution)/shard_map/stack | solution.py:145
  50.0 2.8 %shard_map.41 = bf16[2,1536,256]{2,1,0:T(8,128)(2,1)} custom-call(bf16[2,1536,256]{2,1,0:T(8,128)(2,1)} %anomaly_ref.1, f32[2,256,256]{2,1,0:T(8,128)} %pad_maximum_fusion.suffix_ref), custom_call_target="tpu_custom_call" | custom-call | flops 402653184 | bytes 3670016 | tf_op jit(solution)/shard_map/pallas_call | solution.py:119
  (16 shorter events, 0.3 us)
Async XLA Ops:
  4.3 1.7 %collective-permute-start = (f32[256,256]{1,0:T(8,128)S(1)}, f32[256,256]{1,0:T(8,128)S(1)}, u32[]{:S(2)}, u32[]{:S(2)}) collective-permute-start(f32[256,256]{1,0:T(8,128)S(1)} %select_bitcast_fusion), channel_id=1, source_target_pairs={{0,1},{1,0},{2,3},{3,2},{4,5},{5,4},{6,7},{7,6},{8,9},{9,8},{10,11... | collective-permute-start | bytes 786440 | tf_op jit(solution)/shard_map/ppermute | solution.py:46
  6.0 6.5 %collective-permute-start.1 = (f32[64,256]{1,0:T(8,128)S(1)}, f32[64,256]{1,0:T(8,128)S(1)}, u32[]{:S(2)}, u32[]{:S(2)}) collective-permute-start(f32[64,256]{1,0:T(8,128)S(1)} %get-tuple-element.2), channel_id=1, source_target_pairs={{0,2},{1,3},{2,4},{3,5},{4,6},{5,7},{6,0},{7,1},{8,10},{9,11},{10,... | collective-permute-start | bytes 196616 | tf_op jit(solution)/shard_map/ppermute | solution.py:53
  9.0 4.8 %collective-permute-start.3 = (f32[64,256]{1,0:T(8,128)S(1)}, f32[64,256]{1,0:T(8,128)S(1)}, u32[]{:S(2)}, u32[]{:S(2)}) collective-permute-start(f32[64,256]{1,0:T(8,128)S(1)} %get-tuple-element.3), channel_id=1, source_target_pairs={{0,6},{1,7},{2,0},{3,1},{4,2},{5,3},{6,4},{7,5},{8,14},{9,15},{10,... | collective-permute-start | bytes 196616 | tf_op jit(solution)/shard_map/ppermute | solution.py:53
  10.0 5.1 %collective-permute-start.2 = (f32[64,256]{1,0:T(8,128)S(1)}, f32[64,256]{1,0:T(8,128)S(1)}, u32[]{:S(2)}, u32[]{:S(2)}) collective-permute-start(f32[64,256]{1,0:T(8,128)S(1)} %get-tuple-element.4), channel_id=1, source_target_pairs={{0,4},{1,5},{2,6},{3,7},{4,0},{5,1},{6,2},{7,3},{8,12},{9,13},{10,... | collective-permute-start | bytes 196616 | tf_op jit(solution)/shard_map/ppermute | solution.py:53
  15.2 4.9 %collective-permute-start.4 = (f32[32,256]{1,0:T(8,128)S(1)}, f32[32,256]{1,0:T(8,128)S(1)}, u32[]{:S(2)}, u32[]{:S(2)}) collective-permute-start(f32[32,256]{1,0:T(8,128)S(1)} %slice_select_fusion.1), channel_id=1, source_target_pairs={{0,8},{1,9},{2,10},{3,11},{4,12},{5,13},{6,14},{7,15},{8,0},{9,1},... | collective-permute-start | bytes 98312 | tf_op jit(solution)/shard_map/ppermute | solution.py:46
  20.1 4.9 %collective-permute-start.5 = (f32[32,256]{1,0:T(8,128)S(1)}, f32[32,256]{1,0:T(8,128)S(1)}, u32[]{:S(2)}, u32[]{:S(2)}) collective-permute-start(f32[32,256]{1,0:T(8,128)S(1)} %select_add_fusion), channel_id=1, source_target_pairs={{0,8},{1,9},{2,10},{3,11},{4,12},{5,13},{6,14},{7,15},{8,0},{9,1},... | collective-permute-start | bytes 98312 | tf_op jit(solution)/shard_map/ppermute | solution.py:58
  25.0 4.3 %collective-permute-start.8 = (f32[64,256]{1,0:T(8,128)S(1)}, f32[64,256]{1,0:T(8,128)S(1)}, u32[]{:S(2)}, u32[]{:S(2)}) collective-permute-start(f32[64,256]{1,0:T(8,128)S(1)} %maximum_select_fusion.3), channel_id=1, source_target_pairs={{0,6},{1,7},{2,0},{3,1},{4,2},{5,3},{6,4},{7,5},{8,14},{9,15},{10,... | collective-permute-start | bytes 196616 | tf_op jit(solution)/shard_map/ppermute | solution.py:61
  26.1 4.3 %collective-permute-start.7 = (f32[64,256]{1,0:T(8,128)S(1)}, f32[64,256]{1,0:T(8,128)S(1)}, u32[]{:S(2)}, u32[]{:S(2)}) collective-permute-start(f32[64,256]{1,0:T(8,128)S(1)} %maximum_select_fusion.3), channel_id=1, source_target_pairs={{0,4},{1,5},{2,6},{3,7},{4,0},{5,1},{6,2},{7,3},{8,12},{9,13},{10,... | collective-permute-start | bytes 196616 | tf_op jit(solution)/shard_map/ppermute | solution.py:61
  27.2 5.2 %collective-permute-start.6 = (f32[64,256]{1,0:T(8,128)S(1)}, f32[64,256]{1,0:T(8,128)S(1)}, u32[]{:S(2)}, u32[]{:S(2)}) collective-permute-start(f32[64,256]{1,0:T(8,128)S(1)} %maximum_select_fusion.3), channel_id=1, source_target_pairs={{0,2},{1,3},{2,4},{3,5},{4,6},{5,7},{6,0},{7,1},{8,10},{9,11},{10,... | collective-permute-start | bytes 196616 | tf_op jit(solution)/shard_map/ppermute | solution.py:61
  33.1 1.6 %collective-permute-start.9 = (f32[256,256]{1,0:T(8,128)S(1)}, f32[256,256]{1,0:T(8,128)S(1)}, u32[]{:S(2)}, u32[]{:S(2)}) collective-permute-start(f32[256,256]{1,0:T(8,128)S(1)} %bitcast_select_fusion), channel_id=1, source_target_pairs={{0,1},{1,0},{2,3},{3,2},{4,5},{5,4},{6,7},{7,6},{8,9},{9,8},{10,11... | collective-permute-start | bytes 786440 | tf_op jit(solution)/shard_map/ppermute | solution.py:58
  39.8 7.4 %collective-permute-start.10 = (f32[128,256]{1,0:T(8,128)S(1)}, f32[128,256]{1,0:T(8,128)S(1)}, u32[]{:S(2)}, u32[]{:S(2)}) collective-permute-start(f32[128,256]{1,0:T(8,128)S(1)} %slice_select_fusion), channel_id=1, source_target_pairs={{16,0},{17,1},{18,2},{19,3},{20,4},{21,5},{22,6},{23,7},{24,8},{25... | collective-permute-start | bytes 393224 | tf_op jit(solution)/shard_map/ppermute | solution.py:92
  47.2 1.3 %collective-permute-start.11 = (f32[128,256]{1,0:T(8,128)S(1)}, f32[128,256]{1,0:T(8,128)S(1)}, u32[]{:S(2)}, u32[]{:S(2)}) collective-permute-start(f32[128,256]{1,0:T(8,128)S(1)} %collective-permute-done.10), channel_id=1, source_target_pairs={{0,1},{1,0},{2,3},{3,2},{4,5},{5,4},{6,7},{7,6},{8,9},{9,8},{10,11... | collective-permute-start | bytes 393224 | tf_op jit(solution)/shard_map/ppermute | solution.py:93

commit v4 on v3

--- a/solution.py
+++ b/solution.py
@@ -6,7 +6,8 @@
 from jax.experimental.pallas import tpu as pltpu
 
 NS_STEPS = 4
-HI = lax.Precision.HIGH
+HI = lax.Precision.HIGHEST
+NS_PRECISION = lax.Precision.HIGH
 CHIP_RADIX = 4
 SPLIT = True
 PALLAS_SMOOTH = True
@@ -76,9 +77,9 @@
     iterate = covariance / row_bound[:, None, None]
     inverse_root = jnp.broadcast_to(identity, covariance.shape)
     for sweep_index in range(NS_STEPS):
-        factor = 1.5 * identity - 0.5 * jnp.matmul(inverse_root, iterate, precision=HI)
-        iterate = jnp.matmul(iterate, factor, precision=HI)
-        inverse_root = jnp.matmul(factor, inverse_root, precision=HI)
+        factor = 1.5 * identity - 0.5 * jnp.matmul(inverse_root, iterate, precision=NS_PRECISION)
+        iterate = jnp.matmul(iterate, factor, precision=NS_PRECISION)
+        inverse_root = jnp.matmul(factor, inverse_root, precision=NS_PRECISION)
     return inverse_root / jnp.sqrt(row_bound)[:, None, None]
 
 

time: 53 us -> 53.3 us (level)
  no operation moved by 1% of the time
where the time goes in v4:
time: 53.3 us; the launch traced here: 53.1 us
  waiting for transfers between devices  22 us (41%)
  starting transfers between devices  16.1 us (30%)
  matrix products  9.09 us (17%)
  Pallas kernels  2.83 us (5%)
  other arithmetic  1.5 us (3%)
  between operations  0.88 us (2%)
  local copies, waits for them, and re-layouts  0.76 us (1%)
    ppermute x1, waiting for transfers between devices, split_shift(): got = lax.ppermute(part, axis, pairs)  6.13 us
    ppermute x3, starting transfers between devices, grouped_sum(): lax.ppermute(send, axis, digit_pairs(count, radix, place, offset))  5.92 us
    ppermute x3, waiting for transfers between devices, grouped_sum(): lax.ppermute(value, axis, digit_pairs(count, radix, place, offset))  4.34 us
    ppermute x2, waiting for transfers between devices, grouped_sum(): other = lax.ppermute(value, axis, digit_pairs(count, radix, place, 1))  3.62 us
    dot_general x1, matrix products, on_device(): jnp.einsum('trm,trn->tmn', weighted, weighted, preferred_element_type=jnp...  3.57 us
    ppermute x2, waiting for transfers between devices, grouped_sum(): value = keep + lax.ppermute(send, axis, digit_pairs(count, radix, place, 1))  3.38 us
    ppermute x3, waiting for transfers between devices, grouped_sum(): lax.ppermute(send, axis, digit_pairs(count, radix, place, offset))  3.22 us
    ppermute x2, starting transfers between devices, grouped_sum(): value = keep + lax.ppermute(send, axis, digit_pairs(count, radix, place, 1))  3.17 us
  transfers between devices with their start and end apart: 12, of which 12 were waited for; matrix products, arithmetic and copies ran while one was open for 0% of the time, Pallas kernels for 0%

profile of v4, /device:TPU:0, one launch (start us, length us, event | category | flops | bytes accessed | tf_op | source)
XLA Modules:
  0.0 53.1 jit_solution(14811600646721285289)
XLA Ops:
  0.6 3.6 %fusion = f32[2,256,256]{2,1,0:T(8,128)S(1)} fusion(bf16[2,1536,256]{2,1,0:T(8,128)(2,1)} %anomaly_ref.1, f32[2,1536]{1,0:T(2,128)} %param.3), kind=kOutput, calls=%fused_computation.2 | convolution fusion | flops 405012480 | bytes 2109440 | tf_op jit(solution)/shard_map/trm,trn->tmn/dot_general | solution.py:134
  4.3 0.5 collective-permute-start
  4.8 1.2 %collective-permute-done = f32[256,256]{1,0:T(8,128)S(1)} collective-permute-done((f32[256,256]{1,0:T(8,128)S(1)}, f32[256,256]{1,0:T(8,128)S(1)}, u32[]{:S(2)}, u32[]{:S(2)}) %collective-permute-start) | collective-permute-done | bytes 262176 | tf_op jit(solution)/shard_map/ppermute | solution.py:47
  6.0 2.9 %collective-permute-start.1 = (f32[64,256]{1,0:T(8,128)S(1)}, f32[64,256]{1,0:T(8,128)S(1)}, u32[]{:S(2)}, u32[]{:S(2)}) collective-permute-start(f32[64,256]{1,0:T(8,128)S(1)} %get-tuple-element.2), channel_id=1, source_target_pairs={{0,2},{1,3},{2,4},{3,5},{4,6},{5,7},{6,0},{7,1},{8,10},{9,11},{10,... | collective-permute-start | bytes 196616 | tf_op jit(solution)/shard_map/ppermute | solution.py:54
  9.0 1.1 %collective-permute-start.3 = (f32[64,256]{1,0:T(8,128)S(1)}, f32[64,256]{1,0:T(8,128)S(1)}, u32[]{:S(2)}, u32[]{:S(2)}) collective-permute-start(f32[64,256]{1,0:T(8,128)S(1)} %get-tuple-element.3), channel_id=1, source_target_pairs={{0,6},{1,7},{2,0},{3,1},{4,2},{5,3},{6,4},{7,5},{8,14},{9,15},{10,... | collective-permute-start | bytes 196616 | tf_op jit(solution)/shard_map/ppermute | solution.py:54
  10.0 1.9 %collective-permute-start.2 = (f32[64,256]{1,0:T(8,128)S(1)}, f32[64,256]{1,0:T(8,128)S(1)}, u32[]{:S(2)}, u32[]{:S(2)}) collective-permute-start(f32[64,256]{1,0:T(8,128)S(1)} %get-tuple-element.4), channel_id=1, source_target_pairs={{0,4},{1,5},{2,6},{3,7},{4,0},{5,1},{6,2},{7,3},{8,12},{9,13},{10,... | collective-permute-start | bytes 196616 | tf_op jit(solution)/shard_map/ppermute | solution.py:54
  12.0 0.5 collective-permute-done.1
  12.5 1.3 %collective-permute-done.3 = f32[64,256]{1,0:T(8,128)S(1)} collective-permute-done((f32[64,256]{1,0:T(8,128)S(1)}, f32[64,256]{1,0:T(8,128)S(1)}, u32[]{:S(2)}, u32[]{:S(2)}) %collective-permute-start.3) | collective-permute-done | bytes 65568 | tf_op jit(solution)/shard_map/ppermute | solution.py:54
  13.8 1.4 %collective-permute-done.2 = f32[64,256]{1,0:T(8,128)S(1)} collective-permute-done((f32[64,256]{1,0:T(8,128)S(1)}, f32[64,256]{1,0:T(8,128)S(1)}, u32[]{:S(2)}, u32[]{:S(2)}) %collective-permute-start.2) | collective-permute-done | bytes 65568 | tf_op jit(solution)/shard_map/ppermute | solution.py:54
  15.2 2.7 %collective-permute-start.4 = (f32[32,256]{1,0:T(8,128)S(1)}, f32[32,256]{1,0:T(8,128)S(1)}, u32[]{:S(2)}, u32[]{:S(2)}) collective-permute-start(f32[32,256]{1,0:T(8,128)S(1)} %slice_select_fusion.1), channel_id=1, source_target_pairs={{0,8},{1,9},{2,10},{3,11},{4,12},{5,13},{6,14},{7,15},{8,0},{9,1},... | collective-permute-start | bytes 98312 | tf_op jit(solution)/shard_map/ppermute | solution.py:47
  17.9 2.2 %collective-permute-done.4 = f32[32,256]{1,0:T(8,128)S(1)} collective-permute-done((f32[32,256]{1,0:T(8,128)S(1)}, f32[32,256]{1,0:T(8,128)S(1)}, u32[]{:S(2)}, u32[]{:S(2)}) %collective-permute-start.4) | collective-permute-done | bytes 32800 | tf_op jit(solution)/shard_map/ppermute | solution.py:47
  20.1 2.6 %collective-permute-start.5 = (f32[32,256]{1,0:T(8,128)S(1)}, f32[32,256]{1,0:T(8,128)S(1)}, u32[]{:S(2)}, u32[]{:S(2)}) collective-permute-start(f32[32,256]{1,0:T(8,128)S(1)} %select_add_fusion), channel_id=1, source_target_pairs={{0,8},{1,9},{2,10},{3,11},{4,12},{5,13},{6,14},{7,15},{8,0},{9,1},... | collective-permute-start | bytes 98312 | tf_op jit(solution)/shard_map/ppermute | solution.py:59
  22.7 0.1 broadcast_in_dim.30
  22.8 0.1 broadcast_in_dim.31
  22.9 2.1 %collective-permute-done.5 = f32[32,256]{1,0:T(8,128)S(1)} collective-permute-done((f32[32,256]{1,0:T(8,128)S(1)}, f32[32,256]{1,0:T(8,128)S(1)}, u32[]{:S(2)}, u32[]{:S(2)}) %collective-permute-start.5) | collective-permute-done | bytes 32800 | tf_op jit(solution)/shard_map/ppermute | solution.py:59
  25.0 1.1 %collective-permute-start.8 = (f32[64,256]{1,0:T(8,128)S(1)}, f32[64,256]{1,0:T(8,128)S(1)}, u32[]{:S(2)}, u32[]{:S(2)}) collective-permute-start(f32[64,256]{1,0:T(8,128)S(1)} %maximum_select_fusion.3), channel_id=1, source_target_pairs={{0,6},{1,7},{2,0},{3,1},{4,2},{5,3},{6,4},{7,5},{8,14},{9,15},{10,... | collective-permute-start | bytes 196616 | tf_op jit(solution)/shard_map/ppermute | solution.py:62
  26.1 1.1 %collective-permute-start.7 = (f32[64,256]{1,0:T(8,128)S(1)}, f32[64,256]{1,0:T(8,128)S(1)}, u32[]{:S(2)}, u32[]{:S(2)}) collective-permute-start(f32[64,256]{1,0:T(8,128)S(1)} %maximum_select_fusion.3), channel_id=1, source_target_pairs={{0,4},{1,5},{2,6},{3,7},{4,0},{5,1},{6,2},{7,3},{8,12},{9,13},{10,... | collective-permute-start | bytes 196616 | tf_op jit(solution)/shard_map/ppermute | solution.py:62
  27.2 0.8 %collective-permute-start.6 = (f32[64,256]{1,0:T(8,128)S(1)}, f32[64,256]{1,0:T(8,128)S(1)}, u32[]{:S(2)}, u32[]{:S(2)}) collective-permute-start(f32[64,256]{1,0:T(8,128)S(1)} %maximum_select_fusion.3), channel_id=1, source_target_pairs={{0,2},{1,3},{2,4},{3,5},{4,6},{5,7},{6,0},{7,1},{8,10},{9,11},{10,... | collective-permute-start | bytes 196616 | tf_op jit(solution)/shard_map/ppermute | solution.py:62
  28.1 1.3 %collective-permute-done.8 = f32[64,256]{1,0:T(8,128)S(1)} collective-permute-done((f32[64,256]{1,0:T(8,128)S(1)}, f32[64,256]{1,0:T(8,128)S(1)}, u32[]{:S(2)}, u32[]{:S(2)}) %collective-permute-start.8) | collective-permute-done | bytes 65568 | tf_op jit(solution)/shard_map/ppermute | solution.py:62
  29.3 1.0 %collective-permute-done.7 = f32[64,256]{1,0:T(8,128)S(1)} collective-permute-done((f32[64,256]{1,0:T(8,128)S(1)}, f32[64,256]{1,0:T(8,128)S(1)}, u32[]{:S(2)}, u32[]{:S(2)}) %collective-permute-start.7) | collective-permute-done | bytes 65568 | tf_op jit(solution)/shard_map/ppermute | solution.py:62
  30.4 2.0 %collective-permute-done.6 = f32[64,256]{1,0:T(8,128)S(1)} collective-permute-done((f32[64,256]{1,0:T(8,128)S(1)}, f32[64,256]{1,0:T(8,128)S(1)}, u32[]{:S(2)}, u32[]{:S(2)}) %collective-permute-start.6) | collective-permute-done | bytes 65568 | tf_op jit(solution)/shard_map/ppermute | solution.py:62
  32.4 0.6 %gather_fusion = f32[4,64,256]{2,1,0:T(8,128)S(1)} fusion(f32[4,64,256]{2,1,0:T(8,128)S(1)} %pad_maximum_fusion.1, s32[1024]{0:T(1024)S(1)} %pad_clamp_fusion), kind=kCustom, calls=%fused_computation | custom fusion | bytes 524304 | tf_op jit(solution)/shard_map/jit(_take)/gather | solution.py:65
  33.0 0.1 bitcast_select_fusion
  33.1 0.1 collective-permute-start.9
  33.2 1.5 %collective-permute-done.9 = f32[256,256]{1,0:T(8,128)S(1)} collective-permute-done((f32[256,256]{1,0:T(8,128)S(1)}, f32[256,256]{1,0:T(8,128)S(1)}, u32[]{:S(2)}, u32[]{:S(2)}) %collective-permute-start.9) | collective-permute-done | bytes 262176 | tf_op jit(solution)/shard_map/ppermute | solution.py:59
  34.7 0.1 fusion.6
  34.8 0.2 abs_reduce_fusion
  34.9 0.1 reduce_max.9
  35.1 0.5 fusion.5
  35.5 0.4 fusion.26
  36.0 0.4 fusion.15
  36.3 0.4 fusion.4
  36.7 0.4 fusion.32
  37.1 0.4 fusion.31
  37.5 0.4 fusion.3
  37.9 0.4 fusion.33
  38.3 0.4 fusion.34
  38.7 0.4 fusion.2
  39.1 0.4 convolution_divide_fusion
  39.5 0.4 fusion.20
  39.9 1.3 %collective-permute-start.10 = (f32[128,256]{1,0:T(8,128)S(1)}, f32[128,256]{1,0:T(8,128)S(1)}, u32[]{:S(2)}, u32[]{:S(2)}) collective-permute-start(f32[128,256]{1,0:T(8,128)S(1)} %slice_select_fusion), channel_id=1, source_target_pairs={{16,0},{17,1},{18,2},{19,3},{20,4},{21,5},{22,6},{23,7},{24,8},{25... | collective-permute-start | bytes 393224 | tf_op jit(solution)/shard_map/ppermute | solution.py:93
  41.2 6.1 %collective-permute-done.10 = f32[128,256]{1,0:T(8,128)S(1)} collective-permute-done((f32[128,256]{1,0:T(8,128)S(1)}, f32[128,256]{1,0:T(8,128)S(1)}, u32[]{:S(2)}, u32[]{:S(2)}) %collective-permute-start.10) | collective-permute-done | bytes 131104 | tf_op jit(solution)/shard_map/ppermute | solution.py:93
  47.3 0.0 collective-permute-start.11
  47.3 1.3 %collective-permute-done.11 = f32[128,256]{1,0:T(8,128)S(1)} collective-permute-done((f32[128,256]{1,0:T(8,128)S(1)}, f32[128,256]{1,0:T(8,128)S(1)}, u32[]{:S(2)}, u32[]{:S(2)}) %collective-permute-start.11) | collective-permute-done | bytes 131104 | tf_op jit(solution)/shard_map/ppermute | solution.py:94
  48.7 0.4 fusion.8
  49.1 0.4 convolution_bitcast_fusion
  49.5 0.8 %pad_maximum_fusion.suffix_ref = f32[2,256,256]{2,1,0:T(8,128)} fusion(f32[1,256,256]{2,1,0:T(8,128)S(1)} %bitcast.60, f32[1,256,256]{2,1,0:T(8,128)S(1)} %convolution_bitcast_fusion), kind=kLoop, calls=%fused_computation.16 | loop fusion | flops 131072 | bytes 1048576 | tf_op jit(solution)/shard_map/stack | solution.py:146
  50.3 2.8 %shard_map.41 = bf16[2,1536,256]{2,1,0:T(8,128)(2,1)} custom-call(bf16[2,1536,256]{2,1,0:T(8,128)(2,1)} %anomaly_ref.1, f32[2,256,256]{2,1,0:T(8,128)} %pad_maximum_fusion.suffix_ref), custom_call_target="tpu_custom_call" | custom-call | flops 402653184 | bytes 3670016 | tf_op jit(solution)/shard_map/pallas_call | solution.py:120
  (16 shorter events, 0.3 us)
Async XLA Ops:
  4.3 1.7 %collective-permute-start = (f32[256,256]{1,0:T(8,128)S(1)}, f32[256,256]{1,0:T(8,128)S(1)}, u32[]{:S(2)}, u32[]{:S(2)}) collective-permute-start(f32[256,256]{1,0:T(8,128)S(1)} %select_bitcast_fusion), channel_id=1, source_target_pairs={{0,1},{1,0},{2,3},{3,2},{4,5},{5,4},{6,7},{7,6},{8,9},{9,8},{10,11... | collective-permute-start | bytes 786440 | tf_op jit(solution)/shard_map/ppermute | solution.py:47
  6.0 6.5 %collective-permute-start.1 = (f32[64,256]{1,0:T(8,128)S(1)}, f32[64,256]{1,0:T(8,128)S(1)}, u32[]{:S(2)}, u32[]{:S(2)}) collective-permute-start(f32[64,256]{1,0:T(8,128)S(1)} %get-tuple-element.2), channel_id=1, source_target_pairs={{0,2},{1,3},{2,4},{3,5},{4,6},{5,7},{6,0},{7,1},{8,10},{9,11},{10,... | collective-permute-start | bytes 196616 | tf_op jit(solution)/shard_map/ppermute | solution.py:54
  9.0 4.8 %collective-permute-start.3 = (f32[64,256]{1,0:T(8,128)S(1)}, f32[64,256]{1,0:T(8,128)S(1)}, u32[]{:S(2)}, u32[]{:S(2)}) collective-permute-start(f32[64,256]{1,0:T(8,128)S(1)} %get-tuple-element.3), channel_id=1, source_target_pairs={{0,6},{1,7},{2,0},{3,1},{4,2},{5,3},{6,4},{7,5},{8,14},{9,15},{10,... | collective-permute-start | bytes 196616 | tf_op jit(solution)/shard_map/ppermute | solution.py:54
  10.0 5.1 %collective-permute-start.2 = (f32[64,256]{1,0:T(8,128)S(1)}, f32[64,256]{1,0:T(8,128)S(1)}, u32[]{:S(2)}, u32[]{:S(2)}) collective-permute-start(f32[64,256]{1,0:T(8,128)S(1)} %get-tuple-element.4), channel_id=1, source_target_pairs={{0,4},{1,5},{2,6},{3,7},{4,0},{5,1},{6,2},{7,3},{8,12},{9,13},{10,... | collective-permute-start | bytes 196616 | tf_op jit(solution)/shard_map/ppermute | solution.py:54
  15.2 4.9 %collective-permute-start.4 = (f32[32,256]{1,0:T(8,128)S(1)}, f32[32,256]{1,0:T(8,128)S(1)}, u32[]{:S(2)}, u32[]{:S(2)}) collective-permute-start(f32[32,256]{1,0:T(8,128)S(1)} %slice_select_fusion.1), channel_id=1, source_target_pairs={{0,8},{1,9},{2,10},{3,11},{4,12},{5,13},{6,14},{7,15},{8,0},{9,1},... | collective-permute-start | bytes 98312 | tf_op jit(solution)/shard_map/ppermute | solution.py:47
  20.1 4.9 %collective-permute-start.5 = (f32[32,256]{1,0:T(8,128)S(1)}, f32[32,256]{1,0:T(8,128)S(1)}, u32[]{:S(2)}, u32[]{:S(2)}) collective-permute-start(f32[32,256]{1,0:T(8,128)S(1)} %select_add_fusion), channel_id=1, source_target_pairs={{0,8},{1,9},{2,10},{3,11},{4,12},{5,13},{6,14},{7,15},{8,0},{9,1},... | collective-permute-start | bytes 98312 | tf_op jit(solution)/shard_map/ppermute | solution.py:59
  25.0 4.3 %collective-permute-start.8 = (f32[64,256]{1,0:T(8,128)S(1)}, f32[64,256]{1,0:T(8,128)S(1)}, u32[]{:S(2)}, u32[]{:S(2)}) collective-permute-start(f32[64,256]{1,0:T(8,128)S(1)} %maximum_select_fusion.3), channel_id=1, source_target_pairs={{0,6},{1,7},{2,0},{3,1},{4,2},{5,3},{6,4},{7,5},{8,14},{9,15},{10,... | collective-permute-start | bytes 196616 | tf_op jit(solution)/shard_map/ppermute | solution.py:62
  26.1 4.3 %collective-permute-start.7 = (f32[64,256]{1,0:T(8,128)S(1)}, f32[64,256]{1,0:T(8,128)S(1)}, u32[]{:S(2)}, u32[]{:S(2)}) collective-permute-start(f32[64,256]{1,0:T(8,128)S(1)} %maximum_select_fusion.3), channel_id=1, source_target_pairs={{0,4},{1,5},{2,6},{3,7},{4,0},{5,1},{6,2},{7,3},{8,12},{9,13},{10,... | collective-permute-start | bytes 196616 | tf_op jit(solution)/shard_map/ppermute | solution.py:62
  27.2 5.2 %collective-permute-start.6 = (f32[64,256]{1,0:T(8,128)S(1)}, f32[64,256]{1,0:T(8,128)S(1)}, u32[]{:S(2)}, u32[]{:S(2)}) collective-permute-start(f32[64,256]{1,0:T(8,128)S(1)} %maximum_select_fusion.3), channel_id=1, source_target_pairs={{0,2},{1,3},{2,4},{3,5},{4,6},{5,7},{6,0},{7,1},{8,10},{9,11},{10,... | collective-permute-start | bytes 196616 | tf_op jit(solution)/shard_map/ppermute | solution.py:62
  33.1 1.6 %collective-permute-start.9 = (f32[256,256]{1,0:T(8,128)S(1)}, f32[256,256]{1,0:T(8,128)S(1)}, u32[]{:S(2)}, u32[]{:S(2)}) collective-permute-start(f32[256,256]{1,0:T(8,128)S(1)} %bitcast_select_fusion), channel_id=1, source_target_pairs={{0,1},{1,0},{2,3},{3,2},{4,5},{5,4},{6,7},{7,6},{8,9},{9,8},{10,11... | collective-permute-start | bytes 786440 | tf_op jit(solution)/shard_map/ppermute | solution.py:59
  39.9 7.4 %collective-permute-start.10 = (f32[128,256]{1,0:T(8,128)S(1)}, f32[128,256]{1,0:T(8,128)S(1)}, u32[]{:S(2)}, u32[]{:S(2)}) collective-permute-start(f32[128,256]{1,0:T(8,128)S(1)} %slice_select_fusion), channel_id=1, source_target_pairs={{16,0},{17,1},{18,2},{19,3},{20,4},{21,5},{22,6},{23,7},{24,8},{25... | collective-permute-start | bytes 393224 | tf_op jit(solution)/shard_map/ppermute | solution.py:93
  47.3 1.3 %collective-permute-start.11 = (f32[128,256]{1,0:T(8,128)S(1)}, f32[128,256]{1,0:T(8,128)S(1)}, u32[]{:S(2)}, u32[]{:S(2)}) collective-permute-start(f32[128,256]{1,0:T(8,128)S(1)} %collective-permute-done.10), channel_id=1, source_target_pairs={{0,1},{1,0},{2,3},{3,2},{4,5},{5,4},{6,7},{7,6},{8,9},{9,8},{10,11... | collective-permute-start | bytes 393224 | tf_op jit(solution)/shard_map/ppermute | solution.py:94

commit v5 on v3

--- a/solution.py
+++ b/solution.py
@@ -3,13 +3,14 @@
 from jax import lax
 from jax.sharding import PartitionSpec as P
 from jax.experimental import pallas as pl
+from jax.experimental.layout import Layout, with_layout_constraint
 from jax.experimental.pallas import tpu as pltpu
 
 NS_STEPS = 4
 HI = lax.Precision.HIGH
 CHIP_RADIX = 4
 SPLIT = True
-PALLAS_SMOOTH = True
+PALLAS_SMOOTH = False
 
 
 def radix_plan(count):
@@ -147,6 +148,7 @@
         smoothed = smooth(anomalies, suffix)
     else:
         smoothed = jnp.einsum("trm,tmn->trn", anomalies, suffix.astype(jnp.bfloat16), preferred_element_type=jnp.float32).astype(jnp.bfloat16)
+        smoothed = with_layout_constraint(smoothed, Layout(major_to_minor=(0, 1, 2)))
     return (smoothed, suffix)
 
 

time: 53 us -> 51.3 us (0.968)
  Pallas kernels: 2.83 us -> 0 us
  matrix products: 8.76 us -> 10.5 us
  other arithmetic: 1.5 us -> 0.7 us
    pallas_call x1 -> x0, Pallas kernels: 2.83 us -> none  [smooth(): pl.pallas_call(smooth_kernel, out_shape=jax.ShapeDtypeStruct(anomalies.sh...]
    dot_general x0 -> x1, matrix products: none -> 1.72 us  [on_device(): jnp.einsum('trm,tmn->trn', anomalies, suffix.astype(jnp.bfloat16), prefer...]
    another operation x1, other arithmetic: 0.83 us -> 0.04 us  [on_device(): suffix = jnp.stack(suffixes[::-1])]
where the time goes in v5:
time: 51.3 us; the launch traced here: 51.1 us
  waiting for transfers between devices  22 us (43%)
  starting transfers between devices  16.2 us (32%)
  matrix products  10.5 us (20%)
  between operations  0.91 us (2%)
  local copies, waits for them, and re-layouts  0.77 us (2%)
  other arithmetic  0.7 us (1%)
    ppermute x1, waiting for transfers between devices, split_shift(): got = lax.ppermute(part, axis, pairs)  6.13 us
    ppermute x3, starting transfers between devices, grouped_sum(): lax.ppermute(send, axis, digit_pairs(count, radix, place, offset))  5.92 us
    ppermute x3, waiting for transfers between devices, grouped_sum(): lax.ppermute(value, axis, digit_pairs(count, radix, place, offset))  4.34 us
    ppermute x2, waiting for transfers between devices, grouped_sum(): other = lax.ppermute(value, axis, digit_pairs(count, radix, place, 1))  3.62 us
    dot_general x1, matrix products, on_device(): jnp.einsum('trm,trn->tmn', weighted, weighted, preferred_element_type=jnp...  3.57 us
    ppermute x2, waiting for transfers between devices, grouped_sum(): value = keep + lax.ppermute(send, axis, digit_pairs(count, radix, place, 1))  3.38 us
    ppermute x3, waiting for transfers between devices, grouped_sum(): lax.ppermute(send, axis, digit_pairs(count, radix, place, offset))  3.22 us
    ppermute x2, starting transfers between devices, grouped_sum(): value = keep + lax.ppermute(send, axis, digit_pairs(count, radix, place, 1))  3.17 us
  transfers between devices with their start and end apart: 12, of which 12 were waited for; matrix products, arithmetic and copies ran while one was open for 0% of the time, Pallas kernels for 0%

profile of v5, /device:TPU:0, one launch (start us, length us, event | category | flops | bytes accessed | tf_op | source)
XLA Modules:
  0.0 51.1 jit_solution(16867137204533035814)
XLA Ops:
  0.6 3.6 %fusion.1 = f32[2,256,256]{2,1,0:T(8,128)S(1)} fusion(bf16[2,1536,256]{2,1,0:T(8,128)(2,1)} %param.2, f32[2,1536]{1,0:T(2,128)} %param.3), kind=kOutput, calls=%fused_computation.4 | convolution fusion | flops 405012480 | bytes 2109440 | tf_op jit(solution)/shard_map/trm,trn->tmn/dot_general | solution.py:134
  4.3 0.5 %collective-permute-start = (f32[256,256]{1,0:T(8,128)S(1)}, f32[256,256]{1,0:T(8,128)S(1)}, u32[]{:S(2)}, u32[]{:S(2)}) collective-permute-start(f32[256,256]{1,0:T(8,128)S(1)} %select_bitcast_fusion), channel_id=1, source_target_pairs={{0,1},{1,0},{2,3},{3,2},{4,5},{5,4},{6,7},{7,6},{8,9},{9,8},{10,11... | collective-permute-start | bytes 786440 | tf_op jit(solution)/shard_map/ppermute | solution.py:47
  4.8 1.2 %collective-permute-done = f32[256,256]{1,0:T(8,128)S(1)} collective-permute-done((f32[256,256]{1,0:T(8,128)S(1)}, f32[256,256]{1,0:T(8,128)S(1)}, u32[]{:S(2)}, u32[]{:S(2)}) %collective-permute-start) | collective-permute-done | bytes 262176 | tf_op jit(solution)/shard_map/ppermute | solution.py:47
  6.0 2.9 %collective-permute-start.1 = (f32[64,256]{1,0:T(8,128)S(1)}, f32[64,256]{1,0:T(8,128)S(1)}, u32[]{:S(2)}, u32[]{:S(2)}) collective-permute-start(f32[64,256]{1,0:T(8,128)S(1)} %get-tuple-element.2), channel_id=1, source_target_pairs={{0,2},{1,3},{2,4},{3,5},{4,6},{5,7},{6,0},{7,1},{8,10},{9,11},{10,... | collective-permute-start | bytes 196616 | tf_op jit(solution)/shard_map/ppermute | solution.py:54
  9.0 1.1 %collective-permute-start.3 = (f32[64,256]{1,0:T(8,128)S(1)}, f32[64,256]{1,0:T(8,128)S(1)}, u32[]{:S(2)}, u32[]{:S(2)}) collective-permute-start(f32[64,256]{1,0:T(8,128)S(1)} %get-tuple-element.3), channel_id=1, source_target_pairs={{0,6},{1,7},{2,0},{3,1},{4,2},{5,3},{6,4},{7,5},{8,14},{9,15},{10,... | collective-permute-start | bytes 196616 | tf_op jit(solution)/shard_map/ppermute | solution.py:54
  10.0 1.9 %collective-permute-start.2 = (f32[64,256]{1,0:T(8,128)S(1)}, f32[64,256]{1,0:T(8,128)S(1)}, u32[]{:S(2)}, u32[]{:S(2)}) collective-permute-start(f32[64,256]{1,0:T(8,128)S(1)} %get-tuple-element.4), channel_id=1, source_target_pairs={{0,4},{1,5},{2,6},{3,7},{4,0},{5,1},{6,2},{7,3},{8,12},{9,13},{10,... | collective-permute-start | bytes 196616 | tf_op jit(solution)/shard_map/ppermute | solution.py:54
  12.0 0.5 %collective-permute-done.1 = f32[64,256]{1,0:T(8,128)S(1)} collective-permute-done((f32[64,256]{1,0:T(8,128)S(1)}, f32[64,256]{1,0:T(8,128)S(1)}, u32[]{:S(2)}, u32[]{:S(2)}) %collective-permute-start.1) | collective-permute-done | bytes 65568 | tf_op jit(solution)/shard_map/ppermute | solution.py:54
  12.5 1.3 %collective-permute-done.3 = f32[64,256]{1,0:T(8,128)S(1)} collective-permute-done((f32[64,256]{1,0:T(8,128)S(1)}, f32[64,256]{1,0:T(8,128)S(1)}, u32[]{:S(2)}, u32[]{:S(2)}) %collective-permute-start.3) | collective-permute-done | bytes 65568 | tf_op jit(solution)/shard_map/ppermute | solution.py:54
  13.8 1.4 %collective-permute-done.2 = f32[64,256]{1,0:T(8,128)S(1)} collective-permute-done((f32[64,256]{1,0:T(8,128)S(1)}, f32[64,256]{1,0:T(8,128)S(1)}, u32[]{:S(2)}, u32[]{:S(2)}) %collective-permute-start.2) | collective-permute-done | bytes 65568 | tf_op jit(solution)/shard_map/ppermute | solution.py:54
  15.2 2.7 %collective-permute-start.4 = (f32[32,256]{1,0:T(8,128)S(1)}, f32[32,256]{1,0:T(8,128)S(1)}, u32[]{:S(2)}, u32[]{:S(2)}) collective-permute-start(f32[32,256]{1,0:T(8,128)S(1)} %slice_select_fusion.1), channel_id=1, source_target_pairs={{0,8},{1,9},{2,10},{3,11},{4,12},{5,13},{6,14},{7,15},{8,0},{9,1},... | collective-permute-start | bytes 98312 | tf_op jit(solution)/shard_map/ppermute | solution.py:47
  17.9 2.2 %collective-permute-done.4 = f32[32,256]{1,0:T(8,128)S(1)} collective-permute-done((f32[32,256]{1,0:T(8,128)S(1)}, f32[32,256]{1,0:T(8,128)S(1)}, u32[]{:S(2)}, u32[]{:S(2)}) %collective-permute-start.4) | collective-permute-done | bytes 32800 | tf_op jit(solution)/shard_map/ppermute | solution.py:47
  20.1 2.6 %collective-permute-start.5 = (f32[32,256]{1,0:T(8,128)S(1)}, f32[32,256]{1,0:T(8,128)S(1)}, u32[]{:S(2)}, u32[]{:S(2)}) collective-permute-start(f32[32,256]{1,0:T(8,128)S(1)} %select_add_fusion), channel_id=1, source_target_pairs={{0,8},{1,9},{2,10},{3,11},{4,12},{5,13},{6,14},{7,15},{8,0},{9,1},... | collective-permute-start | bytes 98312 | tf_op jit(solution)/shard_map/ppermute | solution.py:59
  22.7 0.1 broadcast_in_dim.30
  22.8 0.1 broadcast_in_dim.31
  22.9 2.1 %collective-permute-done.5 = f32[32,256]{1,0:T(8,128)S(1)} collective-permute-done((f32[32,256]{1,0:T(8,128)S(1)}, f32[32,256]{1,0:T(8,128)S(1)}, u32[]{:S(2)}, u32[]{:S(2)}) %collective-permute-start.5) | collective-permute-done | bytes 32800 | tf_op jit(solution)/shard_map/ppermute | solution.py:59
  25.0 1.1 %collective-permute-start.8 = (f32[64,256]{1,0:T(8,128)S(1)}, f32[64,256]{1,0:T(8,128)S(1)}, u32[]{:S(2)}, u32[]{:S(2)}) collective-permute-start(f32[64,256]{1,0:T(8,128)S(1)} %maximum_select_fusion.3), channel_id=1, source_target_pairs={{0,6},{1,7},{2,0},{3,1},{4,2},{5,3},{6,4},{7,5},{8,14},{9,15},{10,... | collective-permute-start | bytes 196616 | tf_op jit(solution)/shard_map/ppermute | solution.py:62
  26.1 1.1 %collective-permute-start.7 = (f32[64,256]{1,0:T(8,128)S(1)}, f32[64,256]{1,0:T(8,128)S(1)}, u32[]{:S(2)}, u32[]{:S(2)}) collective-permute-start(f32[64,256]{1,0:T(8,128)S(1)} %maximum_select_fusion.3), channel_id=1, source_target_pairs={{0,4},{1,5},{2,6},{3,7},{4,0},{5,1},{6,2},{7,3},{8,12},{9,13},{10,... | collective-permute-start | bytes 196616 | tf_op jit(solution)/shard_map/ppermute | solution.py:62
  27.2 0.8 %collective-permute-start.6 = (f32[64,256]{1,0:T(8,128)S(1)}, f32[64,256]{1,0:T(8,128)S(1)}, u32[]{:S(2)}, u32[]{:S(2)}) collective-permute-start(f32[64,256]{1,0:T(8,128)S(1)} %maximum_select_fusion.3), channel_id=1, source_target_pairs={{0,2},{1,3},{2,4},{3,5},{4,6},{5,7},{6,0},{7,1},{8,10},{9,11},{10,... | collective-permute-start | bytes 196616 | tf_op jit(solution)/shard_map/ppermute | solution.py:62
  28.1 1.3 %collective-permute-done.8 = f32[64,256]{1,0:T(8,128)S(1)} collective-permute-done((f32[64,256]{1,0:T(8,128)S(1)}, f32[64,256]{1,0:T(8,128)S(1)}, u32[]{:S(2)}, u32[]{:S(2)}) %collective-permute-start.8) | collective-permute-done | bytes 65568 | tf_op jit(solution)/shard_map/ppermute | solution.py:62
  29.3 1.0 %collective-permute-done.7 = f32[64,256]{1,0:T(8,128)S(1)} collective-permute-done((f32[64,256]{1,0:T(8,128)S(1)}, f32[64,256]{1,0:T(8,128)S(1)}, u32[]{:S(2)}, u32[]{:S(2)}) %collective-permute-start.7) | collective-permute-done | bytes 65568 | tf_op jit(solution)/shard_map/ppermute | solution.py:62
  30.4 2.0 %collective-permute-done.6 = f32[64,256]{1,0:T(8,128)S(1)} collective-permute-done((f32[64,256]{1,0:T(8,128)S(1)}, f32[64,256]{1,0:T(8,128)S(1)}, u32[]{:S(2)}, u32[]{:S(2)}) %collective-permute-start.6) | collective-permute-done | bytes 65568 | tf_op jit(solution)/shard_map/ppermute | solution.py:62
  32.4 0.6 %gather_fusion = f32[4,64,256]{2,1,0:T(8,128)S(1)} fusion(f32[4,64,256]{2,1,0:T(8,128)S(1)} %pad_maximum_fusion.1, s32[1024]{0:T(1024)S(1)} %pad_clamp_fusion), kind=kCustom, calls=%fused_computation | custom fusion | bytes 524304 | tf_op jit(solution)/shard_map/jit(_take)/gather | solution.py:65
  33.0 0.1 bitcast_select_fusion
  33.1 0.1 collective-permute-start.9
  33.2 1.5 %collective-permute-done.9 = f32[256,256]{1,0:T(8,128)S(1)} collective-permute-done((f32[256,256]{1,0:T(8,128)S(1)}, f32[256,256]{1,0:T(8,128)S(1)}, u32[]{:S(2)}, u32[]{:S(2)}) %collective-permute-start.9) | collective-permute-done | bytes 262176 | tf_op jit(solution)/shard_map/ppermute | solution.py:59
  34.7 0.1 fusion.7
  34.8 0.2 abs_reduce_fusion
  34.9 0.1 reduce_max.9
  35.1 0.5 fusion.6
  35.5 0.4 fusion.28
  36.0 0.4 fusion.17
  36.3 0.4 fusion.5
  36.7 0.4 fusion.34
  37.1 0.4 fusion.33
  37.5 0.4 fusion.4
  37.9 0.4 fusion.35
  38.3 0.4 fusion.36
  38.7 0.4 fusion.3
  39.1 0.4 convolution_divide_fusion
  39.5 0.3 fusion.22
  39.8 0.0 copy-start.1
  39.8 1.4 %collective-permute-start.10 = (f32[128,256]{1,0:T(8,128)S(1)}, f32[128,256]{1,0:T(8,128)S(1)}, u32[]{:S(2)}, u32[]{:S(2)}) collective-permute-start(f32[128,256]{1,0:T(8,128)S(1)} %slice_select_fusion), channel_id=1, source_target_pairs={{16,0},{17,1},{18,2},{19,3},{20,4},{21,5},{22,6},{23,7},{24,8},{25... | collective-permute-start | bytes 393224 | tf_op jit(solution)/shard_map/ppermute | solution.py:93
  41.2 6.1 %collective-permute-done.10 = f32[128,256]{1,0:T(8,128)S(1)} collective-permute-done((f32[128,256]{1,0:T(8,128)S(1)}, f32[128,256]{1,0:T(8,128)S(1)}, u32[]{:S(2)}, u32[]{:S(2)}) %collective-permute-start.10) | collective-permute-done | bytes 131104 | tf_op jit(solution)/shard_map/ppermute | solution.py:93
  47.4 1.3 %collective-permute-done.11 = f32[128,256]{1,0:T(8,128)S(1)} collective-permute-done((f32[128,256]{1,0:T(8,128)S(1)}, f32[128,256]{1,0:T(8,128)S(1)}, u32[]{:S(2)}, u32[]{:S(2)}) %collective-permute-start.11) | collective-permute-done | bytes 131104 | tf_op jit(solution)/shard_map/ppermute | solution.py:94
  48.7 0.3 fusion.9
  49.0 0.3 convolution_bitcast_fusion
  49.4 0.0 copy-start
  49.4 1.7 %fusion = bf16[2,1536,256]{2,1,0:T(8,128)(2,1)} fusion(bf16[2,1536,256]{2,1,0:T(8,128)(2,1)S(1)} %copy-done.1, f32[2,256,256]{2,1,0:T(8,128)S(1)} %pad_maximum_fusion), kind=kOutput, calls=%fused_computation.3 | convolution fusion | flops 403570688 | bytes 3670016 | tf_op jit(solution)/shard_map/trm,tmn->trn/dot_general | solution.py:150
  (20 shorter events, 0.3 us)
Async XLA Ops:
  4.3 1.7 %collective-permute-start = (f32[256,256]{1,0:T(8,128)S(1)}, f32[256,256]{1,0:T(8,128)S(1)}, u32[]{:S(2)}, u32[]{:S(2)}) collective-permute-start(f32[256,256]{1,0:T(8,128)S(1)} %select_bitcast_fusion), channel_id=1, source_target_pairs={{0,1},{1,0},{2,3},{3,2},{4,5},{5,4},{6,7},{7,6},{8,9},{9,8},{10,11... | collective-permute-start | bytes 786440 | tf_op jit(solution)/shard_map/ppermute | solution.py:47
  6.0 6.5 %collective-permute-start.1 = (f32[64,256]{1,0:T(8,128)S(1)}, f32[64,256]{1,0:T(8,128)S(1)}, u32[]{:S(2)}, u32[]{:S(2)}) collective-permute-start(f32[64,256]{1,0:T(8,128)S(1)} %get-tuple-element.2), channel_id=1, source_target_pairs={{0,2},{1,3},{2,4},{3,5},{4,6},{5,7},{6,0},{7,1},{8,10},{9,11},{10,... | collective-permute-start | bytes 196616 | tf_op jit(solution)/shard_map/ppermute | solution.py:54
  9.0 4.8 %collective-permute-start.3 = (f32[64,256]{1,0:T(8,128)S(1)}, f32[64,256]{1,0:T(8,128)S(1)}, u32[]{:S(2)}, u32[]{:S(2)}) collective-permute-start(f32[64,256]{1,0:T(8,128)S(1)} %get-tuple-element.3), channel_id=1, source_target_pairs={{0,6},{1,7},{2,0},{3,1},{4,2},{5,3},{6,4},{7,5},{8,14},{9,15},{10,... | collective-permute-start | bytes 196616 | tf_op jit(solution)/shard_map/ppermute | solution.py:54
  10.0 5.1 %collective-permute-start.2 = (f32[64,256]{1,0:T(8,128)S(1)}, f32[64,256]{1,0:T(8,128)S(1)}, u32[]{:S(2)}, u32[]{:S(2)}) collective-permute-start(f32[64,256]{1,0:T(8,128)S(1)} %get-tuple-element.4), channel_id=1, source_target_pairs={{0,4},{1,5},{2,6},{3,7},{4,0},{5,1},{6,2},{7,3},{8,12},{9,13},{10,... | collective-permute-start | bytes 196616 | tf_op jit(solution)/shard_map/ppermute | solution.py:54
  15.2 4.9 %collective-permute-start.4 = (f32[32,256]{1,0:T(8,128)S(1)}, f32[32,256]{1,0:T(8,128)S(1)}, u32[]{:S(2)}, u32[]{:S(2)}) collective-permute-start(f32[32,256]{1,0:T(8,128)S(1)} %slice_select_fusion.1), channel_id=1, source_target_pairs={{0,8},{1,9},{2,10},{3,11},{4,12},{5,13},{6,14},{7,15},{8,0},{9,1},... | collective-permute-start | bytes 98312 | tf_op jit(solution)/shard_map/ppermute | solution.py:47
  20.1 4.9 %collective-permute-start.5 = (f32[32,256]{1,0:T(8,128)S(1)}, f32[32,256]{1,0:T(8,128)S(1)}, u32[]{:S(2)}, u32[]{:S(2)}) collective-permute-start(f32[32,256]{1,0:T(8,128)S(1)} %select_add_fusion), channel_id=1, source_target_pairs={{0,8},{1,9},{2,10},{3,11},{4,12},{5,13},{6,14},{7,15},{8,0},{9,1},... | collective-permute-start | bytes 98312 | tf_op jit(solution)/shard_map/ppermute | solution.py:59
  25.0 4.3 %collective-permute-start.8 = (f32[64,256]{1,0:T(8,128)S(1)}, f32[64,256]{1,0:T(8,128)S(1)}, u32[]{:S(2)}, u32[]{:S(2)}) collective-permute-start(f32[64,256]{1,0:T(8,128)S(1)} %maximum_select_fusion.3), channel_id=1, source_target_pairs={{0,6},{1,7},{2,0},{3,1},{4,2},{5,3},{6,4},{7,5},{8,14},{9,15},{10,... | collective-permute-start | bytes 196616 | tf_op jit(solution)/shard_map/ppermute | solution.py:62
  26.1 4.3 %collective-permute-start.7 = (f32[64,256]{1,0:T(8,128)S(1)}, f32[64,256]{1,0:T(8,128)S(1)}, u32[]{:S(2)}, u32[]{:S(2)}) collective-permute-start(f32[64,256]{1,0:T(8,128)S(1)} %maximum_select_fusion.3), channel_id=1, source_target_pairs={{0,4},{1,5},{2,6},{3,7},{4,0},{5,1},{6,2},{7,3},{8,12},{9,13},{10,... | collective-permute-start | bytes 196616 | tf_op jit(solution)/shard_map/ppermute | solution.py:62
  27.2 5.2 %collective-permute-start.6 = (f32[64,256]{1,0:T(8,128)S(1)}, f32[64,256]{1,0:T(8,128)S(1)}, u32[]{:S(2)}, u32[]{:S(2)}) collective-permute-start(f32[64,256]{1,0:T(8,128)S(1)} %maximum_select_fusion.3), channel_id=1, source_target_pairs={{0,2},{1,3},{2,4},{3,5},{4,6},{5,7},{6,0},{7,1},{8,10},{9,11},{10,... | collective-permute-start | bytes 196616 | tf_op jit(solution)/shard_map/ppermute | solution.py:62
  33.1 1.6 %collective-permute-start.9 = (f32[256,256]{1,0:T(8,128)S(1)}, f32[256,256]{1,0:T(8,128)S(1)}, u32[]{:S(2)}, u32[]{:S(2)}) collective-permute-start(f32[256,256]{1,0:T(8,128)S(1)} %bitcast_select_fusion), channel_id=1, source_target_pairs={{0,1},{1,0},{2,3},{3,2},{4,5},{5,4},{6,7},{7,6},{8,9},{9,8},{10,11... | collective-permute-start | bytes 786440 | tf_op jit(solution)/shard_map/ppermute | solution.py:59
  39.8 9.6 %copy-start.1 = (bf16[2,1536,256]{2,1,0:T(8,128)(2,1)S(1)}, bf16[2,1536,256]{2,1,0:T(8,128)(2,1)}, u32[]{:S(2)}) copy-start(bf16[2,1536,256]{2,1,0:T(8,128)(2,1)} %param.2) | copy-start | bytes 4718596
  39.8 7.6 %collective-permute-start.10 = (f32[128,256]{1,0:T(8,128)S(1)}, f32[128,256]{1,0:T(8,128)S(1)}, u32[]{:S(2)}, u32[]{:S(2)}) collective-permute-start(f32[128,256]{1,0:T(8,128)S(1)} %slice_select_fusion), channel_id=1, source_target_pairs={{16,0},{17,1},{18,2},{19,3},{20,4},{21,5},{22,6},{23,7},{24,8},{25... | collective-permute-start | bytes 393224 | tf_op jit(solution)/shard_map/ppermute | solution.py:93
  47.4 1.3 %collective-permute-start.11 = (f32[128,256]{1,0:T(8,128)S(1)}, f32[128,256]{1,0:T(8,128)S(1)}, u32[]{:S(2)}, u32[]{:S(2)}) collective-permute-start(f32[128,256]{1,0:T(8,128)S(1)} %collective-permute-done.10), channel_id=1, source_target_pairs={{0,1},{1,0},{2,3},{3,2},{4,5},{5,4},{6,7},{7,6},{8,9},{9,8},{10,11... | collective-permute-start | bytes 393224 | tf_op jit(solution)/shard_map/ppermute | solution.py:94
  49.4 1.7 %copy-start = (f32[2,256,256]{2,1,0:T(8,128)}, f32[2,256,256]{2,1,0:T(8,128)S(1)}, u32[]{:S(2)}) copy-start(f32[2,256,256]{2,1,0:T(8,128)S(1)} %pad_maximum_fusion) | copy-start | bytes 1572868

commit v6 on v5

--- a/solution.py
+++ b/solution.py
@@ -8,6 +8,7 @@
 
 NS_STEPS = 4
 HI = lax.Precision.HIGH
+NS_PRECISION = lax.Precision.HIGH
 CHIP_RADIX = 4
 SPLIT = True
 PALLAS_SMOOTH = False
@@ -75,12 +76,12 @@
     identity = jnp.eye(covariance.shape[-1], dtype=jnp.float32)
     row_bound = jnp.max(jnp.sum(jnp.abs(covariance), axis=-1), axis=-1)
     iterate = covariance / row_bound[:, None, None]
-    inverse_root = jnp.broadcast_to(identity, covariance.shape)
-    for sweep_index in range(NS_STEPS):
-        factor = 1.5 * identity - 0.5 * jnp.matmul(inverse_root, iterate, precision=HI)
-        iterate = jnp.matmul(iterate, factor, precision=HI)
-        inverse_root = jnp.matmul(factor, inverse_root, precision=HI)
-    return inverse_root / jnp.sqrt(row_bound)[:, None, None]
+    factor = 1.5 * identity - 0.5 * iterate
+    pair = jnp.stack([jnp.matmul(iterate, factor, precision=NS_PRECISION), factor], axis=1)
+    for sweep_index in range(NS_STEPS - 1):
+        factor = 1.5 * identity - 0.5 * jnp.matmul(pair[:, 1], pair[:, 0], precision=NS_PRECISION)
+        pair = jnp.einsum("tkij,tjl->tkil", pair, factor, precision=NS_PRECISION)
+    return pair[:, 1] / jnp.sqrt(row_bound)[:, None, None]
 
 
 def split_shift(value, axis, pairs):
@@ -131,7 +132,8 @@
     times_dev, rows_dev, members = anomalies.shape
     total_rows = rows_dev * lax.axis_size("state")
     weighted = (anomalies * obs_weight[:, :, None]).astype(jnp.bfloat16)
-    partial_gram = jnp.einsum("trm,trn->tmn", weighted, weighted, preferred_element_type=jnp.float32)
+    half = rows_dev // 2
+    partial_gram = jnp.einsum("trm,trn->tmn", weighted[:, :half], weighted[:, :half], preferred_element_type=jnp.float32) + jnp.einsum("trm,trn->tmn", weighted[:, half:], weighted[:, half:], preferred_element_type=jnp.float32)
     gram_sum = state_sum(partial_gram, "state")
     covariance = gram_sum / total_rows + jnp.eye(members, dtype=jnp.float32)
     transform = newton_root(covariance)

time: 51.3 us -> 49.5 us (0.965)
  matrix products: 10.5 us -> 6.74 us
  other arithmetic: 0.7 us -> 2.72 us
    dot_general x12 -> x8, matrix products: 7.93 us -> 3.8 us  [the longest x3 1.24 us: newton_root(): jnp.matmul(pair[:, 1], pair[:, 0], precision=NS_PRECISION)]
    convert_element_type x1 -> x2, other arithmetic: 0.02 us -> 1.9 us  [the longest x1 1.88 us: on_device(): weighted = (anomalies * obs_weight[:, :, None]).astype(jnp.bfloat16)]
where the time goes in v6:
time: 49.5 us; the launch traced here: 49.3 us
  waiting for transfers between devices  22 us (44%)
  starting transfers between devices  16.2 us (33%)
  matrix products  6.74 us (14%)
  other arithmetic  2.72 us (5%)
  between operations  0.9 us (2%)
  local copies, waits for them, and re-layouts  0.77 us (2%)
    ppermute x1, waiting for transfers between devices, split_shift(): got = lax.ppermute(part, axis, pairs)  6.13 us
    ppermute x3, starting transfers between devices, grouped_sum(): lax.ppermute(send, axis, digit_pairs(count, radix, place, offset))  5.92 us
    ppermute x3, waiting for transfers between devices, grouped_sum(): lax.ppermute(value, axis, digit_pairs(count, radix, place, offset))  4.34 us
    ppermute x2, waiting for transfers between devices, grouped_sum(): other = lax.ppermute(value, axis, digit_pairs(count, radix, place, 1))  3.61 us
    ppermute x2, waiting for transfers between devices, grouped_sum(): value = keep + lax.ppermute(send, axis, digit_pairs(count, radix, place, 1))  3.38 us
    ppermute x3, waiting for transfers between devices, grouped_sum(): lax.ppermute(send, axis, digit_pairs(count, radix, place, offset))  3.22 us
    ppermute x2, starting transfers between devices, grouped_sum(): value = keep + lax.ppermute(send, axis, digit_pairs(count, radix, place, 1))  3.17 us
    ppermute x3, starting transfers between devices, grouped_sum(): lax.ppermute(value, axis, digit_pairs(count, radix, place, offset))  3.01 us
  transfers between devices with their start and end apart: 12, of which 12 were waited for; matrix products, arithmetic and copies ran while one was open for 0% of the time, Pallas kernels for 0%

profile of v6, /device:TPU:0, one launch (start us, length us, event | category | flops | bytes accessed | tf_op | source)
XLA Modules:
  0.0 49.3 jit_solution(3808711663580587879)
XLA Ops:
  0.6 1.9 %multiply_convert_fusion = bf16[2,1536,256]{2,1,0:T(8,128)(2,1)S(1)} fusion(bf16[2,1536,256]{2,1,0:T(8,128)(2,1)} %param.2, f32[2,1536]{1,0:T(2,128)} %param.3), kind=kLoop, calls=%fused_computation.1 | loop fusion | flops 2359296 | bytes 3158016 | tf_op jit(solution)/shard_map/convert_element_type | solution.py:134
  2.5 0.4 fusion.11
  3.0 0.4 convolution_add_fusion
  3.4 0.5 %collective-permute-start = (f32[256,256]{1,0:T(8,128)S(1)}, f32[256,256]{1,0:T(8,128)S(1)}, u32[]{:S(2)}, u32[]{:S(2)}) collective-permute-start(f32[256,256]{1,0:T(8,128)S(1)} %select_bitcast_fusion), channel_id=1, source_target_pairs={{0,1},{1,0},{2,3},{3,2},{4,5},{5,4},{6,7},{7,6},{8,9},{9,8},{10,11... | collective-permute-start | bytes 786440 | tf_op jit(solution)/shard_map/ppermute | solution.py:48
  4.0 1.2 %collective-permute-done = f32[256,256]{1,0:T(8,128)S(1)} collective-permute-done((f32[256,256]{1,0:T(8,128)S(1)}, f32[256,256]{1,0:T(8,128)S(1)}, u32[]{:S(2)}, u32[]{:S(2)}) %collective-permute-start) | collective-permute-done | bytes 262176 | tf_op jit(solution)/shard_map/ppermute | solution.py:48
  5.2 2.9 %collective-permute-start.1 = (f32[64,256]{1,0:T(8,128)S(1)}, f32[64,256]{1,0:T(8,128)S(1)}, u32[]{:S(2)}, u32[]{:S(2)}) collective-permute-start(f32[64,256]{1,0:T(8,128)S(1)} %get-tuple-element.2), channel_id=1, source_target_pairs={{0,2},{1,3},{2,4},{3,5},{4,6},{5,7},{6,0},{7,1},{8,10},{9,11},{10,... | collective-permute-start | bytes 196616 | tf_op jit(solution)/shard_map/ppermute | solution.py:55
  8.2 1.1 %collective-permute-start.3 = (f32[64,256]{1,0:T(8,128)S(1)}, f32[64,256]{1,0:T(8,128)S(1)}, u32[]{:S(2)}, u32[]{:S(2)}) collective-permute-start(f32[64,256]{1,0:T(8,128)S(1)} %get-tuple-element.3), channel_id=1, source_target_pairs={{0,6},{1,7},{2,0},{3,1},{4,2},{5,3},{6,4},{7,5},{8,14},{9,15},{10,... | collective-permute-start | bytes 196616 | tf_op jit(solution)/shard_map/ppermute | solution.py:55
  9.2 1.9 %collective-permute-start.2 = (f32[64,256]{1,0:T(8,128)S(1)}, f32[64,256]{1,0:T(8,128)S(1)}, u32[]{:S(2)}, u32[]{:S(2)}) collective-permute-start(f32[64,256]{1,0:T(8,128)S(1)} %get-tuple-element.4), channel_id=1, source_target_pairs={{0,4},{1,5},{2,6},{3,7},{4,0},{5,1},{6,2},{7,3},{8,12},{9,13},{10,... | collective-permute-start | bytes 196616 | tf_op jit(solution)/shard_map/ppermute | solution.py:55
  11.1 0.5 %collective-permute-done.1 = f32[64,256]{1,0:T(8,128)S(1)} collective-permute-done((f32[64,256]{1,0:T(8,128)S(1)}, f32[64,256]{1,0:T(8,128)S(1)}, u32[]{:S(2)}, u32[]{:S(2)}) %collective-permute-start.1) | collective-permute-done | bytes 65568 | tf_op jit(solution)/shard_map/ppermute | solution.py:55
  11.7 1.3 %collective-permute-done.3 = f32[64,256]{1,0:T(8,128)S(1)} collective-permute-done((f32[64,256]{1,0:T(8,128)S(1)}, f32[64,256]{1,0:T(8,128)S(1)}, u32[]{:S(2)}, u32[]{:S(2)}) %collective-permute-start.3) | collective-permute-done | bytes 65568 | tf_op jit(solution)/shard_map/ppermute | solution.py:55
  13.0 1.4 %collective-permute-done.2 = f32[64,256]{1,0:T(8,128)S(1)} collective-permute-done((f32[64,256]{1,0:T(8,128)S(1)}, f32[64,256]{1,0:T(8,128)S(1)}, u32[]{:S(2)}, u32[]{:S(2)}) %collective-permute-start.2) | collective-permute-done | bytes 65568 | tf_op jit(solution)/shard_map/ppermute | solution.py:55
  14.4 2.7 %collective-permute-start.4 = (f32[32,256]{1,0:T(8,128)S(1)}, f32[32,256]{1,0:T(8,128)S(1)}, u32[]{:S(2)}, u32[]{:S(2)}) collective-permute-start(f32[32,256]{1,0:T(8,128)S(1)} %slice_select_fusion.1), channel_id=1, source_target_pairs={{0,8},{1,9},{2,10},{3,11},{4,12},{5,13},{6,14},{7,15},{8,0},{9,1},... | collective-permute-start | bytes 98312 | tf_op jit(solution)/shard_map/ppermute | solution.py:48
  17.1 2.2 %collective-permute-done.4 = f32[32,256]{1,0:T(8,128)S(1)} collective-permute-done((f32[32,256]{1,0:T(8,128)S(1)}, f32[32,256]{1,0:T(8,128)S(1)}, u32[]{:S(2)}, u32[]{:S(2)}) %collective-permute-start.4) | collective-permute-done | bytes 32800 | tf_op jit(solution)/shard_map/ppermute | solution.py:48
  19.3 2.6 %collective-permute-start.5 = (f32[32,256]{1,0:T(8,128)S(1)}, f32[32,256]{1,0:T(8,128)S(1)}, u32[]{:S(2)}, u32[]{:S(2)}) collective-permute-start(f32[32,256]{1,0:T(8,128)S(1)} %select_add_fusion), channel_id=1, source_target_pairs={{0,8},{1,9},{2,10},{3,11},{4,12},{5,13},{6,14},{7,15},{8,0},{9,1},... | collective-permute-start | bytes 98312 | tf_op jit(solution)/shard_map/ppermute | solution.py:60
  21.9 0.1 broadcast_in_dim.22
  22.0 0.1 broadcast_in_dim.23
  22.1 2.1 %collective-permute-done.5 = f32[32,256]{1,0:T(8,128)S(1)} collective-permute-done((f32[32,256]{1,0:T(8,128)S(1)}, f32[32,256]{1,0:T(8,128)S(1)}, u32[]{:S(2)}, u32[]{:S(2)}) %collective-permute-start.5) | collective-permute-done | bytes 32800 | tf_op jit(solution)/shard_map/ppermute | solution.py:60
  24.2 1.1 %collective-permute-start.8 = (f32[64,256]{1,0:T(8,128)S(1)}, f32[64,256]{1,0:T(8,128)S(1)}, u32[]{:S(2)}, u32[]{:S(2)}) collective-permute-start(f32[64,256]{1,0:T(8,128)S(1)} %maximum_select_fusion.3), channel_id=1, source_target_pairs={{0,6},{1,7},{2,0},{3,1},{4,2},{5,3},{6,4},{7,5},{8,14},{9,15},{10,... | collective-permute-start | bytes 196616 | tf_op jit(solution)/shard_map/ppermute | solution.py:63
  25.3 1.1 %collective-permute-start.7 = (f32[64,256]{1,0:T(8,128)S(1)}, f32[64,256]{1,0:T(8,128)S(1)}, u32[]{:S(2)}, u32[]{:S(2)}) collective-permute-start(f32[64,256]{1,0:T(8,128)S(1)} %maximum_select_fusion.3), channel_id=1, source_target_pairs={{0,4},{1,5},{2,6},{3,7},{4,0},{5,1},{6,2},{7,3},{8,12},{9,13},{10,... | collective-permute-start | bytes 196616 | tf_op jit(solution)/shard_map/ppermute | solution.py:63
  26.4 0.8 %collective-permute-start.6 = (f32[64,256]{1,0:T(8,128)S(1)}, f32[64,256]{1,0:T(8,128)S(1)}, u32[]{:S(2)}, u32[]{:S(2)}) collective-permute-start(f32[64,256]{1,0:T(8,128)S(1)} %maximum_select_fusion.3), channel_id=1, source_target_pairs={{0,2},{1,3},{2,4},{3,5},{4,6},{5,7},{6,0},{7,1},{8,10},{9,11},{10,... | collective-permute-start | bytes 196616 | tf_op jit(solution)/shard_map/ppermute | solution.py:63
  27.2 1.3 %collective-permute-done.8 = f32[64,256]{1,0:T(8,128)S(1)} collective-permute-done((f32[64,256]{1,0:T(8,128)S(1)}, f32[64,256]{1,0:T(8,128)S(1)}, u32[]{:S(2)}, u32[]{:S(2)}) %collective-permute-start.8) | collective-permute-done | bytes 65568 | tf_op jit(solution)/shard_map/ppermute | solution.py:63
  28.5 1.0 %collective-permute-done.7 = f32[64,256]{1,0:T(8,128)S(1)} collective-permute-done((f32[64,256]{1,0:T(8,128)S(1)}, f32[64,256]{1,0:T(8,128)S(1)}, u32[]{:S(2)}, u32[]{:S(2)}) %collective-permute-start.7) | collective-permute-done | bytes 65568 | tf_op jit(solution)/shard_map/ppermute | solution.py:63
  29.6 2.0 %collective-permute-done.6 = f32[64,256]{1,0:T(8,128)S(1)} collective-permute-done((f32[64,256]{1,0:T(8,128)S(1)}, f32[64,256]{1,0:T(8,128)S(1)}, u32[]{:S(2)}, u32[]{:S(2)}) %collective-permute-start.6) | collective-permute-done | bytes 65568 | tf_op jit(solution)/shard_map/ppermute | solution.py:63
  31.6 0.6 %gather_fusion = f32[4,64,256]{2,1,0:T(8,128)S(1)} fusion(f32[4,64,256]{2,1,0:T(8,128)S(1)} %pad_maximum_fusion.2, s32[1024]{0:T(1024)S(1)} %pad_clamp_fusion), kind=kCustom, calls=%fused_computation | custom fusion | bytes 524304 | tf_op jit(solution)/shard_map/jit(_take)/gather | solution.py:66
  32.2 0.1 bitcast_select_fusion
  32.3 0.1 collective-permute-start.9
  32.4 1.5 %collective-permute-done.9 = f32[256,256]{1,0:T(8,128)S(1)} collective-permute-done((f32[256,256]{1,0:T(8,128)S(1)}, f32[256,256]{1,0:T(8,128)S(1)}, u32[]{:S(2)}, u32[]{:S(2)}) %collective-permute-start.9) | collective-permute-done | bytes 262176 | tf_op jit(solution)/shard_map/ppermute | solution.py:60
  33.9 0.1 fusion.13
  33.9 0.2 abs_reduce_fusion
  34.1 0.1 reduce_max.9
  34.2 0.5 %fusion.14 = f32[2,256,256]{2,1,0:T(8,128)S(1)} fusion(f32[256,256]{1,0:T(8,128)S(1)} %fusion.28, f32[2]{0:T(128)S(1)} %reduce_max.9, f32[256,256]{1,0:T(8,128)S(1)} %fusion.29, f32[512,256]{1,0:T(8,128)S(1)} %fusion.13), kind=kOutput, calls=%fused_computation.32 | convolution fusion | flops 202113024 | bytes 1572872 | tf_op jit(solution)/shard_map/dot_general | solution.py:80
  34.8 0.5 fusion.6
  35.2 0.1 multiply_subtract_fusion
  35.4 0.6 %fusion.7 = f32[2,2,256,256]{3,2,1,0:T(8,128)S(1)} fusion(f32[2,256,256,1]{2,1,3,0:T(8,128)S(1)} %fusion.6, f32[2,1,256,256]{3,2,0,1:T(8,128)S(1)} %multiply_subtract_fusion, f32[2,1,256,256]{3,2,0,1:T(8,128)S(1)} %bitcast.90), kind=kOutput, calls=%fused_computation.17 | convolution fusion | flops 402915328 | bytes 2621440 | tf_op jit(solution)/shard_map/tkij,tjl->tkil/dot_general | solution.py:83
  36.0 0.4 fusion.4
  36.4 0.6 %fusion.42 = f32[2,2,256,256]{3,2,1,0:T(8,128)S(1)} fusion(f32[2,2,256,256]{3,2,1,0:T(8,128)S(1)} %fusion.7, f32[2,256,256,1]{2,1,3,0:T(8,128)S(1)} %fusion.4), kind=kOutput, calls=%fused_computation.87 | convolution fusion | flops 402653184 | bytes 2621440 | tf_op jit(solution)/shard_map/tkij,tjl->tkil/dot_general | solution.py:83
  37.0 0.4 fusion.2
  37.4 0.4 fusion.9
  37.8 0.3 fusion.30
  38.0 0.0 copy-start
  38.1 1.4 %collective-permute-start.10 = (f32[128,256]{1,0:T(8,128)S(1)}, f32[128,256]{1,0:T(8,128)S(1)}, u32[]{:S(2)}, u32[]{:S(2)}) collective-permute-start(f32[128,256]{1,0:T(8,128)S(1)} %slice_select_fusion), channel_id=1, source_target_pairs={{16,0},{17,1},{18,2},{19,3},{20,4},{21,5},{22,6},{23,7},{24,8},{25... | collective-permute-start | bytes 393224 | tf_op jit(solution)/shard_map/ppermute | solution.py:94
  39.5 6.1 %collective-permute-done.10 = f32[128,256]{1,0:T(8,128)S(1)} collective-permute-done((f32[128,256]{1,0:T(8,128)S(1)}, f32[128,256]{1,0:T(8,128)S(1)}, u32[]{:S(2)}, u32[]{:S(2)}) %collective-permute-start.10) | collective-permute-done | bytes 131104 | tf_op jit(solution)/shard_map/ppermute | solution.py:94
  45.6 0.0 collective-permute-start.11
  45.6 1.3 %collective-permute-done.11 = f32[128,256]{1,0:T(8,128)S(1)} collective-permute-done((f32[128,256]{1,0:T(8,128)S(1)}, f32[128,256]{1,0:T(8,128)S(1)}, u32[]{:S(2)}, u32[]{:S(2)}) %collective-permute-start.11) | collective-permute-done | bytes 131104 | tf_op jit(solution)/shard_map/ppermute | solution.py:95
  47.0 0.3 fusion.16
  47.3 0.3 convolution_bitcast_fusion.1
  47.6 0.0 copy-start.1
  47.6 1.7 %fusion = bf16[2,1536,256]{2,1,0:T(8,128)(2,1)} fusion(bf16[2,1536,256]{2,1,0:T(8,128)(2,1)S(1)} %copy-done, f32[2,256,256]{2,1,0:T(8,128)S(1)} %pad_maximum_fusion.1), kind=kOutput, calls=%fused_computation.3 | convolution fusion | flops 403570688 | bytes 3670016 | tf_op jit(solution)/shard_map/trm,tmn->trn/dot_general | solution.py:152
  (19 shorter events, 0.3 us)
Async XLA Ops:
  3.4 1.7 %collective-permute-start = (f32[256,256]{1,0:T(8,128)S(1)}, f32[256,256]{1,0:T(8,128)S(1)}, u32[]{:S(2)}, u32[]{:S(2)}) collective-permute-start(f32[256,256]{1,0:T(8,128)S(1)} %select_bitcast_fusion), channel_id=1, source_target_pairs={{0,1},{1,0},{2,3},{3,2},{4,5},{5,4},{6,7},{7,6},{8,9},{9,8},{10,11... | collective-permute-start | bytes 786440 | tf_op jit(solution)/shard_map/ppermute | solution.py:48
  5.2 6.4 %collective-permute-start.1 = (f32[64,256]{1,0:T(8,128)S(1)}, f32[64,256]{1,0:T(8,128)S(1)}, u32[]{:S(2)}, u32[]{:S(2)}) collective-permute-start(f32[64,256]{1,0:T(8,128)S(1)} %get-tuple-element.2), channel_id=1, source_target_pairs={{0,2},{1,3},{2,4},{3,5},{4,6},{5,7},{6,0},{7,1},{8,10},{9,11},{10,... | collective-permute-start | bytes 196616 | tf_op jit(solution)/shard_map/ppermute | solution.py:55
  8.2 4.8 %collective-permute-start.3 = (f32[64,256]{1,0:T(8,128)S(1)}, f32[64,256]{1,0:T(8,128)S(1)}, u32[]{:S(2)}, u32[]{:S(2)}) collective-permute-start(f32[64,256]{1,0:T(8,128)S(1)} %get-tuple-element.3), channel_id=1, source_target_pairs={{0,6},{1,7},{2,0},{3,1},{4,2},{5,3},{6,4},{7,5},{8,14},{9,15},{10,... | collective-permute-start | bytes 196616 | tf_op jit(solution)/shard_map/ppermute | solution.py:55
  9.2 5.1 %collective-permute-start.2 = (f32[64,256]{1,0:T(8,128)S(1)}, f32[64,256]{1,0:T(8,128)S(1)}, u32[]{:S(2)}, u32[]{:S(2)}) collective-permute-start(f32[64,256]{1,0:T(8,128)S(1)} %get-tuple-element.4), channel_id=1, source_target_pairs={{0,4},{1,5},{2,6},{3,7},{4,0},{5,1},{6,2},{7,3},{8,12},{9,13},{10,... | collective-permute-start | bytes 196616 | tf_op jit(solution)/shard_map/ppermute | solution.py:55
  14.4 4.9 %collective-permute-start.4 = (f32[32,256]{1,0:T(8,128)S(1)}, f32[32,256]{1,0:T(8,128)S(1)}, u32[]{:S(2)}, u32[]{:S(2)}) collective-permute-start(f32[32,256]{1,0:T(8,128)S(1)} %slice_select_fusion.1), channel_id=1, source_target_pairs={{0,8},{1,9},{2,10},{3,11},{4,12},{5,13},{6,14},{7,15},{8,0},{9,1},... | collective-permute-start | bytes 98312 | tf_op jit(solution)/shard_map/ppermute | solution.py:48
  19.3 4.9 %collective-permute-start.5 = (f32[32,256]{1,0:T(8,128)S(1)}, f32[32,256]{1,0:T(8,128)S(1)}, u32[]{:S(2)}, u32[]{:S(2)}) collective-permute-start(f32[32,256]{1,0:T(8,128)S(1)} %select_add_fusion), channel_id=1, source_target_pairs={{0,8},{1,9},{2,10},{3,11},{4,12},{5,13},{6,14},{7,15},{8,0},{9,1},... | collective-permute-start | bytes 98312 | tf_op jit(solution)/shard_map/ppermute | solution.py:60
  24.2 4.3 %collective-permute-start.8 = (f32[64,256]{1,0:T(8,128)S(1)}, f32[64,256]{1,0:T(8,128)S(1)}, u32[]{:S(2)}, u32[]{:S(2)}) collective-permute-start(f32[64,256]{1,0:T(8,128)S(1)} %maximum_select_fusion.3), channel_id=1, source_target_pairs={{0,6},{1,7},{2,0},{3,1},{4,2},{5,3},{6,4},{7,5},{8,14},{9,15},{10,... | collective-permute-start | bytes 196616 | tf_op jit(solution)/shard_map/ppermute | solution.py:63
  25.3 4.3 %collective-permute-start.7 = (f32[64,256]{1,0:T(8,128)S(1)}, f32[64,256]{1,0:T(8,128)S(1)}, u32[]{:S(2)}, u32[]{:S(2)}) collective-permute-start(f32[64,256]{1,0:T(8,128)S(1)} %maximum_select_fusion.3), channel_id=1, source_target_pairs={{0,4},{1,5},{2,6},{3,7},{4,0},{5,1},{6,2},{7,3},{8,12},{9,13},{10,... | collective-permute-start | bytes 196616 | tf_op jit(solution)/shard_map/ppermute | solution.py:63
  26.4 5.2 %collective-permute-start.6 = (f32[64,256]{1,0:T(8,128)S(1)}, f32[64,256]{1,0:T(8,128)S(1)}, u32[]{:S(2)}, u32[]{:S(2)}) collective-permute-start(f32[64,256]{1,0:T(8,128)S(1)} %maximum_select_fusion.3), channel_id=1, source_target_pairs={{0,2},{1,3},{2,4},{3,5},{4,6},{5,7},{6,0},{7,1},{8,10},{9,11},{10,... | collective-permute-start | bytes 196616 | tf_op jit(solution)/shard_map/ppermute | solution.py:63
  32.3 1.6 %collective-permute-start.9 = (f32[256,256]{1,0:T(8,128)S(1)}, f32[256,256]{1,0:T(8,128)S(1)}, u32[]{:S(2)}, u32[]{:S(2)}) collective-permute-start(f32[256,256]{1,0:T(8,128)S(1)} %bitcast_select_fusion), channel_id=1, source_target_pairs={{0,1},{1,0},{2,3},{3,2},{4,5},{5,4},{6,7},{7,6},{8,9},{9,8},{10,11... | collective-permute-start | bytes 786440 | tf_op jit(solution)/shard_map/ppermute | solution.py:60
  38.0 9.6 %copy-start = (bf16[2,1536,256]{2,1,0:T(8,128)(2,1)S(1)}, bf16[2,1536,256]{2,1,0:T(8,128)(2,1)}, u32[]{:S(2)}) copy-start(bf16[2,1536,256]{2,1,0:T(8,128)(2,1)} %param.2) | copy-start | bytes 4718596
  38.1 7.6 %collective-permute-start.10 = (f32[128,256]{1,0:T(8,128)S(1)}, f32[128,256]{1,0:T(8,128)S(1)}, u32[]{:S(2)}, u32[]{:S(2)}) collective-permute-start(f32[128,256]{1,0:T(8,128)S(1)} %slice_select_fusion), channel_id=1, source_target_pairs={{16,0},{17,1},{18,2},{19,3},{20,4},{21,5},{22,6},{23,7},{24,8},{25... | collective-permute-start | bytes 393224 | tf_op jit(solution)/shard_map/ppermute | solution.py:94
  45.6 1.3 %collective-permute-start.11 = (f32[128,256]{1,0:T(8,128)S(1)}, f32[128,256]{1,0:T(8,128)S(1)}, u32[]{:S(2)}, u32[]{:S(2)}) collective-permute-start(f32[128,256]{1,0:T(8,128)S(1)} %collective-permute-done.10), channel_id=1, source_target_pairs={{0,1},{1,0},{2,3},{3,2},{4,5},{5,4},{6,7},{7,6},{8,9},{9,8},{10,11... | collective-permute-start | bytes 393224 | tf_op jit(solution)/shard_map/ppermute | solution.py:95
  47.6 1.7 %copy-start.1 = (f32[2,256,256]{2,1,0:T(8,128)}, f32[2,256,256]{2,1,0:T(8,128)S(1)}, u32[]{:S(2)}) copy-start(f32[2,256,256]{2,1,0:T(8,128)S(1)} %pad_maximum_fusion.1) | copy-start | bytes 1572868

commit v7 on v6

--- a/solution.py
+++ b/solution.py
@@ -8,7 +8,7 @@
 
 NS_STEPS = 4
 HI = lax.Precision.HIGH
-NS_PRECISION = lax.Precision.HIGH
+NS_PRECISION = lax.Precision.HIGHEST
 CHIP_RADIX = 4
 SPLIT = True
 PALLAS_SMOOTH = False

time: 49.5 us -> 51.9 us (1.048)
  matrix products: 6.74 us -> 9.07 us
    dot_general x2, matrix products: 1.18 us -> 2.14 us  [newton_root(): pair = jnp.einsum('tkij,tjl->tkil', pair, factor, precision=NS_PRECISION)]
    dot_general x3, matrix products: 1.24 us -> 2.04 us  [newton_root(): jnp.matmul(pair[:, 1], pair[:, 0], precision=NS_PRECISION)]
where the time goes in v7:
time: 51.9 us; the launch traced here: 51.7 us
  waiting for transfers between devices  22 us (42%)
  starting transfers between devices  16.2 us (31%)
  matrix products  9.07 us (17%)
  other arithmetic  2.72 us (5%)
  between operations  0.9 us (2%)
  local copies, waits for them, and re-layouts  0.77 us (1%)
    ppermute x1, waiting for transfers between devices, split_shift(): got = lax.ppermute(part, axis, pairs)  6.13 us
    ppermute x3, starting transfers between devices, grouped_sum(): lax.ppermute(send, axis, digit_pairs(count, radix, place, offset))  5.92 us
    ppermute x3, waiting for transfers between devices, grouped_sum(): lax.ppermute(value, axis, digit_pairs(count, radix, place, offset))  4.34 us
    ppermute x2, waiting for transfers between devices, grouped_sum(): other = lax.ppermute(value, axis, digit_pairs(count, radix, place, 1))  3.61 us
    ppermute x2, waiting for transfers between devices, grouped_sum(): value = keep + lax.ppermute(send, axis, digit_pairs(count, radix, place, 1))  3.38 us
    ppermute x3, waiting for transfers between devices, grouped_sum(): lax.ppermute(send, axis, digit_pairs(count, radix, place, offset))  3.22 us
    ppermute x2, starting transfers between devices, grouped_sum(): value = keep + lax.ppermute(send, axis, digit_pairs(count, radix, place, 1))  3.17 us
    ppermute x3, starting transfers between devices, grouped_sum(): lax.ppermute(value, axis, digit_pairs(count, radix, place, offset))  3.01 us
  transfers between devices with their start and end apart: 12, of which 12 were waited for; matrix products, arithmetic and copies ran while one was open for 0% of the time, Pallas kernels for 0%

profile of v7, /device:TPU:0, one launch (start us, length us, event | category | flops | bytes accessed | tf_op | source)
XLA Modules:
  0.0 51.7 jit_solution(12648165576841892100)
XLA Ops:
  0.6 1.9 %multiply_convert_fusion = bf16[2,1536,256]{2,1,0:T(8,128)(2,1)S(1)} fusion(bf16[2,1536,256]{2,1,0:T(8,128)(2,1)} %param.2, f32[2,1536]{1,0:T(2,128)} %param.3), kind=kLoop, calls=%fused_computation.1 | loop fusion | flops 2359296 | bytes 3158016 | tf_op jit(solution)/shard_map/convert_element_type | solution.py:134
  2.5 0.4 fusion.11
  3.0 0.4 convolution_add_fusion
  3.4 0.5 %collective-permute-start = (f32[256,256]{1,0:T(8,128)S(1)}, f32[256,256]{1,0:T(8,128)S(1)}, u32[]{:S(2)}, u32[]{:S(2)}) collective-permute-start(f32[256,256]{1,0:T(8,128)S(1)} %select_bitcast_fusion), channel_id=1, source_target_pairs={{0,1},{1,0},{2,3},{3,2},{4,5},{5,4},{6,7},{7,6},{8,9},{9,8},{10,11... | collective-permute-start | bytes 786440 | tf_op jit(solution)/shard_map/ppermute | solution.py:48
  4.0 1.2 %collective-permute-done = f32[256,256]{1,0:T(8,128)S(1)} collective-permute-done((f32[256,256]{1,0:T(8,128)S(1)}, f32[256,256]{1,0:T(8,128)S(1)}, u32[]{:S(2)}, u32[]{:S(2)}) %collective-permute-start) | collective-permute-done | bytes 262176 | tf_op jit(solution)/shard_map/ppermute | solution.py:48
  5.2 2.9 %collective-permute-start.1 = (f32[64,256]{1,0:T(8,128)S(1)}, f32[64,256]{1,0:T(8,128)S(1)}, u32[]{:S(2)}, u32[]{:S(2)}) collective-permute-start(f32[64,256]{1,0:T(8,128)S(1)} %get-tuple-element.2), channel_id=1, source_target_pairs={{0,2},{1,3},{2,4},{3,5},{4,6},{5,7},{6,0},{7,1},{8,10},{9,11},{10,... | collective-permute-start | bytes 196616 | tf_op jit(solution)/shard_map/ppermute | solution.py:55
  8.2 1.1 %collective-permute-start.3 = (f32[64,256]{1,0:T(8,128)S(1)}, f32[64,256]{1,0:T(8,128)S(1)}, u32[]{:S(2)}, u32[]{:S(2)}) collective-permute-start(f32[64,256]{1,0:T(8,128)S(1)} %get-tuple-element.3), channel_id=1, source_target_pairs={{0,6},{1,7},{2,0},{3,1},{4,2},{5,3},{6,4},{7,5},{8,14},{9,15},{10,... | collective-permute-start | bytes 196616 | tf_op jit(solution)/shard_map/ppermute | solution.py:55
  9.2 1.9 %collective-permute-start.2 = (f32[64,256]{1,0:T(8,128)S(1)}, f32[64,256]{1,0:T(8,128)S(1)}, u32[]{:S(2)}, u32[]{:S(2)}) collective-permute-start(f32[64,256]{1,0:T(8,128)S(1)} %get-tuple-element.4), channel_id=1, source_target_pairs={{0,4},{1,5},{2,6},{3,7},{4,0},{5,1},{6,2},{7,3},{8,12},{9,13},{10,... | collective-permute-start | bytes 196616 | tf_op jit(solution)/shard_map/ppermute | solution.py:55
  11.1 0.5 collective-permute-done.1
  11.7 1.3 %collective-permute-done.3 = f32[64,256]{1,0:T(8,128)S(1)} collective-permute-done((f32[64,256]{1,0:T(8,128)S(1)}, f32[64,256]{1,0:T(8,128)S(1)}, u32[]{:S(2)}, u32[]{:S(2)}) %collective-permute-start.3) | collective-permute-done | bytes 65568 | tf_op jit(solution)/shard_map/ppermute | solution.py:55
  13.0 1.4 %collective-permute-done.2 = f32[64,256]{1,0:T(8,128)S(1)} collective-permute-done((f32[64,256]{1,0:T(8,128)S(1)}, f32[64,256]{1,0:T(8,128)S(1)}, u32[]{:S(2)}, u32[]{:S(2)}) %collective-permute-start.2) | collective-permute-done | bytes 65568 | tf_op jit(solution)/shard_map/ppermute | solution.py:55
  14.4 2.7 %collective-permute-start.4 = (f32[32,256]{1,0:T(8,128)S(1)}, f32[32,256]{1,0:T(8,128)S(1)}, u32[]{:S(2)}, u32[]{:S(2)}) collective-permute-start(f32[32,256]{1,0:T(8,128)S(1)} %slice_select_fusion.1), channel_id=1, source_target_pairs={{0,8},{1,9},{2,10},{3,11},{4,12},{5,13},{6,14},{7,15},{8,0},{9,1},... | collective-permute-start | bytes 98312 | tf_op jit(solution)/shard_map/ppermute | solution.py:48
  17.1 2.2 %collective-permute-done.4 = f32[32,256]{1,0:T(8,128)S(1)} collective-permute-done((f32[32,256]{1,0:T(8,128)S(1)}, f32[32,256]{1,0:T(8,128)S(1)}, u32[]{:S(2)}, u32[]{:S(2)}) %collective-permute-start.4) | collective-permute-done | bytes 32800 | tf_op jit(solution)/shard_map/ppermute | solution.py:48
  19.3 2.6 %collective-permute-start.5 = (f32[32,256]{1,0:T(8,128)S(1)}, f32[32,256]{1,0:T(8,128)S(1)}, u32[]{:S(2)}, u32[]{:S(2)}) collective-permute-start(f32[32,256]{1,0:T(8,128)S(1)} %select_add_fusion), channel_id=1, source_target_pairs={{0,8},{1,9},{2,10},{3,11},{4,12},{5,13},{6,14},{7,15},{8,0},{9,1},... | collective-permute-start | bytes 98312 | tf_op jit(solution)/shard_map/ppermute | solution.py:60
  21.9 0.1 broadcast_in_dim.22
  22.0 0.1 broadcast_in_dim.23
  22.1 2.1 %collective-permute-done.5 = f32[32,256]{1,0:T(8,128)S(1)} collective-permute-done((f32[32,256]{1,0:T(8,128)S(1)}, f32[32,256]{1,0:T(8,128)S(1)}, u32[]{:S(2)}, u32[]{:S(2)}) %collective-permute-start.5) | collective-permute-done | bytes 32800 | tf_op jit(solution)/shard_map/ppermute | solution.py:60
  24.2 1.1 %collective-permute-start.8 = (f32[64,256]{1,0:T(8,128)S(1)}, f32[64,256]{1,0:T(8,128)S(1)}, u32[]{:S(2)}, u32[]{:S(2)}) collective-permute-start(f32[64,256]{1,0:T(8,128)S(1)} %maximum_select_fusion.3), channel_id=1, source_target_pairs={{0,6},{1,7},{2,0},{3,1},{4,2},{5,3},{6,4},{7,5},{8,14},{9,15},{10,... | collective-permute-start | bytes 196616 | tf_op jit(solution)/shard_map/ppermute | solution.py:63
  25.3 1.1 %collective-permute-start.7 = (f32[64,256]{1,0:T(8,128)S(1)}, f32[64,256]{1,0:T(8,128)S(1)}, u32[]{:S(2)}, u32[]{:S(2)}) collective-permute-start(f32[64,256]{1,0:T(8,128)S(1)} %maximum_select_fusion.3), channel_id=1, source_target_pairs={{0,4},{1,5},{2,6},{3,7},{4,0},{5,1},{6,2},{7,3},{8,12},{9,13},{10,... | collective-permute-start | bytes 196616 | tf_op jit(solution)/shard_map/ppermute | solution.py:63
  26.4 0.8 %collective-permute-start.6 = (f32[64,256]{1,0:T(8,128)S(1)}, f32[64,256]{1,0:T(8,128)S(1)}, u32[]{:S(2)}, u32[]{:S(2)}) collective-permute-start(f32[64,256]{1,0:T(8,128)S(1)} %maximum_select_fusion.3), channel_id=1, source_target_pairs={{0,2},{1,3},{2,4},{3,5},{4,6},{5,7},{6,0},{7,1},{8,10},{9,11},{10,... | collective-permute-start | bytes 196616 | tf_op jit(solution)/shard_map/ppermute | solution.py:63
  27.2 1.3 %collective-permute-done.8 = f32[64,256]{1,0:T(8,128)S(1)} collective-permute-done((f32[64,256]{1,0:T(8,128)S(1)}, f32[64,256]{1,0:T(8,128)S(1)}, u32[]{:S(2)}, u32[]{:S(2)}) %collective-permute-start.8) | collective-permute-done | bytes 65568 | tf_op jit(solution)/shard_map/ppermute | solution.py:63
  28.5 1.0 %collective-permute-done.7 = f32[64,256]{1,0:T(8,128)S(1)} collective-permute-done((f32[64,256]{1,0:T(8,128)S(1)}, f32[64,256]{1,0:T(8,128)S(1)}, u32[]{:S(2)}, u32[]{:S(2)}) %collective-permute-start.7) | collective-permute-done | bytes 65568 | tf_op jit(solution)/shard_map/ppermute | solution.py:63
  29.6 2.0 %collective-permute-done.6 = f32[64,256]{1,0:T(8,128)S(1)} collective-permute-done((f32[64,256]{1,0:T(8,128)S(1)}, f32[64,256]{1,0:T(8,128)S(1)}, u32[]{:S(2)}, u32[]{:S(2)}) %collective-permute-start.6) | collective-permute-done | bytes 65568 | tf_op jit(solution)/shard_map/ppermute | solution.py:63
  31.6 0.6 %gather_fusion = f32[4,64,256]{2,1,0:T(8,128)S(1)} fusion(f32[4,64,256]{2,1,0:T(8,128)S(1)} %pad_maximum_fusion.2, s32[1024]{0:T(1024)S(1)} %pad_clamp_fusion), kind=kCustom, calls=%fused_computation | custom fusion | bytes 524304 | tf_op jit(solution)/shard_map/jit(_take)/gather | solution.py:66
  32.2 0.1 bitcast_select_fusion
  32.3 0.1 collective-permute-start.9
  32.4 1.5 %collective-permute-done.9 = f32[256,256]{1,0:T(8,128)S(1)} collective-permute-done((f32[256,256]{1,0:T(8,128)S(1)}, f32[256,256]{1,0:T(8,128)S(1)}, u32[]{:S(2)}, u32[]{:S(2)}) %collective-permute-start.9) | collective-permute-done | bytes 262176 | tf_op jit(solution)/shard_map/ppermute | solution.py:60
  33.9 0.1 fusion.13
  33.9 0.2 abs_reduce_fusion
  34.1 0.1 reduce_max.9
  34.2 0.8 %fusion.14 = f32[2,256,256]{2,1,0:T(8,128)S(1)} fusion(f32[256,256]{1,0:T(8,128)S(1)} %fusion.28, f32[2]{0:T(128)S(1)} %reduce_max.9, f32[256,256]{1,0:T(8,128)S(1)} %fusion.29, f32[512,256]{1,0:T(8,128)S(1)} %fusion.13), kind=kOutput, calls=%fused_computation.32 | convolution fusion | flops 403439616 | bytes 1572872 | tf_op jit(solution)/shard_map/dot_general | solution.py:80
  35.1 0.7 %fusion.6 = f32[2,256,256,1]{2,1,3,0:T(8,128)S(1)} fusion(f32[2,256,256]{2,1,0:T(8,128)S(1)} %fusion.14, f32[256,256]{1,0:T(8,128)S(1)} %fusion.28, f32[2]{0:T(128)S(1)} %reduce_max.9, f32[256,256]{1,0:T(8,128)S(1)} %fusion.29, f32[512,256]{1,0:T(8,128)S(1)} %fusion.13), kind=kOutput, calls=%fused_computation.14 | convolution fusion | flops 403439616 | bytes 2097160 | tf_op jit(solution)/shard_map/dot_general | solution.py:82
  35.8 0.1 multiply_subtract_fusion
  35.9 1.1 %fusion.7 = f32[2,2,256,256]{3,2,1,0:T(8,128)S(1)} fusion(f32[2,256,256,1]{2,1,3,0:T(8,128)S(1)} %fusion.6, f32[2,1,256,256]{3,2,0,1:T(8,128)S(1)} %multiply_subtract_fusion, f32[2,1,256,256]{3,2,0,1:T(8,128)S(1)} %bitcast.90), kind=kOutput, calls=%fused_computation.17 | convolution fusion | flops 805568512 | bytes 2621440 | tf_op jit(solution)/shard_map/tkij,tjl->tkil/dot_general | solution.py:83
  37.0 0.7 %fusion.4 = f32[2,256,256,1]{2,1,3,0:T(8,128)S(1)} fusion(f32[2,2,256,256]{3,2,1,0:T(8,128)S(1)} %fusion.7, f32[256,256]{1,0:T(8,128)S(1)} %fusion.28), kind=kOutput, calls=%fused_computation.11 | convolution fusion | flops 402915328 | bytes 1835008 | tf_op jit(solution)/shard_map/dot_general | solution.py:82
  37.7 1.1 %fusion.42 = f32[2,2,256,256]{3,2,1,0:T(8,128)S(1)} fusion(f32[2,2,256,256]{3,2,1,0:T(8,128)S(1)} %fusion.7, f32[2,256,256,1]{2,1,3,0:T(8,128)S(1)} %fusion.4), kind=kOutput, calls=%fused_computation.87 | convolution fusion | flops 805306368 | bytes 2621440 | tf_op jit(solution)/shard_map/tkij,tjl->tkil/dot_general | solution.py:83
  38.8 0.7 %fusion.2 = f32[2,256,256,1]{2,1,3,0:T(8,128)S(1)} fusion(f32[2,2,256,256]{3,2,1,0:T(8,128)S(1)} %fusion.42, f32[256,256]{1,0:T(8,128)S(1)} %fusion.28), kind=kOutput, calls=%fused_computation.8 | convolution fusion | flops 402915328 | bytes 1835008 | tf_op jit(solution)/shard_map/dot_general | solution.py:82
  39.4 0.7 %fusion.9 = f32[2,256,256]{2,1,0:T(8,128)S(1)} fusion(f32[2,2,256,256]{3,2,1,0:T(8,128)S(1)} %fusion.42, f32[2,256,256,1]{2,1,3,0:T(8,128)S(1)} %fusion.2, f32[2]{0:T(128)S(1)} %sqrt.7), kind=kOutput, calls=%fused_computation.19 | convolution fusion | flops 402784256 | bytes 2097160 | tf_op jit(solution)/shard_map/slice | solution.py:84
  40.1 0.3 fusion.30
  40.4 0.0 copy-start
  40.4 1.4 %collective-permute-start.10 = (f32[128,256]{1,0:T(8,128)S(1)}, f32[128,256]{1,0:T(8,128)S(1)}, u32[]{:S(2)}, u32[]{:S(2)}) collective-permute-start(f32[128,256]{1,0:T(8,128)S(1)} %slice_select_fusion), channel_id=1, source_target_pairs={{16,0},{17,1},{18,2},{19,3},{20,4},{21,5},{22,6},{23,7},{24,8},{25... | collective-permute-start | bytes 393224 | tf_op jit(solution)/shard_map/ppermute | solution.py:94
  41.8 6.1 %collective-permute-done.10 = f32[128,256]{1,0:T(8,128)S(1)} collective-permute-done((f32[128,256]{1,0:T(8,128)S(1)}, f32[128,256]{1,0:T(8,128)S(1)}, u32[]{:S(2)}, u32[]{:S(2)}) %collective-permute-start.10) | collective-permute-done | bytes 131104 | tf_op jit(solution)/shard_map/ppermute | solution.py:94
  48.0 0.0 collective-permute-start.11
  48.0 1.3 %collective-permute-done.11 = f32[128,256]{1,0:T(8,128)S(1)} collective-permute-done((f32[128,256]{1,0:T(8,128)S(1)}, f32[128,256]{1,0:T(8,128)S(1)}, u32[]{:S(2)}, u32[]{:S(2)}) %collective-permute-start.11) | collective-permute-done | bytes 131104 | tf_op jit(solution)/shard_map/ppermute | solution.py:95
  49.3 0.3 fusion.16
  49.6 0.3 convolution_bitcast_fusion.1
  49.9 0.0 copy-start.1
  50.0 1.7 %fusion = bf16[2,1536,256]{2,1,0:T(8,128)(2,1)} fusion(bf16[2,1536,256]{2,1,0:T(8,128)(2,1)S(1)} %copy-done, f32[2,256,256]{2,1,0:T(8,128)S(1)} %pad_maximum_fusion.1), kind=kOutput, calls=%fused_computation.3 | convolution fusion | flops 403570688 | bytes 3670016 | tf_op jit(solution)/shard_map/trm,tmn->trn/dot_general | solution.py:152
  (19 shorter events, 0.3 us)
Async XLA Ops:
  3.4 1.7 %collective-permute-start = (f32[256,256]{1,0:T(8,128)S(1)}, f32[256,256]{1,0:T(8,128)S(1)}, u32[]{:S(2)}, u32[]{:S(2)}) collective-permute-start(f32[256,256]{1,0:T(8,128)S(1)} %select_bitcast_fusion), channel_id=1, source_target_pairs={{0,1},{1,0},{2,3},{3,2},{4,5},{5,4},{6,7},{7,6},{8,9},{9,8},{10,11... | collective-permute-start | bytes 786440 | tf_op jit(solution)/shard_map/ppermute | solution.py:48
  5.2 6.4 %collective-permute-start.1 = (f32[64,256]{1,0:T(8,128)S(1)}, f32[64,256]{1,0:T(8,128)S(1)}, u32[]{:S(2)}, u32[]{:S(2)}) collective-permute-start(f32[64,256]{1,0:T(8,128)S(1)} %get-tuple-element.2), channel_id=1, source_target_pairs={{0,2},{1,3},{2,4},{3,5},{4,6},{5,7},{6,0},{7,1},{8,10},{9,11},{10,... | collective-permute-start | bytes 196616 | tf_op jit(solution)/shard_map/ppermute | solution.py:55
  8.2 4.8 %collective-permute-start.3 = (f32[64,256]{1,0:T(8,128)S(1)}, f32[64,256]{1,0:T(8,128)S(1)}, u32[]{:S(2)}, u32[]{:S(2)}) collective-permute-start(f32[64,256]{1,0:T(8,128)S(1)} %get-tuple-element.3), channel_id=1, source_target_pairs={{0,6},{1,7},{2,0},{3,1},{4,2},{5,3},{6,4},{7,5},{8,14},{9,15},{10,... | collective-permute-start | bytes 196616 | tf_op jit(solution)/shard_map/ppermute | solution.py:55
  9.2 5.1 %collective-permute-start.2 = (f32[64,256]{1,0:T(8,128)S(1)}, f32[64,256]{1,0:T(8,128)S(1)}, u32[]{:S(2)}, u32[]{:S(2)}) collective-permute-start(f32[64,256]{1,0:T(8,128)S(1)} %get-tuple-element.4), channel_id=1, source_target_pairs={{0,4},{1,5},{2,6},{3,7},{4,0},{5,1},{6,2},{7,3},{8,12},{9,13},{10,... | collective-permute-start | bytes 196616 | tf_op jit(solution)/shard_map/ppermute | solution.py:55
  14.4 4.9 %collective-permute-start.4 = (f32[32,256]{1,0:T(8,128)S(1)}, f32[32,256]{1,0:T(8,128)S(1)}, u32[]{:S(2)}, u32[]{:S(2)}) collective-permute-start(f32[32,256]{1,0:T(8,128)S(1)} %slice_select_fusion.1), channel_id=1, source_target_pairs={{0,8},{1,9},{2,10},{3,11},{4,12},{5,13},{6,14},{7,15},{8,0},{9,1},... | collective-permute-start | bytes 98312 | tf_op jit(solution)/shard_map/ppermute | solution.py:48
  19.3 4.9 %collective-permute-start.5 = (f32[32,256]{1,0:T(8,128)S(1)}, f32[32,256]{1,0:T(8,128)S(1)}, u32[]{:S(2)}, u32[]{:S(2)}) collective-permute-start(f32[32,256]{1,0:T(8,128)S(1)} %select_add_fusion), channel_id=1, source_target_pairs={{0,8},{1,9},{2,10},{3,11},{4,12},{5,13},{6,14},{7,15},{8,0},{9,1},... | collective-permute-start | bytes 98312 | tf_op jit(solution)/shard_map/ppermute | solution.py:60
  24.2 4.3 %collective-permute-start.8 = (f32[64,256]{1,0:T(8,128)S(1)}, f32[64,256]{1,0:T(8,128)S(1)}, u32[]{:S(2)}, u32[]{:S(2)}) collective-permute-start(f32[64,256]{1,0:T(8,128)S(1)} %maximum_select_fusion.3), channel_id=1, source_target_pairs={{0,6},{1,7},{2,0},{3,1},{4,2},{5,3},{6,4},{7,5},{8,14},{9,15},{10,... | collective-permute-start | bytes 196616 | tf_op jit(solution)/shard_map/ppermute | solution.py:63
  25.3 4.3 %collective-permute-start.7 = (f32[64,256]{1,0:T(8,128)S(1)}, f32[64,256]{1,0:T(8,128)S(1)}, u32[]{:S(2)}, u32[]{:S(2)}) collective-permute-start(f32[64,256]{1,0:T(8,128)S(1)} %maximum_select_fusion.3), channel_id=1, source_target_pairs={{0,4},{1,5},{2,6},{3,7},{4,0},{5,1},{6,2},{7,3},{8,12},{9,13},{10,... | collective-permute-start | bytes 196616 | tf_op jit(solution)/shard_map/ppermute | solution.py:63
  26.4 5.2 %collective-permute-start.6 = (f32[64,256]{1,0:T(8,128)S(1)}, f32[64,256]{1,0:T(8,128)S(1)}, u32[]{:S(2)}, u32[]{:S(2)}) collective-permute-start(f32[64,256]{1,0:T(8,128)S(1)} %maximum_select_fusion.3), channel_id=1, source_target_pairs={{0,2},{1,3},{2,4},{3,5},{4,6},{5,7},{6,0},{7,1},{8,10},{9,11},{10,... | collective-permute-start | bytes 196616 | tf_op jit(solution)/shard_map/ppermute | solution.py:63
  32.3 1.6 %collective-permute-start.9 = (f32[256,256]{1,0:T(8,128)S(1)}, f32[256,256]{1,0:T(8,128)S(1)}, u32[]{:S(2)}, u32[]{:S(2)}) collective-permute-start(f32[256,256]{1,0:T(8,128)S(1)} %bitcast_select_fusion), channel_id=1, source_target_pairs={{0,1},{1,0},{2,3},{3,2},{4,5},{5,4},{6,7},{7,6},{8,9},{9,8},{10,11... | collective-permute-start | bytes 786440 | tf_op jit(solution)/shard_map/ppermute | solution.py:60
  40.4 9.6 %copy-start = (bf16[2,1536,256]{2,1,0:T(8,128)(2,1)S(1)}, bf16[2,1536,256]{2,1,0:T(8,128)(2,1)}, u32[]{:S(2)}) copy-start(bf16[2,1536,256]{2,1,0:T(8,128)(2,1)} %param.2) | copy-start | bytes 4718596
  40.4 7.6 %collective-permute-start.10 = (f32[128,256]{1,0:T(8,128)S(1)}, f32[128,256]{1,0:T(8,128)S(1)}, u32[]{:S(2)}, u32[]{:S(2)}) collective-permute-start(f32[128,256]{1,0:T(8,128)S(1)} %slice_select_fusion), channel_id=1, source_target_pairs={{16,0},{17,1},{18,2},{19,3},{20,4},{21,5},{22,6},{23,7},{24,8},{25... | collective-permute-start | bytes 393224 | tf_op jit(solution)/shard_map/ppermute | solution.py:94
  48.0 1.3 %collective-permute-start.11 = (f32[128,256]{1,0:T(8,128)S(1)}, f32[128,256]{1,0:T(8,128)S(1)}, u32[]{:S(2)}, u32[]{:S(2)}) collective-permute-start(f32[128,256]{1,0:T(8,128)S(1)} %collective-permute-done.10), channel_id=1, source_target_pairs={{0,1},{1,0},{2,3},{3,2},{4,5},{5,4},{6,7},{7,6},{8,9},{9,8},{10,11... | collective-permute-start | bytes 393224 | tf_op jit(solution)/shard_map/ppermute | solution.py:95
  49.9 1.7 %copy-start.1 = (f32[2,256,256]{2,1,0:T(8,128)}, f32[2,256,256]{2,1,0:T(8,128)S(1)}, u32[]{:S(2)}) copy-start(f32[2,256,256]{2,1,0:T(8,128)S(1)} %pad_maximum_fusion.1) | copy-start | bytes 1572868

commit v8 on v6

--- a/solution.py
+++ b/solution.py
@@ -79,8 +79,9 @@
     factor = 1.5 * identity - 0.5 * iterate
     pair = jnp.stack([jnp.matmul(iterate, factor, precision=NS_PRECISION), factor], axis=1)
     for sweep_index in range(NS_STEPS - 1):
-        factor = 1.5 * identity - 0.5 * jnp.matmul(pair[:, 1], pair[:, 0], precision=NS_PRECISION)
-        pair = jnp.einsum("tkij,tjl->tkil", pair, factor, precision=NS_PRECISION)
+        precision = lax.Precision.HIGHEST if sweep_index == NS_STEPS - 2 else NS_PRECISION
+        factor = 1.5 * identity - 0.5 * jnp.matmul(pair[:, 1], pair[:, 0], precision=precision)
+        pair = jnp.einsum("tkij,tjl->tkil", pair, factor, precision=precision)
     return pair[:, 1] / jnp.sqrt(row_bound)[:, None, None]
 
 

time: 49.5 us -> 50.1 us (1.012)
  matrix products: 6.74 us -> 7.27 us
where the time goes in v8:
time: 50.1 us; the launch traced here: 49.9 us
  waiting for transfers between devices  22 us (44%)
  starting transfers between devices  16.2 us (32%)
  matrix products  7.27 us (15%)
  other arithmetic  2.72 us (5%)
  between operations  0.9 us (2%)
  local copies, waits for them, and re-layouts  0.77 us (2%)
    ppermute x1, waiting for transfers between devices, split_shift(): got = lax.ppermute(part, axis, pairs)  6.13 us
    ppermute x3, starting transfers between devices, grouped_sum(): lax.ppermute(send, axis, digit_pairs(count, radix, place, offset))  5.92 us
    ppermute x3, waiting for transfers between devices, grouped_sum(): lax.ppermute(value, axis, digit_pairs(count, radix, place, offset))  4.34 us
    ppermute x2, waiting for transfers between devices, grouped_sum(): other = lax.ppermute(value, axis, digit_pairs(count, radix, place, 1))  3.61 us
    ppermute x2, waiting for transfers between devices, grouped_sum(): value = keep + lax.ppermute(send, axis, digit_pairs(count, radix, place, 1))  3.38 us
    ppermute x3, waiting for transfers between devices, grouped_sum(): lax.ppermute(send, axis, digit_pairs(count, radix, place, offset))  3.22 us
    ppermute x2, starting transfers between devices, grouped_sum(): value = keep + lax.ppermute(send, axis, digit_pairs(count, radix, place, 1))  3.17 us
    ppermute x3, starting transfers between devices, grouped_sum(): lax.ppermute(value, axis, digit_pairs(count, radix, place, offset))  3.01 us
  transfers between devices with their start and end apart: 12, of which 12 were waited for; matrix products, arithmetic and copies ran while one was open for 0% of the time, Pallas kernels for 0%

profile of v8, /device:TPU:0, one launch (start us, length us, event | category | flops | bytes accessed | tf_op | source)
XLA Modules:
  0.0 49.9 jit_solution(4584187263114736812)
XLA Ops:
  0.6 1.9 %multiply_convert_fusion = bf16[2,1536,256]{2,1,0:T(8,128)(2,1)S(1)} fusion(bf16[2,1536,256]{2,1,0:T(8,128)(2,1)} %param.2, f32[2,1536]{1,0:T(2,128)} %param.3), kind=kLoop, calls=%fused_computation.1 | loop fusion | flops 2359296 | bytes 3158016 | tf_op jit(solution)/shard_map/convert_element_type | solution.py:135
  2.5 0.4 fusion.11
  3.0 0.4 convolution_add_fusion
  3.4 0.5 %collective-permute-start = (f32[256,256]{1,0:T(8,128)S(1)}, f32[256,256]{1,0:T(8,128)S(1)}, u32[]{:S(2)}, u32[]{:S(2)}) collective-permute-start(f32[256,256]{1,0:T(8,128)S(1)} %select_bitcast_fusion), channel_id=1, source_target_pairs={{0,1},{1,0},{2,3},{3,2},{4,5},{5,4},{6,7},{7,6},{8,9},{9,8},{10,11... | collective-permute-start | bytes 786440 | tf_op jit(solution)/shard_map/ppermute | solution.py:48
  4.0 1.2 %collective-permute-done = f32[256,256]{1,0:T(8,128)S(1)} collective-permute-done((f32[256,256]{1,0:T(8,128)S(1)}, f32[256,256]{1,0:T(8,128)S(1)}, u32[]{:S(2)}, u32[]{:S(2)}) %collective-permute-start) | collective-permute-done | bytes 262176 | tf_op jit(solution)/shard_map/ppermute | solution.py:48
  5.2 2.9 %collective-permute-start.1 = (f32[64,256]{1,0:T(8,128)S(1)}, f32[64,256]{1,0:T(8,128)S(1)}, u32[]{:S(2)}, u32[]{:S(2)}) collective-permute-start(f32[64,256]{1,0:T(8,128)S(1)} %get-tuple-element.2), channel_id=1, source_target_pairs={{0,2},{1,3},{2,4},{3,5},{4,6},{5,7},{6,0},{7,1},{8,10},{9,11},{10,... | collective-permute-start | bytes 196616 | tf_op jit(solution)/shard_map/ppermute | solution.py:55
  8.2 1.1 %collective-permute-start.3 = (f32[64,256]{1,0:T(8,128)S(1)}, f32[64,256]{1,0:T(8,128)S(1)}, u32[]{:S(2)}, u32[]{:S(2)}) collective-permute-start(f32[64,256]{1,0:T(8,128)S(1)} %get-tuple-element.3), channel_id=1, source_target_pairs={{0,6},{1,7},{2,0},{3,1},{4,2},{5,3},{6,4},{7,5},{8,14},{9,15},{10,... | collective-permute-start | bytes 196616 | tf_op jit(solution)/shard_map/ppermute | solution.py:55
  9.2 1.9 %collective-permute-start.2 = (f32[64,256]{1,0:T(8,128)S(1)}, f32[64,256]{1,0:T(8,128)S(1)}, u32[]{:S(2)}, u32[]{:S(2)}) collective-permute-start(f32[64,256]{1,0:T(8,128)S(1)} %get-tuple-element.4), channel_id=1, source_target_pairs={{0,4},{1,5},{2,6},{3,7},{4,0},{5,1},{6,2},{7,3},{8,12},{9,13},{10,... | collective-permute-start | bytes 196616 | tf_op jit(solution)/shard_map/ppermute | solution.py:55
  11.1 0.5 %collective-permute-done.1 = f32[64,256]{1,0:T(8,128)S(1)} collective-permute-done((f32[64,256]{1,0:T(8,128)S(1)}, f32[64,256]{1,0:T(8,128)S(1)}, u32[]{:S(2)}, u32[]{:S(2)}) %collective-permute-start.1) | collective-permute-done | bytes 65568 | tf_op jit(solution)/shard_map/ppermute | solution.py:55
  11.7 1.3 %collective-permute-done.3 = f32[64,256]{1,0:T(8,128)S(1)} collective-permute-done((f32[64,256]{1,0:T(8,128)S(1)}, f32[64,256]{1,0:T(8,128)S(1)}, u32[]{:S(2)}, u32[]{:S(2)}) %collective-permute-start.3) | collective-permute-done | bytes 65568 | tf_op jit(solution)/shard_map/ppermute | solution.py:55
  13.0 1.4 %collective-permute-done.2 = f32[64,256]{1,0:T(8,128)S(1)} collective-permute-done((f32[64,256]{1,0:T(8,128)S(1)}, f32[64,256]{1,0:T(8,128)S(1)}, u32[]{:S(2)}, u32[]{:S(2)}) %collective-permute-start.2) | collective-permute-done | bytes 65568 | tf_op jit(solution)/shard_map/ppermute | solution.py:55
  14.4 2.7 %collective-permute-start.4 = (f32[32,256]{1,0:T(8,128)S(1)}, f32[32,256]{1,0:T(8,128)S(1)}, u32[]{:S(2)}, u32[]{:S(2)}) collective-permute-start(f32[32,256]{1,0:T(8,128)S(1)} %slice_select_fusion.1), channel_id=1, source_target_pairs={{0,8},{1,9},{2,10},{3,11},{4,12},{5,13},{6,14},{7,15},{8,0},{9,1},... | collective-permute-start | bytes 98312 | tf_op jit(solution)/shard_map/ppermute | solution.py:48
  17.1 2.2 %collective-permute-done.4 = f32[32,256]{1,0:T(8,128)S(1)} collective-permute-done((f32[32,256]{1,0:T(8,128)S(1)}, f32[32,256]{1,0:T(8,128)S(1)}, u32[]{:S(2)}, u32[]{:S(2)}) %collective-permute-start.4) | collective-permute-done | bytes 32800 | tf_op jit(solution)/shard_map/ppermute | solution.py:48
  19.3 2.6 %collective-permute-start.5 = (f32[32,256]{1,0:T(8,128)S(1)}, f32[32,256]{1,0:T(8,128)S(1)}, u32[]{:S(2)}, u32[]{:S(2)}) collective-permute-start(f32[32,256]{1,0:T(8,128)S(1)} %select_add_fusion), channel_id=1, source_target_pairs={{0,8},{1,9},{2,10},{3,11},{4,12},{5,13},{6,14},{7,15},{8,0},{9,1},... | collective-permute-start | bytes 98312 | tf_op jit(solution)/shard_map/ppermute | solution.py:60
  21.9 0.1 broadcast_in_dim.22
  22.0 0.1 broadcast_in_dim.23
  22.1 2.1 %collective-permute-done.5 = f32[32,256]{1,0:T(8,128)S(1)} collective-permute-done((f32[32,256]{1,0:T(8,128)S(1)}, f32[32,256]{1,0:T(8,128)S(1)}, u32[]{:S(2)}, u32[]{:S(2)}) %collective-permute-start.5) | collective-permute-done | bytes 32800 | tf_op jit(solution)/shard_map/ppermute | solution.py:60
  24.2 1.1 %collective-permute-start.8 = (f32[64,256]{1,0:T(8,128)S(1)}, f32[64,256]{1,0:T(8,128)S(1)}, u32[]{:S(2)}, u32[]{:S(2)}) collective-permute-start(f32[64,256]{1,0:T(8,128)S(1)} %maximum_select_fusion.3), channel_id=1, source_target_pairs={{0,6},{1,7},{2,0},{3,1},{4,2},{5,3},{6,4},{7,5},{8,14},{9,15},{10,... | collective-permute-start | bytes 196616 | tf_op jit(solution)/shard_map/ppermute | solution.py:63
  25.3 1.1 %collective-permute-start.7 = (f32[64,256]{1,0:T(8,128)S(1)}, f32[64,256]{1,0:T(8,128)S(1)}, u32[]{:S(2)}, u32[]{:S(2)}) collective-permute-start(f32[64,256]{1,0:T(8,128)S(1)} %maximum_select_fusion.3), channel_id=1, source_target_pairs={{0,4},{1,5},{2,6},{3,7},{4,0},{5,1},{6,2},{7,3},{8,12},{9,13},{10,... | collective-permute-start | bytes 196616 | tf_op jit(solution)/shard_map/ppermute | solution.py:63
  26.4 0.8 %collective-permute-start.6 = (f32[64,256]{1,0:T(8,128)S(1)}, f32[64,256]{1,0:T(8,128)S(1)}, u32[]{:S(2)}, u32[]{:S(2)}) collective-permute-start(f32[64,256]{1,0:T(8,128)S(1)} %maximum_select_fusion.3), channel_id=1, source_target_pairs={{0,2},{1,3},{2,4},{3,5},{4,6},{5,7},{6,0},{7,1},{8,10},{9,11},{10,... | collective-permute-start | bytes 196616 | tf_op jit(solution)/shard_map/ppermute | solution.py:63
  27.2 1.3 %collective-permute-done.8 = f32[64,256]{1,0:T(8,128)S(1)} collective-permute-done((f32[64,256]{1,0:T(8,128)S(1)}, f32[64,256]{1,0:T(8,128)S(1)}, u32[]{:S(2)}, u32[]{:S(2)}) %collective-permute-start.8) | collective-permute-done | bytes 65568 | tf_op jit(solution)/shard_map/ppermute | solution.py:63
  28.5 1.0 %collective-permute-done.7 = f32[64,256]{1,0:T(8,128)S(1)} collective-permute-done((f32[64,256]{1,0:T(8,128)S(1)}, f32[64,256]{1,0:T(8,128)S(1)}, u32[]{:S(2)}, u32[]{:S(2)}) %collective-permute-start.7) | collective-permute-done | bytes 65568 | tf_op jit(solution)/shard_map/ppermute | solution.py:63
  29.6 2.0 %collective-permute-done.6 = f32[64,256]{1,0:T(8,128)S(1)} collective-permute-done((f32[64,256]{1,0:T(8,128)S(1)}, f32[64,256]{1,0:T(8,128)S(1)}, u32[]{:S(2)}, u32[]{:S(2)}) %collective-permute-start.6) | collective-permute-done | bytes 65568 | tf_op jit(solution)/shard_map/ppermute | solution.py:63
  31.6 0.6 %gather_fusion = f32[4,64,256]{2,1,0:T(8,128)S(1)} fusion(f32[4,64,256]{2,1,0:T(8,128)S(1)} %pad_maximum_fusion.2, s32[1024]{0:T(1024)S(1)} %pad_clamp_fusion), kind=kCustom, calls=%fused_computation | custom fusion | bytes 524304 | tf_op jit(solution)/shard_map/jit(_take)/gather | solution.py:66
  32.2 0.1 bitcast_select_fusion
  32.3 0.1 collective-permute-start.9
  32.4 1.5 %collective-permute-done.9 = f32[256,256]{1,0:T(8,128)S(1)} collective-permute-done((f32[256,256]{1,0:T(8,128)S(1)}, f32[256,256]{1,0:T(8,128)S(1)}, u32[]{:S(2)}, u32[]{:S(2)}) %collective-permute-start.9) | collective-permute-done | bytes 262176 | tf_op jit(solution)/shard_map/ppermute | solution.py:60
  33.9 0.1 fusion.13
  33.9 0.2 abs_reduce_fusion
  34.1 0.1 reduce_max.9
  34.2 0.5 %fusion.14 = f32[2,256,256]{2,1,0:T(8,128)S(1)} fusion(f32[256,256]{1,0:T(8,128)S(1)} %fusion.28, f32[2]{0:T(128)S(1)} %reduce_max.9, f32[256,256]{1,0:T(8,128)S(1)} %fusion.29, f32[512,256]{1,0:T(8,128)S(1)} %fusion.13), kind=kOutput, calls=%fused_computation.32 | convolution fusion | flops 202113024 | bytes 1572872 | tf_op jit(solution)/shard_map/dot_general | solution.py:80
  34.8 0.5 fusion.6
  35.2 0.1 multiply_subtract_fusion
  35.4 0.6 %fusion.7 = f32[2,2,256,256]{3,2,1,0:T(8,128)S(1)} fusion(f32[2,256,256,1]{2,1,3,0:T(8,128)S(1)} %fusion.6, f32[2,1,256,256]{3,2,0,1:T(8,128)S(1)} %multiply_subtract_fusion, f32[2,1,256,256]{3,2,0,1:T(8,128)S(1)} %bitcast.90), kind=kOutput, calls=%fused_computation.17 | convolution fusion | flops 402915328 | bytes 2621440 | tf_op jit(solution)/shard_map/tkij,tjl->tkil/dot_general | solution.py:84
  36.0 0.4 fusion.4
  36.4 0.6 %fusion.42 = f32[2,2,256,256]{3,2,1,0:T(8,128)S(1)} fusion(f32[2,2,256,256]{3,2,1,0:T(8,128)S(1)} %fusion.7, f32[2,256,256,1]{2,1,3,0:T(8,128)S(1)} %fusion.4), kind=kOutput, calls=%fused_computation.87 | convolution fusion | flops 402653184 | bytes 2621440 | tf_op jit(solution)/shard_map/tkij,tjl->tkil/dot_general | solution.py:84
  37.0 0.7 %fusion.2 = f32[2,256,256,1]{2,1,3,0:T(8,128)S(1)} fusion(f32[2,2,256,256]{3,2,1,0:T(8,128)S(1)} %fusion.42, f32[256,256]{1,0:T(8,128)S(1)} %fusion.28), kind=kOutput, calls=%fused_computation.8 | convolution fusion | flops 402915328 | bytes 1835008 | tf_op jit(solution)/shard_map/dot_general | solution.py:83
  37.6 0.7 %fusion.9 = f32[2,256,256]{2,1,0:T(8,128)S(1)} fusion(f32[2,2,256,256]{3,2,1,0:T(8,128)S(1)} %fusion.42, f32[2,256,256,1]{2,1,3,0:T(8,128)S(1)} %fusion.2, f32[2]{0:T(128)S(1)} %sqrt.7), kind=kOutput, calls=%fused_computation.19 | convolution fusion | flops 402784256 | bytes 2097160 | tf_op jit(solution)/shard_map/slice | solution.py:85
  38.3 0.3 fusion.30
  38.6 0.0 copy-start
  38.6 1.4 %collective-permute-start.10 = (f32[128,256]{1,0:T(8,128)S(1)}, f32[128,256]{1,0:T(8,128)S(1)}, u32[]{:S(2)}, u32[]{:S(2)}) collective-permute-start(f32[128,256]{1,0:T(8,128)S(1)} %slice_select_fusion), channel_id=1, source_target_pairs={{16,0},{17,1},{18,2},{19,3},{20,4},{21,5},{22,6},{23,7},{24,8},{25... | collective-permute-start | bytes 393224 | tf_op jit(solution)/shard_map/ppermute | solution.py:95
  40.0 6.1 %collective-permute-done.10 = f32[128,256]{1,0:T(8,128)S(1)} collective-permute-done((f32[128,256]{1,0:T(8,128)S(1)}, f32[128,256]{1,0:T(8,128)S(1)}, u32[]{:S(2)}, u32[]{:S(2)}) %collective-permute-start.10) | collective-permute-done | bytes 131104 | tf_op jit(solution)/shard_map/ppermute | solution.py:95
  46.2 0.0 collective-permute-start.11
  46.2 1.3 %collective-permute-done.11 = f32[128,256]{1,0:T(8,128)S(1)} collective-permute-done((f32[128,256]{1,0:T(8,128)S(1)}, f32[128,256]{1,0:T(8,128)S(1)}, u32[]{:S(2)}, u32[]{:S(2)}) %collective-permute-start.11) | collective-permute-done | bytes 131104 | tf_op jit(solution)/shard_map/ppermute | solution.py:96
  47.5 0.3 fusion.16
  47.8 0.3 convolution_bitcast_fusion.1
  48.2 0.0 copy-start.1
  48.2 1.7 %fusion = bf16[2,1536,256]{2,1,0:T(8,128)(2,1)} fusion(bf16[2,1536,256]{2,1,0:T(8,128)(2,1)S(1)} %copy-done, f32[2,256,256]{2,1,0:T(8,128)S(1)} %pad_maximum_fusion.1), kind=kOutput, calls=%fused_computation.3 | convolution fusion | flops 403570688 | bytes 3670016 | tf_op jit(solution)/shard_map/trm,tmn->trn/dot_general | solution.py:153
  (19 shorter events, 0.3 us)
Async XLA Ops:
  3.4 1.7 %collective-permute-start = (f32[256,256]{1,0:T(8,128)S(1)}, f32[256,256]{1,0:T(8,128)S(1)}, u32[]{:S(2)}, u32[]{:S(2)}) collective-permute-start(f32[256,256]{1,0:T(8,128)S(1)} %select_bitcast_fusion), channel_id=1, source_target_pairs={{0,1},{1,0},{2,3},{3,2},{4,5},{5,4},{6,7},{7,6},{8,9},{9,8},{10,11... | collective-permute-start | bytes 786440 | tf_op jit(solution)/shard_map/ppermute | solution.py:48
  5.2 6.4 %collective-permute-start.1 = (f32[64,256]{1,0:T(8,128)S(1)}, f32[64,256]{1,0:T(8,128)S(1)}, u32[]{:S(2)}, u32[]{:S(2)}) collective-permute-start(f32[64,256]{1,0:T(8,128)S(1)} %get-tuple-element.2), channel_id=1, source_target_pairs={{0,2},{1,3},{2,4},{3,5},{4,6},{5,7},{6,0},{7,1},{8,10},{9,11},{10,... | collective-permute-start | bytes 196616 | tf_op jit(solution)/shard_map/ppermute | solution.py:55
  8.2 4.8 %collective-permute-start.3 = (f32[64,256]{1,0:T(8,128)S(1)}, f32[64,256]{1,0:T(8,128)S(1)}, u32[]{:S(2)}, u32[]{:S(2)}) collective-permute-start(f32[64,256]{1,0:T(8,128)S(1)} %get-tuple-element.3), channel_id=1, source_target_pairs={{0,6},{1,7},{2,0},{3,1},{4,2},{5,3},{6,4},{7,5},{8,14},{9,15},{10,... | collective-permute-start | bytes 196616 | tf_op jit(solution)/shard_map/ppermute | solution.py:55
  9.2 5.1 %collective-permute-start.2 = (f32[64,256]{1,0:T(8,128)S(1)}, f32[64,256]{1,0:T(8,128)S(1)}, u32[]{:S(2)}, u32[]{:S(2)}) collective-permute-start(f32[64,256]{1,0:T(8,128)S(1)} %get-tuple-element.4), channel_id=1, source_target_pairs={{0,4},{1,5},{2,6},{3,7},{4,0},{5,1},{6,2},{7,3},{8,12},{9,13},{10,... | collective-permute-start | bytes 196616 | tf_op jit(solution)/shard_map/ppermute | solution.py:55
  14.4 4.9 %collective-permute-start.4 = (f32[32,256]{1,0:T(8,128)S(1)}, f32[32,256]{1,0:T(8,128)S(1)}, u32[]{:S(2)}, u32[]{:S(2)}) collective-permute-start(f32[32,256]{1,0:T(8,128)S(1)} %slice_select_fusion.1), channel_id=1, source_target_pairs={{0,8},{1,9},{2,10},{3,11},{4,12},{5,13},{6,14},{7,15},{8,0},{9,1},... | collective-permute-start | bytes 98312 | tf_op jit(solution)/shard_map/ppermute | solution.py:48
  19.3 4.9 %collective-permute-start.5 = (f32[32,256]{1,0:T(8,128)S(1)}, f32[32,256]{1,0:T(8,128)S(1)}, u32[]{:S(2)}, u32[]{:S(2)}) collective-permute-start(f32[32,256]{1,0:T(8,128)S(1)} %select_add_fusion), channel_id=1, source_target_pairs={{0,8},{1,9},{2,10},{3,11},{4,12},{5,13},{6,14},{7,15},{8,0},{9,1},... | collective-permute-start | bytes 98312 | tf_op jit(solution)/shard_map/ppermute | solution.py:60
  24.2 4.3 %collective-permute-start.8 = (f32[64,256]{1,0:T(8,128)S(1)}, f32[64,256]{1,0:T(8,128)S(1)}, u32[]{:S(2)}, u32[]{:S(2)}) collective-permute-start(f32[64,256]{1,0:T(8,128)S(1)} %maximum_select_fusion.3), channel_id=1, source_target_pairs={{0,6},{1,7},{2,0},{3,1},{4,2},{5,3},{6,4},{7,5},{8,14},{9,15},{10,... | collective-permute-start | bytes 196616 | tf_op jit(solution)/shard_map/ppermute | solution.py:63
  25.3 4.3 %collective-permute-start.7 = (f32[64,256]{1,0:T(8,128)S(1)}, f32[64,256]{1,0:T(8,128)S(1)}, u32[]{:S(2)}, u32[]{:S(2)}) collective-permute-start(f32[64,256]{1,0:T(8,128)S(1)} %maximum_select_fusion.3), channel_id=1, source_target_pairs={{0,4},{1,5},{2,6},{3,7},{4,0},{5,1},{6,2},{7,3},{8,12},{9,13},{10,... | collective-permute-start | bytes 196616 | tf_op jit(solution)/shard_map/ppermute | solution.py:63
  26.4 5.2 %collective-permute-start.6 = (f32[64,256]{1,0:T(8,128)S(1)}, f32[64,256]{1,0:T(8,128)S(1)}, u32[]{:S(2)}, u32[]{:S(2)}) collective-permute-start(f32[64,256]{1,0:T(8,128)S(1)} %maximum_select_fusion.3), channel_id=1, source_target_pairs={{0,2},{1,3},{2,4},{3,5},{4,6},{5,7},{6,0},{7,1},{8,10},{9,11},{10,... | collective-permute-start | bytes 196616 | tf_op jit(solution)/shard_map/ppermute | solution.py:63
  32.3 1.6 %collective-permute-start.9 = (f32[256,256]{1,0:T(8,128)S(1)}, f32[256,256]{1,0:T(8,128)S(1)}, u32[]{:S(2)}, u32[]{:S(2)}) collective-permute-start(f32[256,256]{1,0:T(8,128)S(1)} %bitcast_select_fusion), channel_id=1, source_target_pairs={{0,1},{1,0},{2,3},{3,2},{4,5},{5,4},{6,7},{7,6},{8,9},{9,8},{10,11... | collective-permute-start | bytes 786440 | tf_op jit(solution)/shard_map/ppermute | solution.py:60
  38.6 9.6 %copy-start = (bf16[2,1536,256]{2,1,0:T(8,128)(2,1)S(1)}, bf16[2,1536,256]{2,1,0:T(8,128)(2,1)}, u32[]{:S(2)}) copy-start(bf16[2,1536,256]{2,1,0:T(8,128)(2,1)} %param.2) | copy-start | bytes 4718596
  38.6 7.6 %collective-permute-start.10 = (f32[128,256]{1,0:T(8,128)S(1)}, f32[128,256]{1,0:T(8,128)S(1)}, u32[]{:S(2)}, u32[]{:S(2)}) collective-permute-start(f32[128,256]{1,0:T(8,128)S(1)} %slice_select_fusion), channel_id=1, source_target_pairs={{16,0},{17,1},{18,2},{19,3},{20,4},{21,5},{22,6},{23,7},{24,8},{25... | collective-permute-start | bytes 393224 | tf_op jit(solution)/shard_map/ppermute | solution.py:95
  46.2 1.3 %collective-permute-start.11 = (f32[128,256]{1,0:T(8,128)S(1)}, f32[128,256]{1,0:T(8,128)S(1)}, u32[]{:S(2)}, u32[]{:S(2)}) collective-permute-start(f32[128,256]{1,0:T(8,128)S(1)} %collective-permute-done.10), channel_id=1, source_target_pairs={{0,1},{1,0},{2,3},{3,2},{4,5},{5,4},{6,7},{7,6},{8,9},{9,8},{10,11... | collective-permute-start | bytes 393224 | tf_op jit(solution)/shard_map/ppermute | solution.py:96
  48.2 1.7 %copy-start.1 = (f32[2,256,256]{2,1,0:T(8,128)}, f32[2,256,256]{2,1,0:T(8,128)S(1)}, u32[]{:S(2)}) copy-start(f32[2,256,256]{2,1,0:T(8,128)S(1)} %pad_maximum_fusion.1) | copy-start | bytes 1572868

commit v9 on v6

--- a/solution.py
+++ b/solution.py
@@ -61,9 +61,14 @@
             value = jnp.where(digit == 1, jnp.concatenate([other, value]), jnp.concatenate([value, other]))
             continue
         got = [value] + [lax.ppermute(value, axis, digit_pairs(count, radix, place, offset)) for offset in range(1, radix)]
-        stacked = jnp.stack(got)
-        order = (digit - jnp.arange(radix)) % radix
-        value = jnp.take(stacked, order, axis=0).reshape((radix * value.shape[0],) + value.shape[1:])
+        placed = []
+        for k in range(radix):
+            source = (digit - k) % radix
+            piece = got[0]
+            for offset in range(1, radix):
+                piece = jnp.where(source == offset, got[offset], piece)
+            placed.append(piece)
+        value = jnp.concatenate(placed)
     return value
 
 

time: 49.5 us -> 48 us (0.970)
  waiting for transfers between devices: 22 us -> 19.9 us
  starting transfers between devices: 16.2 us -> 17.1 us
  local copies, waits for them, and re-layouts: 0.77 us -> 0.11 us
    ppermute x3, waiting for transfers between devices: 4.34 us -> 2.01 us  [grouped_sum(): lax.ppermute(value, axis, digit_pairs(count, radix, place, offset))]
    ppermute x3, starting transfers between devices: 3.01 us -> 3.9 us  [grouped_sum(): lax.ppermute(value, axis, digit_pairs(count, radix, place, offset))]
    gather x1 -> x0, local copies, waits for them, and re-layouts: 0.57 us -> none  [grouped_sum(): jnp.take(stacked, order, axis=0)]
  transfers between devices with their start and end apart: 12 -> 12, of which waited for: 12 -> 11; matrix products, arithmetic and copies ran while one was open for 0% -> 0% of each run, Pallas kernels for 0% -> 0%
where the time goes in v9:
time: 48 us; the launch traced here: 47.5 us
  waiting for transfers between devices  19.9 us (41%)
  starting transfers between devices  17.1 us (36%)
  matrix products  6.74 us (14%)
  other arithmetic  2.68 us (6%)
  between operations  0.96 us (2%)
    ppermute x1, waiting for transfers between devices, split_shift(): got = lax.ppermute(part, axis, pairs)  6.13 us
    ppermute x3, starting transfers between devices, grouped_sum(): lax.ppermute(send, axis, digit_pairs(count, radix, place, offset))  5.92 us
    ppermute x3, starting transfers between devices, grouped_sum(): lax.ppermute(value, axis, digit_pairs(count, radix, place, offset))  3.9 us
    ppermute x2, waiting for transfers between devices, grouped_sum(): other = lax.ppermute(value, axis, digit_pairs(count, radix, place, 1))  3.8 us
    ppermute x2, waiting for transfers between devices, grouped_sum(): value = keep + lax.ppermute(send, axis, digit_pairs(count, radix, place, 1))  3.38 us
    ppermute x3, waiting for transfers between devices, grouped_sum(): lax.ppermute(send, axis, digit_pairs(count, radix, place, offset))  3.23 us
    ppermute x2, starting transfers between devices, grouped_sum(): value = keep + lax.ppermute(send, axis, digit_pairs(count, radix, place, 1))  3.17 us
    ppermute x2, starting transfers between devices, grouped_sum(): other = lax.ppermute(value, axis, digit_pairs(count, radix, place, 1))  2.66 us
  transfers between devices with their start and end apart: 12, of which 11 were waited for; matrix products, arithmetic and copies ran while one was open for 0% of the time, Pallas kernels for 0%

profile of v9, /device:TPU:0, one launch (start us, length us, event | category | flops | bytes accessed | tf_op | source)
XLA Modules:
  0.0 47.5 jit_solution(17584136525816370989)
XLA Ops:
  0.6 1.9 %multiply_convert_fusion = bf16[2,1536,256]{2,1,0:T(8,128)(2,1)S(1)} fusion(bf16[2,1536,256]{2,1,0:T(8,128)(2,1)} %param.2, f32[2,1536]{1,0:T(2,128)} %param.3), kind=kLoop, calls=%fused_computation | loop fusion | flops 2359296 | bytes 3158016 | tf_op jit(solution)/shard_map/convert_element_type | solution.py:139
  2.5 0.4 fusion.11
  3.0 0.4 convolution_add_fusion
  3.4 0.5 %collective-permute-start = (f32[256,256]{1,0:T(8,128)S(1)}, f32[256,256]{1,0:T(8,128)S(1)}, u32[]{:S(2)}, u32[]{:S(2)}) collective-permute-start(f32[256,256]{1,0:T(8,128)S(1)} %select_bitcast_fusion), channel_id=1, source_target_pairs={{0,1},{1,0},{2,3},{3,2},{4,5},{5,4},{6,7},{7,6},{8,9},{9,8},{10,11... | collective-permute-start | bytes 786440 | tf_op jit(solution)/shard_map/ppermute | solution.py:48
  4.0 1.2 %collective-permute-done = f32[256,256]{1,0:T(8,128)S(1)} collective-permute-done((f32[256,256]{1,0:T(8,128)S(1)}, f32[256,256]{1,0:T(8,128)S(1)}, u32[]{:S(2)}, u32[]{:S(2)}) %collective-permute-start) | collective-permute-done | bytes 262176 | tf_op jit(solution)/shard_map/ppermute | solution.py:48
  5.2 2.9 %collective-permute-start.1 = (f32[64,256]{1,0:T(8,128)S(1)}, f32[64,256]{1,0:T(8,128)S(1)}, u32[]{:S(2)}, u32[]{:S(2)}) collective-permute-start(f32[64,256]{1,0:T(8,128)S(1)} %get-tuple-element.12), channel_id=1, source_target_pairs={{0,2},{1,3},{2,4},{3,5},{4,6},{5,7},{6,0},{7,1},{8,10},{9,11},{10,... | collective-permute-start | bytes 196616 | tf_op jit(solution)/shard_map/ppermute | solution.py:55
  8.2 1.1 %collective-permute-start.3 = (f32[64,256]{1,0:T(8,128)S(1)}, f32[64,256]{1,0:T(8,128)S(1)}, u32[]{:S(2)}, u32[]{:S(2)}) collective-permute-start(f32[64,256]{1,0:T(8,128)S(1)} %get-tuple-element.13), channel_id=1, source_target_pairs={{0,6},{1,7},{2,0},{3,1},{4,2},{5,3},{6,4},{7,5},{8,14},{9,15},{10,... | collective-permute-start | bytes 196616 | tf_op jit(solution)/shard_map/ppermute | solution.py:55
  9.2 1.9 %collective-permute-start.2 = (f32[64,256]{1,0:T(8,128)S(1)}, f32[64,256]{1,0:T(8,128)S(1)}, u32[]{:S(2)}, u32[]{:S(2)}) collective-permute-start(f32[64,256]{1,0:T(8,128)S(1)} %get-tuple-element.14), channel_id=1, source_target_pairs={{0,4},{1,5},{2,6},{3,7},{4,0},{5,1},{6,2},{7,3},{8,12},{9,13},{10,... | collective-permute-start | bytes 196616 | tf_op jit(solution)/shard_map/ppermute | solution.py:55
  11.1 0.5 %collective-permute-done.1 = f32[64,256]{1,0:T(8,128)S(1)} collective-permute-done((f32[64,256]{1,0:T(8,128)S(1)}, f32[64,256]{1,0:T(8,128)S(1)}, u32[]{:S(2)}, u32[]{:S(2)}) %collective-permute-start.1) | collective-permute-done | bytes 65568 | tf_op jit(solution)/shard_map/ppermute | solution.py:55
  11.7 1.3 %collective-permute-done.3 = f32[64,256]{1,0:T(8,128)S(1)} collective-permute-done((f32[64,256]{1,0:T(8,128)S(1)}, f32[64,256]{1,0:T(8,128)S(1)}, u32[]{:S(2)}, u32[]{:S(2)}) %collective-permute-start.3) | collective-permute-done | bytes 65568 | tf_op jit(solution)/shard_map/ppermute | solution.py:55
  13.0 1.4 %collective-permute-done.2 = f32[64,256]{1,0:T(8,128)S(1)} collective-permute-done((f32[64,256]{1,0:T(8,128)S(1)}, f32[64,256]{1,0:T(8,128)S(1)}, u32[]{:S(2)}, u32[]{:S(2)}) %collective-permute-start.2) | collective-permute-done | bytes 65568 | tf_op jit(solution)/shard_map/ppermute | solution.py:55
  14.4 2.7 %collective-permute-start.4 = (f32[32,256]{1,0:T(8,128)S(1)}, f32[32,256]{1,0:T(8,128)S(1)}, u32[]{:S(2)}, u32[]{:S(2)}) collective-permute-start(f32[32,256]{1,0:T(8,128)S(1)} %slice_select_fusion.1), channel_id=1, source_target_pairs={{0,8},{1,9},{2,10},{3,11},{4,12},{5,13},{6,14},{7,15},{8,0},{9,1},... | collective-permute-start | bytes 98312 | tf_op jit(solution)/shard_map/ppermute | solution.py:48
  17.1 2.2 %collective-permute-done.4 = f32[32,256]{1,0:T(8,128)S(1)} collective-permute-done((f32[32,256]{1,0:T(8,128)S(1)}, f32[32,256]{1,0:T(8,128)S(1)}, u32[]{:S(2)}, u32[]{:S(2)}) %collective-permute-start.4) | collective-permute-done | bytes 32800 | tf_op jit(solution)/shard_map/ppermute | solution.py:48
  19.3 2.6 %collective-permute-start.5 = (f32[32,256]{1,0:T(8,128)S(1)}, f32[32,256]{1,0:T(8,128)S(1)}, u32[]{:S(2)}, u32[]{:S(2)}) collective-permute-start(f32[32,256]{1,0:T(8,128)S(1)} %select_add_fusion), channel_id=1, source_target_pairs={{0,8},{1,9},{2,10},{3,11},{4,12},{5,13},{6,14},{7,15},{8,0},{9,1},... | collective-permute-start | bytes 98312 | tf_op jit(solution)/shard_map/ppermute | solution.py:60
  21.9 2.3 %collective-permute-done.5 = f32[32,256]{1,0:T(8,128)S(1)} collective-permute-done((f32[32,256]{1,0:T(8,128)S(1)}, f32[32,256]{1,0:T(8,128)S(1)}, u32[]{:S(2)}, u32[]{:S(2)}) %collective-permute-start.5) | collective-permute-done | bytes 32800 | tf_op jit(solution)/shard_map/ppermute | solution.py:60
  24.2 0.7 %collective-permute-start.8 = (f32[64,256]{1,0:T(8,128)S(1)}, f32[64,256]{1,0:T(8,128)S(1)}, u32[]{:S(2)}, u32[]{:S(2)}) collective-permute-start(f32[64,256]{1,0:T(8,128)S(1)} %maximum_select_fusion.1), channel_id=1, source_target_pairs={{0,2},{1,3},{2,4},{3,5},{4,6},{5,7},{6,0},{7,1},{8,10},{9,11},{10,... | collective-permute-start | bytes 196616 | tf_op jit(solution)/shard_map/ppermute | solution.py:63
  24.9 0.9 %collective-permute-start.7 = (f32[64,256]{1,0:T(8,128)S(1)}, f32[64,256]{1,0:T(8,128)S(1)}, u32[]{:S(2)}, u32[]{:S(2)}) collective-permute-start(f32[64,256]{1,0:T(8,128)S(1)} %maximum_select_fusion.1), channel_id=1, source_target_pairs={{0,4},{1,5},{2,6},{3,7},{4,0},{5,1},{6,2},{7,3},{8,12},{9,13},{10,... | collective-permute-start | bytes 196616 | tf_op jit(solution)/shard_map/ppermute | solution.py:63
  25.9 2.3 %collective-permute-start.6 = (f32[64,256]{1,0:T(8,128)S(1)}, f32[64,256]{1,0:T(8,128)S(1)}, u32[]{:S(2)}, u32[]{:S(2)}) collective-permute-start(f32[64,256]{1,0:T(8,128)S(1)} %maximum_select_fusion.1), channel_id=1, source_target_pairs={{0,6},{1,7},{2,0},{3,1},{4,2},{5,3},{6,4},{7,5},{8,14},{9,15},{10,... | collective-permute-start | bytes 196616 | tf_op jit(solution)/shard_map/ppermute | solution.py:63
  28.1 1.3 %collective-permute-done.8 = f32[64,256]{1,0:T(8,128)S(1)} collective-permute-done((f32[64,256]{1,0:T(8,128)S(1)}, f32[64,256]{1,0:T(8,128)S(1)}, u32[]{:S(2)}, u32[]{:S(2)}) %collective-permute-start.8) | collective-permute-done | bytes 65568 | tf_op jit(solution)/shard_map/ppermute | solution.py:63
  29.4 0.0 collective-permute-done.7
  29.4 0.7 %collective-permute-done.6 = f32[64,256]{1,0:T(8,128)S(1)} collective-permute-done((f32[64,256]{1,0:T(8,128)S(1)}, f32[64,256]{1,0:T(8,128)S(1)}, u32[]{:S(2)}, u32[]{:S(2)}) %collective-permute-start.6) | collective-permute-done | bytes 65568 | tf_op jit(solution)/shard_map/ppermute | solution.py:63
  30.3 0.1 collective-permute-start.9
  30.4 1.5 %collective-permute-done.9 = f32[256,256]{1,0:T(8,128)S(1)} collective-permute-done((f32[256,256]{1,0:T(8,128)S(1)}, f32[256,256]{1,0:T(8,128)S(1)}, u32[]{:S(2)}, u32[]{:S(2)}) %collective-permute-start.9) | collective-permute-done | bytes 262176 | tf_op jit(solution)/shard_map/ppermute | solution.py:60
  32.0 0.1 select_multiply_fusion
  32.0 0.2 abs_reduce_fusion
  32.2 0.1 reduce_max.9
  32.3 0.5 %fusion.13 = f32[2,256,256]{2,1,0:T(8,128)S(1)} fusion(f32[256,256]{1,0:T(8,128)S(1)} %fusion.27, f32[2]{0:T(128)S(1)} %reduce_max.9, f32[256,256]{1,0:T(8,128)S(1)} %fusion.28, f32[512,256]{1,0:T(8,128)S(1)} %select_multiply_fusion), kind=kOutput, calls=%fused_computation.29 | convolution fusion | flops 202113024 | bytes 1572872 | tf_op jit(solution)/shard_map/dot_general | solution.py:85
  32.9 0.5 fusion.6
  33.3 0.1 multiply_subtract_fusion
  33.5 0.6 %fusion.7 = f32[2,2,256,256]{3,2,1,0:T(8,128)S(1)} fusion(f32[2,256,256,1]{2,1,3,0:T(8,128)S(1)} %fusion.6, f32[2,1,256,256]{3,2,0,1:T(8,128)S(1)} %multiply_subtract_fusion, f32[2,1,256,256]{3,2,0,1:T(8,128)S(1)} %bitcast.81), kind=kOutput, calls=%fused_computation.16 | convolution fusion | flops 402915328 | bytes 2621440 | tf_op jit(solution)/shard_map/tkij,tjl->tkil/dot_general | solution.py:88
  34.1 0.4 fusion.4
  34.5 0.6 %fusion.38 = f32[2,2,256,256]{3,2,1,0:T(8,128)S(1)} fusion(f32[2,2,256,256]{3,2,1,0:T(8,128)S(1)} %fusion.7, f32[2,256,256,1]{2,1,3,0:T(8,128)S(1)} %fusion.4), kind=kOutput, calls=%fused_computation.84 | convolution fusion | flops 402653184 | bytes 2621440 | tf_op jit(solution)/shard_map/tkij,tjl->tkil/dot_general | solution.py:88
  35.1 0.4 fusion.2
  35.5 0.4 fusion.9
  35.9 0.3 fusion.29
  36.1 0.0 copy-start
  36.2 1.4 %collective-permute-start.10 = (f32[128,256]{1,0:T(8,128)S(1)}, f32[128,256]{1,0:T(8,128)S(1)}, u32[]{:S(2)}, u32[]{:S(2)}) collective-permute-start(f32[128,256]{1,0:T(8,128)S(1)} %slice_select_fusion), channel_id=1, source_target_pairs={{16,0},{17,1},{18,2},{19,3},{20,4},{21,5},{22,6},{23,7},{24,8},{25... | collective-permute-start | bytes 393224 | tf_op jit(solution)/shard_map/ppermute | solution.py:99
  37.6 6.1 %collective-permute-done.10 = f32[128,256]{1,0:T(8,128)S(1)} collective-permute-done((f32[128,256]{1,0:T(8,128)S(1)}, f32[128,256]{1,0:T(8,128)S(1)}, u32[]{:S(2)}, u32[]{:S(2)}) %collective-permute-start.10) | collective-permute-done | bytes 131104 | tf_op jit(solution)/shard_map/ppermute | solution.py:99
  43.7 0.0 collective-permute-start.11
  43.7 1.3 %collective-permute-done.11 = f32[128,256]{1,0:T(8,128)S(1)} collective-permute-done((f32[128,256]{1,0:T(8,128)S(1)}, f32[128,256]{1,0:T(8,128)S(1)}, u32[]{:S(2)}, u32[]{:S(2)}) %collective-permute-start.11) | collective-permute-done | bytes 131104 | tf_op jit(solution)/shard_map/ppermute | solution.py:100
  45.1 0.3 fusion.15
  45.4 0.3 convolution_bitcast_fusion.1
  45.7 0.0 copy-done
  45.7 0.0 copy-start.1
  45.7 1.7 %fusion = bf16[2,1536,256]{2,1,0:T(8,128)(2,1)} fusion(bf16[2,1536,256]{2,1,0:T(8,128)(2,1)S(1)} %copy-done, f32[2,256,256]{2,1,0:T(8,128)S(1)} %pad_maximum_fusion.1), kind=kOutput, calls=%fused_computation.2 | convolution fusion | flops 403570688 | bytes 3670016 | tf_op jit(solution)/shard_map/trm,tmn->trn/dot_general | solution.py:157
  47.5 0.0 copy-done.1
  (22 shorter events, 0.4 us)
Async XLA Ops:
  3.4 1.7 %collective-permute-start = (f32[256,256]{1,0:T(8,128)S(1)}, f32[256,256]{1,0:T(8,128)S(1)}, u32[]{:S(2)}, u32[]{:S(2)}) collective-permute-start(f32[256,256]{1,0:T(8,128)S(1)} %select_bitcast_fusion), channel_id=1, source_target_pairs={{0,1},{1,0},{2,3},{3,2},{4,5},{5,4},{6,7},{7,6},{8,9},{9,8},{10,11... | collective-permute-start | bytes 786440 | tf_op jit(solution)/shard_map/ppermute | solution.py:48
  5.2 6.4 %collective-permute-start.1 = (f32[64,256]{1,0:T(8,128)S(1)}, f32[64,256]{1,0:T(8,128)S(1)}, u32[]{:S(2)}, u32[]{:S(2)}) collective-permute-start(f32[64,256]{1,0:T(8,128)S(1)} %get-tuple-element.12), channel_id=1, source_target_pairs={{0,2},{1,3},{2,4},{3,5},{4,6},{5,7},{6,0},{7,1},{8,10},{9,11},{10,... | collective-permute-start | bytes 196616 | tf_op jit(solution)/shard_map/ppermute | solution.py:55
  8.2 4.8 %collective-permute-start.3 = (f32[64,256]{1,0:T(8,128)S(1)}, f32[64,256]{1,0:T(8,128)S(1)}, u32[]{:S(2)}, u32[]{:S(2)}) collective-permute-start(f32[64,256]{1,0:T(8,128)S(1)} %get-tuple-element.13), channel_id=1, source_target_pairs={{0,6},{1,7},{2,0},{3,1},{4,2},{5,3},{6,4},{7,5},{8,14},{9,15},{10,... | collective-permute-start | bytes 196616 | tf_op jit(solution)/shard_map/ppermute | solution.py:55
  9.2 5.1 %collective-permute-start.2 = (f32[64,256]{1,0:T(8,128)S(1)}, f32[64,256]{1,0:T(8,128)S(1)}, u32[]{:S(2)}, u32[]{:S(2)}) collective-permute-start(f32[64,256]{1,0:T(8,128)S(1)} %get-tuple-element.14), channel_id=1, source_target_pairs={{0,4},{1,5},{2,6},{3,7},{4,0},{5,1},{6,2},{7,3},{8,12},{9,13},{10,... | collective-permute-start | bytes 196616 | tf_op jit(solution)/shard_map/ppermute | solution.py:55
  14.4 4.9 %collective-permute-start.4 = (f32[32,256]{1,0:T(8,128)S(1)}, f32[32,256]{1,0:T(8,128)S(1)}, u32[]{:S(2)}, u32[]{:S(2)}) collective-permute-start(f32[32,256]{1,0:T(8,128)S(1)} %slice_select_fusion.1), channel_id=1, source_target_pairs={{0,8},{1,9},{2,10},{3,11},{4,12},{5,13},{6,14},{7,15},{8,0},{9,1},... | collective-permute-start | bytes 98312 | tf_op jit(solution)/shard_map/ppermute | solution.py:48
  19.3 4.9 %collective-permute-start.5 = (f32[32,256]{1,0:T(8,128)S(1)}, f32[32,256]{1,0:T(8,128)S(1)}, u32[]{:S(2)}, u32[]{:S(2)}) collective-permute-start(f32[32,256]{1,0:T(8,128)S(1)} %select_add_fusion), channel_id=1, source_target_pairs={{0,8},{1,9},{2,10},{3,11},{4,12},{5,13},{6,14},{7,15},{8,0},{9,1},... | collective-permute-start | bytes 98312 | tf_op jit(solution)/shard_map/ppermute | solution.py:60
  24.2 5.2 %collective-permute-start.8 = (f32[64,256]{1,0:T(8,128)S(1)}, f32[64,256]{1,0:T(8,128)S(1)}, u32[]{:S(2)}, u32[]{:S(2)}) collective-permute-start(f32[64,256]{1,0:T(8,128)S(1)} %maximum_select_fusion.1), channel_id=1, source_target_pairs={{0,2},{1,3},{2,4},{3,5},{4,6},{5,7},{6,0},{7,1},{8,10},{9,11},{10,... | collective-permute-start | bytes 196616 | tf_op jit(solution)/shard_map/ppermute | solution.py:63
  24.9 4.5 %collective-permute-start.7 = (f32[64,256]{1,0:T(8,128)S(1)}, f32[64,256]{1,0:T(8,128)S(1)}, u32[]{:S(2)}, u32[]{:S(2)}) collective-permute-start(f32[64,256]{1,0:T(8,128)S(1)} %maximum_select_fusion.1), channel_id=1, source_target_pairs={{0,4},{1,5},{2,6},{3,7},{4,0},{5,1},{6,2},{7,3},{8,12},{9,13},{10,... | collective-permute-start | bytes 196616 | tf_op jit(solution)/shard_map/ppermute | solution.py:63
  25.9 4.3 %collective-permute-start.6 = (f32[64,256]{1,0:T(8,128)S(1)}, f32[64,256]{1,0:T(8,128)S(1)}, u32[]{:S(2)}, u32[]{:S(2)}) collective-permute-start(f32[64,256]{1,0:T(8,128)S(1)} %maximum_select_fusion.1), channel_id=1, source_target_pairs={{0,6},{1,7},{2,0},{3,1},{4,2},{5,3},{6,4},{7,5},{8,14},{9,15},{10,... | collective-permute-start | bytes 196616 | tf_op jit(solution)/shard_map/ppermute | solution.py:63
  30.3 1.6 %collective-permute-start.9 = (f32[256,256]{1,0:T(8,128)S(1)}, f32[256,256]{1,0:T(8,128)S(1)}, u32[]{:S(2)}, u32[]{:S(2)}) collective-permute-start(f32[256,256]{1,0:T(8,128)S(1)} %pad_maximum_fusion.2), channel_id=1, source_target_pairs={{0,1},{1,0},{2,3},{3,2},{4,5},{5,4},{6,7},{7,6},{8,9},{9,8},{10,11... | collective-permute-start | bytes 786440 | tf_op jit(solution)/shard_map/ppermute | solution.py:60
  36.1 9.6 %copy-start = (bf16[2,1536,256]{2,1,0:T(8,128)(2,1)S(1)}, bf16[2,1536,256]{2,1,0:T(8,128)(2,1)}, u32[]{:S(2)}) copy-start(bf16[2,1536,256]{2,1,0:T(8,128)(2,1)} %param.2) | copy-start | bytes 4718596
  36.2 7.6 %collective-permute-start.10 = (f32[128,256]{1,0:T(8,128)S(1)}, f32[128,256]{1,0:T(8,128)S(1)}, u32[]{:S(2)}, u32[]{:S(2)}) collective-permute-start(f32[128,256]{1,0:T(8,128)S(1)} %slice_select_fusion), channel_id=1, source_target_pairs={{16,0},{17,1},{18,2},{19,3},{20,4},{21,5},{22,6},{23,7},{24,8},{25... | collective-permute-start | bytes 393224 | tf_op jit(solution)/shard_map/ppermute | solution.py:99
  43.7 1.3 %collective-permute-start.11 = (f32[128,256]{1,0:T(8,128)S(1)}, f32[128,256]{1,0:T(8,128)S(1)}, u32[]{:S(2)}, u32[]{:S(2)}) collective-permute-start(f32[128,256]{1,0:T(8,128)S(1)} %collective-permute-done.10), channel_id=1, source_target_pairs={{0,1},{1,0},{2,3},{3,2},{4,5},{5,4},{6,7},{7,6},{8,9},{9,8},{10,11... | collective-permute-start | bytes 393224 | tf_op jit(solution)/shard_map/ppermute | solution.py:100
  45.7 1.7 %copy-start.1 = (f32[2,256,256]{2,1,0:T(8,128)}, f32[2,256,256]{2,1,0:T(8,128)S(1)}, u32[]{:S(2)}) copy-start(f32[2,256,256]{2,1,0:T(8,128)S(1)} %pad_maximum_fusion.1) | copy-start | bytes 1572868

commit v10 on v9

--- a/solution.py
+++ b/solution.py
@@ -84,8 +84,9 @@
     factor = 1.5 * identity - 0.5 * iterate
     pair = jnp.stack([jnp.matmul(iterate, factor, precision=NS_PRECISION), factor], axis=1)
     for sweep_index in range(NS_STEPS - 1):
-        factor = 1.5 * identity - 0.5 * jnp.matmul(pair[:, 1], pair[:, 0], precision=NS_PRECISION)
-        pair = jnp.einsum("tkij,tjl->tkil", pair, factor, precision=NS_PRECISION)
+        precision = lax.Precision.HIGHEST if sweep_index == NS_STEPS - 2 else NS_PRECISION
+        factor = 1.5 * identity - 0.5 * jnp.matmul(pair[:, 1], pair[:, 0], precision=precision)
+        pair = jnp.einsum("tkij,tjl->tkil", pair, factor, precision=precision)
     return pair[:, 1] / jnp.sqrt(row_bound)[:, None, None]
 
 

time: 48 us -> 48.6 us (1.012)
  matrix products: 6.74 us -> 7.28 us
where the time goes in v10:
time: 48.6 us; the launch traced here: 48 us
  waiting for transfers between devices  19.9 us (41%)
  starting transfers between devices  17.1 us (35%)
  matrix products  7.28 us (15%)
  other arithmetic  2.68 us (6%)
  between operations  0.96 us (2%)
    ppermute x1, waiting for transfers between devices, split_shift(): got = lax.ppermute(part, axis, pairs)  6.13 us
    ppermute x3, starting transfers between devices, grouped_sum(): lax.ppermute(send, axis, digit_pairs(count, radix, place, offset))  5.92 us
    ppermute x3, starting transfers between devices, grouped_sum(): lax.ppermute(value, axis, digit_pairs(count, radix, place, offset))  3.9 us
    ppermute x2, waiting for transfers between devices, grouped_sum(): other = lax.ppermute(value, axis, digit_pairs(count, radix, place, 1))  3.8 us
    ppermute x2, waiting for transfers between devices, grouped_sum(): value = keep + lax.ppermute(send, axis, digit_pairs(count, radix, place, 1))  3.38 us
    ppermute x3, waiting for transfers between devices, grouped_sum(): lax.ppermute(send, axis, digit_pairs(count, radix, place, offset))  3.23 us
    ppermute x2, starting transfers between devices, grouped_sum(): value = keep + lax.ppermute(send, axis, digit_pairs(count, radix, place, 1))  3.17 us
    ppermute x2, starting transfers between devices, grouped_sum(): other = lax.ppermute(value, axis, digit_pairs(count, radix, place, 1))  2.66 us
  transfers between devices with their start and end apart: 12, of which 11 were waited for; matrix products, arithmetic and copies ran while one was open for 0% of the time, Pallas kernels for 0%

profile of v10, /device:TPU:0, one launch (start us, length us, event | category | flops | bytes accessed | tf_op | source)
XLA Modules:
  0.0 48.0 jit_solution(7852447332869273030)
XLA Ops:
  0.6 1.9 %multiply_convert_fusion = bf16[2,1536,256]{2,1,0:T(8,128)(2,1)S(1)} fusion(bf16[2,1536,256]{2,1,0:T(8,128)(2,1)} %param.2, f32[2,1536]{1,0:T(2,128)} %param.3), kind=kLoop, calls=%fused_computation | loop fusion | flops 2359296 | bytes 3158016 | tf_op jit(solution)/shard_map/convert_element_type | solution.py:140
  2.5 0.4 fusion.11
  3.0 0.4 convolution_add_fusion
  3.4 0.5 %collective-permute-start = (f32[256,256]{1,0:T(8,128)S(1)}, f32[256,256]{1,0:T(8,128)S(1)}, u32[]{:S(2)}, u32[]{:S(2)}) collective-permute-start(f32[256,256]{1,0:T(8,128)S(1)} %select_bitcast_fusion), channel_id=1, source_target_pairs={{0,1},{1,0},{2,3},{3,2},{4,5},{5,4},{6,7},{7,6},{8,9},{9,8},{10,11... | collective-permute-start | bytes 786440 | tf_op jit(solution)/shard_map/ppermute | solution.py:48
  4.0 1.2 %collective-permute-done = f32[256,256]{1,0:T(8,128)S(1)} collective-permute-done((f32[256,256]{1,0:T(8,128)S(1)}, f32[256,256]{1,0:T(8,128)S(1)}, u32[]{:S(2)}, u32[]{:S(2)}) %collective-permute-start) | collective-permute-done | bytes 262176 | tf_op jit(solution)/shard_map/ppermute | solution.py:48
  5.2 2.9 %collective-permute-start.1 = (f32[64,256]{1,0:T(8,128)S(1)}, f32[64,256]{1,0:T(8,128)S(1)}, u32[]{:S(2)}, u32[]{:S(2)}) collective-permute-start(f32[64,256]{1,0:T(8,128)S(1)} %get-tuple-element.12), channel_id=1, source_target_pairs={{0,2},{1,3},{2,4},{3,5},{4,6},{5,7},{6,0},{7,1},{8,10},{9,11},{10,... | collective-permute-start | bytes 196616 | tf_op jit(solution)/shard_map/ppermute | solution.py:55
  8.2 1.1 %collective-permute-start.3 = (f32[64,256]{1,0:T(8,128)S(1)}, f32[64,256]{1,0:T(8,128)S(1)}, u32[]{:S(2)}, u32[]{:S(2)}) collective-permute-start(f32[64,256]{1,0:T(8,128)S(1)} %get-tuple-element.13), channel_id=1, source_target_pairs={{0,6},{1,7},{2,0},{3,1},{4,2},{5,3},{6,4},{7,5},{8,14},{9,15},{10,... | collective-permute-start | bytes 196616 | tf_op jit(solution)/shard_map/ppermute | solution.py:55
  9.2 1.9 %collective-permute-start.2 = (f32[64,256]{1,0:T(8,128)S(1)}, f32[64,256]{1,0:T(8,128)S(1)}, u32[]{:S(2)}, u32[]{:S(2)}) collective-permute-start(f32[64,256]{1,0:T(8,128)S(1)} %get-tuple-element.14), channel_id=1, source_target_pairs={{0,4},{1,5},{2,6},{3,7},{4,0},{5,1},{6,2},{7,3},{8,12},{9,13},{10,... | collective-permute-start | bytes 196616 | tf_op jit(solution)/shard_map/ppermute | solution.py:55
  11.1 0.5 %collective-permute-done.1 = f32[64,256]{1,0:T(8,128)S(1)} collective-permute-done((f32[64,256]{1,0:T(8,128)S(1)}, f32[64,256]{1,0:T(8,128)S(1)}, u32[]{:S(2)}, u32[]{:S(2)}) %collective-permute-start.1) | collective-permute-done | bytes 65568 | tf_op jit(solution)/shard_map/ppermute | solution.py:55
  11.7 1.3 %collective-permute-done.3 = f32[64,256]{1,0:T(8,128)S(1)} collective-permute-done((f32[64,256]{1,0:T(8,128)S(1)}, f32[64,256]{1,0:T(8,128)S(1)}, u32[]{:S(2)}, u32[]{:S(2)}) %collective-permute-start.3) | collective-permute-done | bytes 65568 | tf_op jit(solution)/shard_map/ppermute | solution.py:55
  13.0 1.4 %collective-permute-done.2 = f32[64,256]{1,0:T(8,128)S(1)} collective-permute-done((f32[64,256]{1,0:T(8,128)S(1)}, f32[64,256]{1,0:T(8,128)S(1)}, u32[]{:S(2)}, u32[]{:S(2)}) %collective-permute-start.2) | collective-permute-done | bytes 65568 | tf_op jit(solution)/shard_map/ppermute | solution.py:55
  14.4 2.7 %collective-permute-start.4 = (f32[32,256]{1,0:T(8,128)S(1)}, f32[32,256]{1,0:T(8,128)S(1)}, u32[]{:S(2)}, u32[]{:S(2)}) collective-permute-start(f32[32,256]{1,0:T(8,128)S(1)} %slice_select_fusion.1), channel_id=1, source_target_pairs={{0,8},{1,9},{2,10},{3,11},{4,12},{5,13},{6,14},{7,15},{8,0},{9,1},... | collective-permute-start | bytes 98312 | tf_op jit(solution)/shard_map/ppermute | solution.py:48
  17.1 2.2 %collective-permute-done.4 = f32[32,256]{1,0:T(8,128)S(1)} collective-permute-done((f32[32,256]{1,0:T(8,128)S(1)}, f32[32,256]{1,0:T(8,128)S(1)}, u32[]{:S(2)}, u32[]{:S(2)}) %collective-permute-start.4) | collective-permute-done | bytes 32800 | tf_op jit(solution)/shard_map/ppermute | solution.py:48
  19.3 2.6 %collective-permute-start.5 = (f32[32,256]{1,0:T(8,128)S(1)}, f32[32,256]{1,0:T(8,128)S(1)}, u32[]{:S(2)}, u32[]{:S(2)}) collective-permute-start(f32[32,256]{1,0:T(8,128)S(1)} %select_add_fusion), channel_id=1, source_target_pairs={{0,8},{1,9},{2,10},{3,11},{4,12},{5,13},{6,14},{7,15},{8,0},{9,1},... | collective-permute-start | bytes 98312 | tf_op jit(solution)/shard_map/ppermute | solution.py:60
  21.9 2.3 %collective-permute-done.5 = f32[32,256]{1,0:T(8,128)S(1)} collective-permute-done((f32[32,256]{1,0:T(8,128)S(1)}, f32[32,256]{1,0:T(8,128)S(1)}, u32[]{:S(2)}, u32[]{:S(2)}) %collective-permute-start.5) | collective-permute-done | bytes 32800 | tf_op jit(solution)/shard_map/ppermute | solution.py:60
  24.2 0.7 %collective-permute-start.8 = (f32[64,256]{1,0:T(8,128)S(1)}, f32[64,256]{1,0:T(8,128)S(1)}, u32[]{:S(2)}, u32[]{:S(2)}) collective-permute-start(f32[64,256]{1,0:T(8,128)S(1)} %maximum_select_fusion.1), channel_id=1, source_target_pairs={{0,2},{1,3},{2,4},{3,5},{4,6},{5,7},{6,0},{7,1},{8,10},{9,11},{10,... | collective-permute-start | bytes 196616 | tf_op jit(solution)/shard_map/ppermute | solution.py:63
  24.9 0.9 %collective-permute-start.7 = (f32[64,256]{1,0:T(8,128)S(1)}, f32[64,256]{1,0:T(8,128)S(1)}, u32[]{:S(2)}, u32[]{:S(2)}) collective-permute-start(f32[64,256]{1,0:T(8,128)S(1)} %maximum_select_fusion.1), channel_id=1, source_target_pairs={{0,4},{1,5},{2,6},{3,7},{4,0},{5,1},{6,2},{7,3},{8,12},{9,13},{10,... | collective-permute-start | bytes 196616 | tf_op jit(solution)/shard_map/ppermute | solution.py:63
  25.9 2.3 %collective-permute-start.6 = (f32[64,256]{1,0:T(8,128)S(1)}, f32[64,256]{1,0:T(8,128)S(1)}, u32[]{:S(2)}, u32[]{:S(2)}) collective-permute-start(f32[64,256]{1,0:T(8,128)S(1)} %maximum_select_fusion.1), channel_id=1, source_target_pairs={{0,6},{1,7},{2,0},{3,1},{4,2},{5,3},{6,4},{7,5},{8,14},{9,15},{10,... | collective-permute-start | bytes 196616 | tf_op jit(solution)/shard_map/ppermute | solution.py:63
  28.1 1.3 %collective-permute-done.8 = f32[64,256]{1,0:T(8,128)S(1)} collective-permute-done((f32[64,256]{1,0:T(8,128)S(1)}, f32[64,256]{1,0:T(8,128)S(1)}, u32[]{:S(2)}, u32[]{:S(2)}) %collective-permute-start.8) | collective-permute-done | bytes 65568 | tf_op jit(solution)/shard_map/ppermute | solution.py:63
  29.4 0.0 collective-permute-done.7
  29.4 0.7 %collective-permute-done.6 = f32[64,256]{1,0:T(8,128)S(1)} collective-permute-done((f32[64,256]{1,0:T(8,128)S(1)}, f32[64,256]{1,0:T(8,128)S(1)}, u32[]{:S(2)}, u32[]{:S(2)}) %collective-permute-start.6) | collective-permute-done | bytes 65568 | tf_op jit(solution)/shard_map/ppermute | solution.py:63
  30.3 0.1 collective-permute-start.9
  30.4 1.5 %collective-permute-done.9 = f32[256,256]{1,0:T(8,128)S(1)} collective-permute-done((f32[256,256]{1,0:T(8,128)S(1)}, f32[256,256]{1,0:T(8,128)S(1)}, u32[]{:S(2)}, u32[]{:S(2)}) %collective-permute-start.9) | collective-permute-done | bytes 262176 | tf_op jit(solution)/shard_map/ppermute | solution.py:60
  32.0 0.1 select_multiply_fusion
  32.0 0.2 abs_reduce_fusion
  32.2 0.1 reduce_max.9
  32.3 0.5 %fusion.13 = f32[2,256,256]{2,1,0:T(8,128)S(1)} fusion(f32[256,256]{1,0:T(8,128)S(1)} %fusion.27, f32[2]{0:T(128)S(1)} %reduce_max.9, f32[256,256]{1,0:T(8,128)S(1)} %fusion.28, f32[512,256]{1,0:T(8,128)S(1)} %select_multiply_fusion), kind=kOutput, calls=%fused_computation.29 | convolution fusion | flops 202113024 | bytes 1572872 | tf_op jit(solution)/shard_map/dot_general | solution.py:85
  32.9 0.5 fusion.6
  33.3 0.1 multiply_subtract_fusion
  33.5 0.6 %fusion.7 = f32[2,2,256,256]{3,2,1,0:T(8,128)S(1)} fusion(f32[2,256,256,1]{2,1,3,0:T(8,128)S(1)} %fusion.6, f32[2,1,256,256]{3,2,0,1:T(8,128)S(1)} %multiply_subtract_fusion, f32[2,1,256,256]{3,2,0,1:T(8,128)S(1)} %bitcast.81), kind=kOutput, calls=%fused_computation.16 | convolution fusion | flops 402915328 | bytes 2621440 | tf_op jit(solution)/shard_map/tkij,tjl->tkil/dot_general | solution.py:89
  34.1 0.4 fusion.4
  34.5 0.6 %fusion.38 = f32[2,2,256,256]{3,2,1,0:T(8,128)S(1)} fusion(f32[2,2,256,256]{3,2,1,0:T(8,128)S(1)} %fusion.7, f32[2,256,256,1]{2,1,3,0:T(8,128)S(1)} %fusion.4), kind=kOutput, calls=%fused_computation.84 | convolution fusion | flops 402653184 | bytes 2621440 | tf_op jit(solution)/shard_map/tkij,tjl->tkil/dot_general | solution.py:89
  35.1 0.7 %fusion.2 = f32[2,256,256,1]{2,1,3,0:T(8,128)S(1)} fusion(f32[2,2,256,256]{3,2,1,0:T(8,128)S(1)} %fusion.38, f32[256,256]{1,0:T(8,128)S(1)} %fusion.27), kind=kOutput, calls=%fused_computation.7 | convolution fusion | flops 402915328 | bytes 1835008 | tf_op jit(solution)/shard_map/dot_general | solution.py:88
  35.7 0.7 %fusion.9 = f32[2,256,256]{2,1,0:T(8,128)S(1)} fusion(f32[2,2,256,256]{3,2,1,0:T(8,128)S(1)} %fusion.38, f32[2,256,256,1]{2,1,3,0:T(8,128)S(1)} %fusion.2, f32[2]{0:T(128)S(1)} %sqrt.7), kind=kOutput, calls=%fused_computation.18 | convolution fusion | flops 402784256 | bytes 2097160 | tf_op jit(solution)/shard_map/slice | solution.py:90
  36.4 0.3 fusion.29
  36.7 0.0 copy-start
  36.7 1.4 %collective-permute-start.10 = (f32[128,256]{1,0:T(8,128)S(1)}, f32[128,256]{1,0:T(8,128)S(1)}, u32[]{:S(2)}, u32[]{:S(2)}) collective-permute-start(f32[128,256]{1,0:T(8,128)S(1)} %slice_select_fusion), channel_id=1, source_target_pairs={{16,0},{17,1},{18,2},{19,3},{20,4},{21,5},{22,6},{23,7},{24,8},{25... | collective-permute-start | bytes 393224 | tf_op jit(solution)/shard_map/ppermute | solution.py:100
  38.2 6.1 %collective-permute-done.10 = f32[128,256]{1,0:T(8,128)S(1)} collective-permute-done((f32[128,256]{1,0:T(8,128)S(1)}, f32[128,256]{1,0:T(8,128)S(1)}, u32[]{:S(2)}, u32[]{:S(2)}) %collective-permute-start.10) | collective-permute-done | bytes 131104 | tf_op jit(solution)/shard_map/ppermute | solution.py:100
  44.3 0.0 collective-permute-start.11
  44.3 1.3 %collective-permute-done.11 = f32[128,256]{1,0:T(8,128)S(1)} collective-permute-done((f32[128,256]{1,0:T(8,128)S(1)}, f32[128,256]{1,0:T(8,128)S(1)}, u32[]{:S(2)}, u32[]{:S(2)}) %collective-permute-start.11) | collective-permute-done | bytes 131104 | tf_op jit(solution)/shard_map/ppermute | solution.py:101
  45.6 0.3 fusion.15
  45.9 0.3 convolution_bitcast_fusion.1
  46.3 0.0 copy-done
  46.3 0.0 copy-start.1
  46.3 1.7 %fusion = bf16[2,1536,256]{2,1,0:T(8,128)(2,1)} fusion(bf16[2,1536,256]{2,1,0:T(8,128)(2,1)S(1)} %copy-done, f32[2,256,256]{2,1,0:T(8,128)S(1)} %pad_maximum_fusion.1), kind=kOutput, calls=%fused_computation.2 | convolution fusion | flops 403570688 | bytes 3670016 | tf_op jit(solution)/shard_map/trm,tmn->trn/dot_general | solution.py:158
  48.0 0.0 copy-done.1
  (22 shorter events, 0.4 us)
Async XLA Ops:
  3.4 1.7 %collective-permute-start = (f32[256,256]{1,0:T(8,128)S(1)}, f32[256,256]{1,0:T(8,128)S(1)}, u32[]{:S(2)}, u32[]{:S(2)}) collective-permute-start(f32[256,256]{1,0:T(8,128)S(1)} %select_bitcast_fusion), channel_id=1, source_target_pairs={{0,1},{1,0},{2,3},{3,2},{4,5},{5,4},{6,7},{7,6},{8,9},{9,8},{10,11... | collective-permute-start | bytes 786440 | tf_op jit(solution)/shard_map/ppermute | solution.py:48
  5.2 6.4 %collective-permute-start.1 = (f32[64,256]{1,0:T(8,128)S(1)}, f32[64,256]{1,0:T(8,128)S(1)}, u32[]{:S(2)}, u32[]{:S(2)}) collective-permute-start(f32[64,256]{1,0:T(8,128)S(1)} %get-tuple-element.12), channel_id=1, source_target_pairs={{0,2},{1,3},{2,4},{3,5},{4,6},{5,7},{6,0},{7,1},{8,10},{9,11},{10,... | collective-permute-start | bytes 196616 | tf_op jit(solution)/shard_map/ppermute | solution.py:55
  8.2 4.8 %collective-permute-start.3 = (f32[64,256]{1,0:T(8,128)S(1)}, f32[64,256]{1,0:T(8,128)S(1)}, u32[]{:S(2)}, u32[]{:S(2)}) collective-permute-start(f32[64,256]{1,0:T(8,128)S(1)} %get-tuple-element.13), channel_id=1, source_target_pairs={{0,6},{1,7},{2,0},{3,1},{4,2},{5,3},{6,4},{7,5},{8,14},{9,15},{10,... | collective-permute-start | bytes 196616 | tf_op jit(solution)/shard_map/ppermute | solution.py:55
  9.2 5.1 %collective-permute-start.2 = (f32[64,256]{1,0:T(8,128)S(1)}, f32[64,256]{1,0:T(8,128)S(1)}, u32[]{:S(2)}, u32[]{:S(2)}) collective-permute-start(f32[64,256]{1,0:T(8,128)S(1)} %get-tuple-element.14), channel_id=1, source_target_pairs={{0,4},{1,5},{2,6},{3,7},{4,0},{5,1},{6,2},{7,3},{8,12},{9,13},{10,... | collective-permute-start | bytes 196616 | tf_op jit(solution)/shard_map/ppermute | solution.py:55
  14.4 4.9 %collective-permute-start.4 = (f32[32,256]{1,0:T(8,128)S(1)}, f32[32,256]{1,0:T(8,128)S(1)}, u32[]{:S(2)}, u32[]{:S(2)}) collective-permute-start(f32[32,256]{1,0:T(8,128)S(1)} %slice_select_fusion.1), channel_id=1, source_target_pairs={{0,8},{1,9},{2,10},{3,11},{4,12},{5,13},{6,14},{7,15},{8,0},{9,1},... | collective-permute-start | bytes 98312 | tf_op jit(solution)/shard_map/ppermute | solution.py:48
  19.3 4.9 %collective-permute-start.5 = (f32[32,256]{1,0:T(8,128)S(1)}, f32[32,256]{1,0:T(8,128)S(1)}, u32[]{:S(2)}, u32[]{:S(2)}) collective-permute-start(f32[32,256]{1,0:T(8,128)S(1)} %select_add_fusion), channel_id=1, source_target_pairs={{0,8},{1,9},{2,10},{3,11},{4,12},{5,13},{6,14},{7,15},{8,0},{9,1},... | collective-permute-start | bytes 98312 | tf_op jit(solution)/shard_map/ppermute | solution.py:60
  24.2 5.2 %collective-permute-start.8 = (f32[64,256]{1,0:T(8,128)S(1)}, f32[64,256]{1,0:T(8,128)S(1)}, u32[]{:S(2)}, u32[]{:S(2)}) collective-permute-start(f32[64,256]{1,0:T(8,128)S(1)} %maximum_select_fusion.1), channel_id=1, source_target_pairs={{0,2},{1,3},{2,4},{3,5},{4,6},{5,7},{6,0},{7,1},{8,10},{9,11},{10,... | collective-permute-start | bytes 196616 | tf_op jit(solution)/shard_map/ppermute | solution.py:63
  24.9 4.5 %collective-permute-start.7 = (f32[64,256]{1,0:T(8,128)S(1)}, f32[64,256]{1,0:T(8,128)S(1)}, u32[]{:S(2)}, u32[]{:S(2)}) collective-permute-start(f32[64,256]{1,0:T(8,128)S(1)} %maximum_select_fusion.1), channel_id=1, source_target_pairs={{0,4},{1,5},{2,6},{3,7},{4,0},{5,1},{6,2},{7,3},{8,12},{9,13},{10,... | collective-permute-start | bytes 196616 | tf_op jit(solution)/shard_map/ppermute | solution.py:63
  25.9 4.3 %collective-permute-start.6 = (f32[64,256]{1,0:T(8,128)S(1)}, f32[64,256]{1,0:T(8,128)S(1)}, u32[]{:S(2)}, u32[]{:S(2)}) collective-permute-start(f32[64,256]{1,0:T(8,128)S(1)} %maximum_select_fusion.1), channel_id=1, source_target_pairs={{0,6},{1,7},{2,0},{3,1},{4,2},{5,3},{6,4},{7,5},{8,14},{9,15},{10,... | collective-permute-start | bytes 196616 | tf_op jit(solution)/shard_map/ppermute | solution.py:63
  30.3 1.6 %collective-permute-start.9 = (f32[256,256]{1,0:T(8,128)S(1)}, f32[256,256]{1,0:T(8,128)S(1)}, u32[]{:S(2)}, u32[]{:S(2)}) collective-permute-start(f32[256,256]{1,0:T(8,128)S(1)} %pad_maximum_fusion.2), channel_id=1, source_target_pairs={{0,1},{1,0},{2,3},{3,2},{4,5},{5,4},{6,7},{7,6},{8,9},{9,8},{10,11... | collective-permute-start | bytes 786440 | tf_op jit(solution)/shard_map/ppermute | solution.py:60
  36.7 9.6 %copy-start = (bf16[2,1536,256]{2,1,0:T(8,128)(2,1)S(1)}, bf16[2,1536,256]{2,1,0:T(8,128)(2,1)}, u32[]{:S(2)}) copy-start(bf16[2,1536,256]{2,1,0:T(8,128)(2,1)} %param.2) | copy-start | bytes 4718596
  36.7 7.6 %collective-permute-start.10 = (f32[128,256]{1,0:T(8,128)S(1)}, f32[128,256]{1,0:T(8,128)S(1)}, u32[]{:S(2)}, u32[]{:S(2)}) collective-permute-start(f32[128,256]{1,0:T(8,128)S(1)} %slice_select_fusion), channel_id=1, source_target_pairs={{16,0},{17,1},{18,2},{19,3},{20,4},{21,5},{22,6},{23,7},{24,8},{25... | collective-permute-start | bytes 393224 | tf_op jit(solution)/shard_map/ppermute | solution.py:100
  44.3 1.3 %collective-permute-start.11 = (f32[128,256]{1,0:T(8,128)S(1)}, f32[128,256]{1,0:T(8,128)S(1)}, u32[]{:S(2)}, u32[]{:S(2)}) collective-permute-start(f32[128,256]{1,0:T(8,128)S(1)} %collective-permute-done.10), channel_id=1, source_target_pairs={{0,1},{1,0},{2,3},{3,2},{4,5},{5,4},{6,7},{7,6},{8,9},{9,8},{10,11... | collective-permute-start | bytes 393224 | tf_op jit(solution)/shard_map/ppermute | solution.py:101
  46.3 1.7 %copy-start.1 = (f32[2,256,256]{2,1,0:T(8,128)}, f32[2,256,256]{2,1,0:T(8,128)S(1)}, u32[]{:S(2)}) copy-start(f32[2,256,256]{2,1,0:T(8,128)S(1)} %pad_maximum_fusion.1) | copy-start | bytes 1572868

commit v11 on v10

--- a/solution.py
+++ b/solution.py
@@ -58,7 +58,8 @@
         digit = (me // place) % radix
         if radix == 2:
             other = lax.ppermute(value, axis, digit_pairs(count, radix, place, 1))
-            value = jnp.where(digit == 1, jnp.concatenate([other, value]), jnp.concatenate([value, other]))
+            upper = digit == 1
+            value = jnp.concatenate([jnp.where(upper, other, value), jnp.where(upper, value, other)])
             continue
         got = [value] + [lax.ppermute(value, axis, digit_pairs(count, radix, place, offset)) for offset in range(1, radix)]
         placed = []
@@ -99,7 +100,7 @@
     part = jnp.where(upper, value[half:], value[:half])
     got = lax.ppermute(part, axis, pairs)
     other = lax.ppermute(got, "state", digit_pairs(count, 2, 1, 1))
-    return jnp.where(upper, jnp.concatenate([other, got]), jnp.concatenate([got, other]))
+    return jnp.concatenate([jnp.where(upper, other, got), jnp.where(upper, got, other)])
 
 
 def later_product(local, axis):

time: 48.6 us -> 48.3 us (level)
  no operation moved by 1% of the time
where the time goes in v11:
time: 48.3 us; the launch traced here: 47.8 us
  waiting for transfers between devices  19.9 us (41%)
  starting transfers between devices  17 us (35%)
  matrix products  7.29 us (15%)
  other arithmetic  2.69 us (6%)
  between operations  0.91 us (2%)
    ppermute x1, waiting for transfers between devices, split_shift(): got = lax.ppermute(part, axis, pairs)  6.14 us
    ppermute x3, starting transfers between devices, grouped_sum(): lax.ppermute(send, axis, digit_pairs(count, radix, place, offset))  5.92 us
    ppermute x3, starting transfers between devices, grouped_sum(): lax.ppermute(value, axis, digit_pairs(count, radix, place, offset))  3.91 us
    ppermute x2, waiting for transfers between devices, grouped_sum(): other = lax.ppermute(value, axis, digit_pairs(count, radix, place, 1))  3.8 us
    ppermute x2, waiting for transfers between devices, grouped_sum(): value = keep + lax.ppermute(send, axis, digit_pairs(count, radix, place, 1))  3.38 us
    ppermute x3, waiting for transfers between devices, grouped_sum(): lax.ppermute(send, axis, digit_pairs(count, radix, place, offset))  3.23 us
    ppermute x2, starting transfers between devices, grouped_sum(): value = keep + lax.ppermute(send, axis, digit_pairs(count, radix, place, 1))  3.17 us
    ppermute x2, starting transfers between devices, grouped_sum(): other = lax.ppermute(value, axis, digit_pairs(count, radix, place, 1))  2.66 us
  transfers between devices with their start and end apart: 12, of which 11 were waited for; matrix products, arithmetic and copies ran while one was open for 0% of the time, Pallas kernels for 0%

profile of v11, /device:TPU:0, one launch (start us, length us, event | category | flops | bytes accessed | tf_op | source)
XLA Modules:
  0.0 47.8 jit_solution(10011168165014402673)
XLA Ops:
  0.6 1.9 %multiply_convert_fusion = bf16[2,1536,256]{2,1,0:T(8,128)(2,1)S(1)} fusion(bf16[2,1536,256]{2,1,0:T(8,128)(2,1)} %param.2, f32[2,1536]{1,0:T(2,128)} %param.3), kind=kLoop, calls=%fused_computation | loop fusion | flops 2359296 | bytes 3158016 | tf_op jit(solution)/shard_map/convert_element_type | solution.py:141
  2.5 0.4 fusion.11
  3.0 0.4 convolution_add_fusion
  3.4 0.5 %collective-permute-start = (f32[256,256]{1,0:T(8,128)S(1)}, f32[256,256]{1,0:T(8,128)S(1)}, u32[]{:S(2)}, u32[]{:S(2)}) collective-permute-start(f32[256,256]{1,0:T(8,128)S(1)} %select_bitcast_fusion), channel_id=1, source_target_pairs={{0,1},{1,0},{2,3},{3,2},{4,5},{5,4},{6,7},{7,6},{8,9},{9,8},{10,11... | collective-permute-start | bytes 786440 | tf_op jit(solution)/shard_map/ppermute | solution.py:48
  4.0 1.2 %collective-permute-done = f32[256,256]{1,0:T(8,128)S(1)} collective-permute-done((f32[256,256]{1,0:T(8,128)S(1)}, f32[256,256]{1,0:T(8,128)S(1)}, u32[]{:S(2)}, u32[]{:S(2)}) %collective-permute-start) | collective-permute-done | bytes 262176 | tf_op jit(solution)/shard_map/ppermute | solution.py:48
  5.2 2.9 %collective-permute-start.1 = (f32[64,256]{1,0:T(8,128)S(1)}, f32[64,256]{1,0:T(8,128)S(1)}, u32[]{:S(2)}, u32[]{:S(2)}) collective-permute-start(f32[64,256]{1,0:T(8,128)S(1)} %get-tuple-element.9), channel_id=1, source_target_pairs={{0,2},{1,3},{2,4},{3,5},{4,6},{5,7},{6,0},{7,1},{8,10},{9,11},{10,... | collective-permute-start | bytes 196616 | tf_op jit(solution)/shard_map/ppermute | solution.py:55
  8.2 1.1 %collective-permute-start.3 = (f32[64,256]{1,0:T(8,128)S(1)}, f32[64,256]{1,0:T(8,128)S(1)}, u32[]{:S(2)}, u32[]{:S(2)}) collective-permute-start(f32[64,256]{1,0:T(8,128)S(1)} %get-tuple-element.10), channel_id=1, source_target_pairs={{0,6},{1,7},{2,0},{3,1},{4,2},{5,3},{6,4},{7,5},{8,14},{9,15},{10,... | collective-permute-start | bytes 196616 | tf_op jit(solution)/shard_map/ppermute | solution.py:55
  9.2 1.9 %collective-permute-start.2 = (f32[64,256]{1,0:T(8,128)S(1)}, f32[64,256]{1,0:T(8,128)S(1)}, u32[]{:S(2)}, u32[]{:S(2)}) collective-permute-start(f32[64,256]{1,0:T(8,128)S(1)} %get-tuple-element.11), channel_id=1, source_target_pairs={{0,4},{1,5},{2,6},{3,7},{4,0},{5,1},{6,2},{7,3},{8,12},{9,13},{10,... | collective-permute-start | bytes 196616 | tf_op jit(solution)/shard_map/ppermute | solution.py:55
  11.1 0.5 %collective-permute-done.1 = f32[64,256]{1,0:T(8,128)S(1)} collective-permute-done((f32[64,256]{1,0:T(8,128)S(1)}, f32[64,256]{1,0:T(8,128)S(1)}, u32[]{:S(2)}, u32[]{:S(2)}) %collective-permute-start.1) | collective-permute-done | bytes 65568 | tf_op jit(solution)/shard_map/ppermute | solution.py:55
  11.7 1.3 %collective-permute-done.3 = f32[64,256]{1,0:T(8,128)S(1)} collective-permute-done((f32[64,256]{1,0:T(8,128)S(1)}, f32[64,256]{1,0:T(8,128)S(1)}, u32[]{:S(2)}, u32[]{:S(2)}) %collective-permute-start.3) | collective-permute-done | bytes 65568 | tf_op jit(solution)/shard_map/ppermute | solution.py:55
  13.0 1.4 %collective-permute-done.2 = f32[64,256]{1,0:T(8,128)S(1)} collective-permute-done((f32[64,256]{1,0:T(8,128)S(1)}, f32[64,256]{1,0:T(8,128)S(1)}, u32[]{:S(2)}, u32[]{:S(2)}) %collective-permute-start.2) | collective-permute-done | bytes 65568 | tf_op jit(solution)/shard_map/ppermute | solution.py:55
  14.4 2.7 %collective-permute-start.4 = (f32[32,256]{1,0:T(8,128)S(1)}, f32[32,256]{1,0:T(8,128)S(1)}, u32[]{:S(2)}, u32[]{:S(2)}) collective-permute-start(f32[32,256]{1,0:T(8,128)S(1)} %slice_select_fusion.1), channel_id=1, source_target_pairs={{0,8},{1,9},{2,10},{3,11},{4,12},{5,13},{6,14},{7,15},{8,0},{9,1},... | collective-permute-start | bytes 98312 | tf_op jit(solution)/shard_map/ppermute | solution.py:48
  17.1 2.2 %collective-permute-done.4 = f32[32,256]{1,0:T(8,128)S(1)} collective-permute-done((f32[32,256]{1,0:T(8,128)S(1)}, f32[32,256]{1,0:T(8,128)S(1)}, u32[]{:S(2)}, u32[]{:S(2)}) %collective-permute-start.4) | collective-permute-done | bytes 32800 | tf_op jit(solution)/shard_map/ppermute | solution.py:48
  19.3 2.6 %collective-permute-start.5 = (f32[32,256]{1,0:T(8,128)S(1)}, f32[32,256]{1,0:T(8,128)S(1)}, u32[]{:S(2)}, u32[]{:S(2)}) collective-permute-start(f32[32,256]{1,0:T(8,128)S(1)} %select_add_fusion), channel_id=1, source_target_pairs={{0,8},{1,9},{2,10},{3,11},{4,12},{5,13},{6,14},{7,15},{8,0},{9,1},... | collective-permute-start | bytes 98312 | tf_op jit(solution)/shard_map/ppermute | solution.py:60
  21.9 2.3 %collective-permute-done.5 = f32[32,256]{1,0:T(8,128)S(1)} collective-permute-done((f32[32,256]{1,0:T(8,128)S(1)}, f32[32,256]{1,0:T(8,128)S(1)}, u32[]{:S(2)}, u32[]{:S(2)}) %collective-permute-start.5) | collective-permute-done | bytes 32800 | tf_op jit(solution)/shard_map/ppermute | solution.py:60
  24.2 0.7 %collective-permute-start.8 = (f32[64,256]{1,0:T(8,128)S(1)}, f32[64,256]{1,0:T(8,128)S(1)}, u32[]{:S(2)}, u32[]{:S(2)}) collective-permute-start(f32[64,256]{1,0:T(8,128)S(1)} %pad_maximum_fusion.3), channel_id=1, source_target_pairs={{0,2},{1,3},{2,4},{3,5},{4,6},{5,7},{6,0},{7,1},{8,10},{9,11},{10,... | collective-permute-start | bytes 196616 | tf_op jit(solution)/shard_map/ppermute | solution.py:64
  25.0 0.9 %collective-permute-start.7 = (f32[64,256]{1,0:T(8,128)S(1)}, f32[64,256]{1,0:T(8,128)S(1)}, u32[]{:S(2)}, u32[]{:S(2)}) collective-permute-start(f32[64,256]{1,0:T(8,128)S(1)} %pad_maximum_fusion.3), channel_id=1, source_target_pairs={{0,4},{1,5},{2,6},{3,7},{4,0},{5,1},{6,2},{7,3},{8,12},{9,13},{10,... | collective-permute-start | bytes 196616 | tf_op jit(solution)/shard_map/ppermute | solution.py:64
  25.9 2.3 %collective-permute-start.6 = (f32[64,256]{1,0:T(8,128)S(1)}, f32[64,256]{1,0:T(8,128)S(1)}, u32[]{:S(2)}, u32[]{:S(2)}) collective-permute-start(f32[64,256]{1,0:T(8,128)S(1)} %pad_maximum_fusion.3), channel_id=1, source_target_pairs={{0,6},{1,7},{2,0},{3,1},{4,2},{5,3},{6,4},{7,5},{8,14},{9,15},{10,... | collective-permute-start | bytes 196616 | tf_op jit(solution)/shard_map/ppermute | solution.py:64
  28.1 1.3 %collective-permute-done.8 = f32[64,256]{1,0:T(8,128)S(1)} collective-permute-done((f32[64,256]{1,0:T(8,128)S(1)}, f32[64,256]{1,0:T(8,128)S(1)}, u32[]{:S(2)}, u32[]{:S(2)}) %collective-permute-start.8) | collective-permute-done | bytes 65568 | tf_op jit(solution)/shard_map/ppermute | solution.py:64
  29.4 0.0 collective-permute-done.7
  29.4 0.7 %collective-permute-done.6 = f32[64,256]{1,0:T(8,128)S(1)} collective-permute-done((f32[64,256]{1,0:T(8,128)S(1)}, f32[64,256]{1,0:T(8,128)S(1)}, u32[]{:S(2)}, u32[]{:S(2)}) %collective-permute-start.6) | collective-permute-done | bytes 65568 | tf_op jit(solution)/shard_map/ppermute | solution.py:64
  30.2 0.1 collective-permute-start.9
  30.4 1.5 %collective-permute-done.9 = f32[256,256]{1,0:T(8,128)S(1)} collective-permute-done((f32[256,256]{1,0:T(8,128)S(1)}, f32[256,256]{1,0:T(8,128)S(1)}, u32[]{:S(2)}, u32[]{:S(2)}) %collective-permute-start.9) | collective-permute-done | bytes 262176 | tf_op jit(solution)/shard_map/ppermute | solution.py:60
  31.9 0.2 abs_reduce_fusion
  32.1 0.1 reduce_max.9
  32.2 0.5 %fusion.13 = f32[2,256,256]{2,1,0:T(8,128)S(1)} fusion(f32[256,256]{1,0:T(8,128)S(1)} %fusion.22, f32[2]{0:T(128)S(1)} %reduce_max.9, f32[256,256]{1,0:T(8,128)S(1)} %fusion.23, f32[256,256]{1,0:T(8,128)S(1)} %get-tuple-element.3, f32[256,256]{1,0:T(8,128)S(1)} %get-tuple-element.2), kind=kOutput, calls=%fused_computation.30 | convolution fusion | flops 202637312 | bytes 1572872 | tf_op jit(solution)/shard_map/dot_general | solution.py:86
  32.8 0.1 multiply_subtract_fusion
  32.9 0.5 %fusion.6 = f32[2,256,256,1]{2,1,3,0:T(8,128)S(1)} fusion(f32[2,256,256]{2,1,0:T(8,128)S(1)} %fusion.13, f32[256,256]{1,0:T(8,128)S(1)} %fusion.22, f32[2]{0:T(128)S(1)} %reduce_max.9, f32[256,256]{1,0:T(8,128)S(1)} %fusion.23, f32[256,256]{1,0:T(8,128)S(1)} %get-tuple-element.3, f32[256,256]{1,0:T(8,128)S(1)} %get-tuple-element.2), kind=kOutput, calls=%fused_computation.13 | convolution fusion | flops 202375168 | bytes 2097160 | tf_op jit(solution)/shard_map/dot_general | solution.py:89
  33.4 0.6 %fusion.7 = f32[2,2,256,256]{3,2,1,0:T(8,128)S(1)} fusion(f32[2,256,256,1]{2,1,3,0:T(8,128)S(1)} %fusion.6, f32[2,1,256,256]{3,2,0,1:T(8,128)S(1)} %multiply_subtract_fusion, f32[2,1,256,256]{3,2,0,1:T(8,128)S(1)} %bitcast.81), kind=kOutput, calls=%fused_computation.16 | convolution fusion | flops 402915328 | bytes 2621440 | tf_op jit(solution)/shard_map/tkij,tjl->tkil/dot_general | solution.py:90
  34.0 0.4 fusion.4
  34.4 0.6 %fusion.32 = f32[2,2,256,256]{3,2,1,0:T(8,128)S(1)} fusion(f32[2,2,256,256]{3,2,1,0:T(8,128)S(1)} %fusion.7, f32[2,256,256,1]{2,1,3,0:T(8,128)S(1)} %fusion.4), kind=kOutput, calls=%fused_computation.75 | convolution fusion | flops 402653184 | bytes 2621440 | tf_op jit(solution)/shard_map/tkij,tjl->tkil/dot_general | solution.py:90
  35.0 0.7 %fusion.2 = f32[2,256,256,1]{2,1,3,0:T(8,128)S(1)} fusion(f32[2,2,256,256]{3,2,1,0:T(8,128)S(1)} %fusion.32, f32[256,256]{1,0:T(8,128)S(1)} %fusion.22), kind=kOutput, calls=%fused_computation.7 | convolution fusion | flops 402915328 | bytes 1835008 | tf_op jit(solution)/shard_map/dot_general | solution.py:89
  35.7 0.7 %fusion.9 = f32[2,256,256]{2,1,0:T(8,128)S(1)} fusion(f32[2,2,256,256]{3,2,1,0:T(8,128)S(1)} %fusion.32, f32[2,256,256,1]{2,1,3,0:T(8,128)S(1)} %fusion.2, f32[2]{0:T(128)S(1)} %sqrt.7), kind=kOutput, calls=%fused_computation.18 | convolution fusion | flops 402784256 | bytes 2097160 | tf_op jit(solution)/shard_map/slice | solution.py:91
  36.3 0.3 fusion.24
  36.6 1.3 %collective-permute-start.10 = (f32[128,256]{1,0:T(8,128)S(1)}, f32[128,256]{1,0:T(8,128)S(1)}, u32[]{:S(2)}, u32[]{:S(2)}) collective-permute-start(f32[128,256]{1,0:T(8,128)S(1)} %slice_select_fusion), channel_id=1, source_target_pairs={{16,0},{17,1},{18,2},{19,3},{20,4},{21,5},{22,6},{23,7},{24,8},{25... | collective-permute-start | bytes 393224 | tf_op jit(solution)/shard_map/ppermute | solution.py:101
  37.9 6.1 %collective-permute-done.10 = f32[128,256]{1,0:T(8,128)S(1)} collective-permute-done((f32[128,256]{1,0:T(8,128)S(1)}, f32[128,256]{1,0:T(8,128)S(1)}, u32[]{:S(2)}, u32[]{:S(2)}) %collective-permute-start.10) | collective-permute-done | bytes 131104 | tf_op jit(solution)/shard_map/ppermute | solution.py:101
  44.1 0.0 collective-permute-start.11
  44.1 0.0 copy-start
  44.1 1.3 %collective-permute-done.11 = f32[128,256]{1,0:T(8,128)S(1)} collective-permute-done((f32[128,256]{1,0:T(8,128)S(1)}, f32[128,256]{1,0:T(8,128)S(1)}, u32[]{:S(2)}, u32[]{:S(2)}) %collective-permute-start.11) | collective-permute-done | bytes 131104 | tf_op jit(solution)/shard_map/ppermute | solution.py:102
  45.4 0.3 fusion.14
  45.7 0.3 convolution_bitcast_fusion.1
  46.0 0.0 copy-done
  46.1 0.0 copy-start.1
  46.1 1.7 %fusion = bf16[2,1536,256]{2,1,0:T(8,128)(2,1)} fusion(bf16[2,1536,256]{2,1,0:T(8,128)(2,1)S(1)} %copy-done, f32[2,256,256]{2,1,0:T(8,128)S(1)} %pad_maximum_fusion.1), kind=kOutput, calls=%fused_computation.2 | convolution fusion | flops 403570688 | bytes 3670016 | tf_op jit(solution)/shard_map/trm,tmn->trn/dot_general | solution.py:159
  47.8 0.0 copy-done.1
  (19 shorter events, 0.4 us)
Async XLA Ops:
  3.4 1.7 %collective-permute-start = (f32[256,256]{1,0:T(8,128)S(1)}, f32[256,256]{1,0:T(8,128)S(1)}, u32[]{:S(2)}, u32[]{:S(2)}) collective-permute-start(f32[256,256]{1,0:T(8,128)S(1)} %select_bitcast_fusion), channel_id=1, source_target_pairs={{0,1},{1,0},{2,3},{3,2},{4,5},{5,4},{6,7},{7,6},{8,9},{9,8},{10,11... | collective-permute-start | bytes 786440 | tf_op jit(solution)/shard_map/ppermute | solution.py:48
  5.2 6.4 %collective-permute-start.1 = (f32[64,256]{1,0:T(8,128)S(1)}, f32[64,256]{1,0:T(8,128)S(1)}, u32[]{:S(2)}, u32[]{:S(2)}) collective-permute-start(f32[64,256]{1,0:T(8,128)S(1)} %get-tuple-element.9), channel_id=1, source_target_pairs={{0,2},{1,3},{2,4},{3,5},{4,6},{5,7},{6,0},{7,1},{8,10},{9,11},{10,... | collective-permute-start | bytes 196616 | tf_op jit(solution)/shard_map/ppermute | solution.py:55
  8.2 4.8 %collective-permute-start.3 = (f32[64,256]{1,0:T(8,128)S(1)}, f32[64,256]{1,0:T(8,128)S(1)}, u32[]{:S(2)}, u32[]{:S(2)}) collective-permute-start(f32[64,256]{1,0:T(8,128)S(1)} %get-tuple-element.10), channel_id=1, source_target_pairs={{0,6},{1,7},{2,0},{3,1},{4,2},{5,3},{6,4},{7,5},{8,14},{9,15},{10,... | collective-permute-start | bytes 196616 | tf_op jit(solution)/shard_map/ppermute | solution.py:55
  9.2 5.1 %collective-permute-start.2 = (f32[64,256]{1,0:T(8,128)S(1)}, f32[64,256]{1,0:T(8,128)S(1)}, u32[]{:S(2)}, u32[]{:S(2)}) collective-permute-start(f32[64,256]{1,0:T(8,128)S(1)} %get-tuple-element.11), channel_id=1, source_target_pairs={{0,4},{1,5},{2,6},{3,7},{4,0},{5,1},{6,2},{7,3},{8,12},{9,13},{10,... | collective-permute-start | bytes 196616 | tf_op jit(solution)/shard_map/ppermute | solution.py:55
  14.4 4.9 %collective-permute-start.4 = (f32[32,256]{1,0:T(8,128)S(1)}, f32[32,256]{1,0:T(8,128)S(1)}, u32[]{:S(2)}, u32[]{:S(2)}) collective-permute-start(f32[32,256]{1,0:T(8,128)S(1)} %slice_select_fusion.1), channel_id=1, source_target_pairs={{0,8},{1,9},{2,10},{3,11},{4,12},{5,13},{6,14},{7,15},{8,0},{9,1},... | collective-permute-start | bytes 98312 | tf_op jit(solution)/shard_map/ppermute | solution.py:48
  19.3 4.9 %collective-permute-start.5 = (f32[32,256]{1,0:T(8,128)S(1)}, f32[32,256]{1,0:T(8,128)S(1)}, u32[]{:S(2)}, u32[]{:S(2)}) collective-permute-start(f32[32,256]{1,0:T(8,128)S(1)} %select_add_fusion), channel_id=1, source_target_pairs={{0,8},{1,9},{2,10},{3,11},{4,12},{5,13},{6,14},{7,15},{8,0},{9,1},... | collective-permute-start | bytes 98312 | tf_op jit(solution)/shard_map/ppermute | solution.py:60
  24.2 5.2 %collective-permute-start.8 = (f32[64,256]{1,0:T(8,128)S(1)}, f32[64,256]{1,0:T(8,128)S(1)}, u32[]{:S(2)}, u32[]{:S(2)}) collective-permute-start(f32[64,256]{1,0:T(8,128)S(1)} %pad_maximum_fusion.3), channel_id=1, source_target_pairs={{0,2},{1,3},{2,4},{3,5},{4,6},{5,7},{6,0},{7,1},{8,10},{9,11},{10,... | collective-permute-start | bytes 196616 | tf_op jit(solution)/shard_map/ppermute | solution.py:64
  25.0 4.5 %collective-permute-start.7 = (f32[64,256]{1,0:T(8,128)S(1)}, f32[64,256]{1,0:T(8,128)S(1)}, u32[]{:S(2)}, u32[]{:S(2)}) collective-permute-start(f32[64,256]{1,0:T(8,128)S(1)} %pad_maximum_fusion.3), channel_id=1, source_target_pairs={{0,4},{1,5},{2,6},{3,7},{4,0},{5,1},{6,2},{7,3},{8,12},{9,13},{10,... | collective-permute-start | bytes 196616 | tf_op jit(solution)/shard_map/ppermute | solution.py:64
  25.9 4.3 %collective-permute-start.6 = (f32[64,256]{1,0:T(8,128)S(1)}, f32[64,256]{1,0:T(8,128)S(1)}, u32[]{:S(2)}, u32[]{:S(2)}) collective-permute-start(f32[64,256]{1,0:T(8,128)S(1)} %pad_maximum_fusion.3), channel_id=1, source_target_pairs={{0,6},{1,7},{2,0},{3,1},{4,2},{5,3},{6,4},{7,5},{8,14},{9,15},{10,... | collective-permute-start | bytes 196616 | tf_op jit(solution)/shard_map/ppermute | solution.py:64
  30.2 1.6 %collective-permute-start.9 = (f32[256,256]{1,0:T(8,128)S(1)}, f32[256,256]{1,0:T(8,128)S(1)}, u32[]{:S(2)}, u32[]{:S(2)}) collective-permute-start(f32[256,256]{1,0:T(8,128)S(1)} %pad_maximum_fusion.2), channel_id=1, source_target_pairs={{0,1},{1,0},{2,3},{3,2},{4,5},{5,4},{6,7},{7,6},{8,9},{9,8},{10,11... | collective-permute-start | bytes 786440 | tf_op jit(solution)/shard_map/ppermute | solution.py:60
  36.6 7.4 %collective-permute-start.10 = (f32[128,256]{1,0:T(8,128)S(1)}, f32[128,256]{1,0:T(8,128)S(1)}, u32[]{:S(2)}, u32[]{:S(2)}) collective-permute-start(f32[128,256]{1,0:T(8,128)S(1)} %slice_select_fusion), channel_id=1, source_target_pairs={{16,0},{17,1},{18,2},{19,3},{20,4},{21,5},{22,6},{23,7},{24,8},{25... | collective-permute-start | bytes 393224 | tf_op jit(solution)/shard_map/ppermute | solution.py:101
  44.1 1.3 %collective-permute-start.11 = (f32[128,256]{1,0:T(8,128)S(1)}, f32[128,256]{1,0:T(8,128)S(1)}, u32[]{:S(2)}, u32[]{:S(2)}) collective-permute-start(f32[128,256]{1,0:T(8,128)S(1)} %collective-permute-done.10), channel_id=1, source_target_pairs={{0,1},{1,0},{2,3},{3,2},{4,5},{5,4},{6,7},{7,6},{8,9},{9,8},{10,11... | collective-permute-start | bytes 393224 | tf_op jit(solution)/shard_map/ppermute | solution.py:102
  44.1 2.0 %copy-start = (bf16[2,1536,256]{2,1,0:T(8,128)(2,1)S(1)}, bf16[2,1536,256]{2,1,0:T(8,128)(2,1)}, u32[]{:S(2)}) copy-start(bf16[2,1536,256]{2,1,0:T(8,128)(2,1)} %param.2) | copy-start | bytes 4718596
  46.1 1.7 %copy-start.1 = (f32[2,256,256]{2,1,0:T(8,128)}, f32[2,256,256]{2,1,0:T(8,128)S(1)}, u32[]{:S(2)}) copy-start(f32[2,256,256]{2,1,0:T(8,128)S(1)} %pad_maximum_fusion.1) | copy-start | bytes 1572868
